TPU v7x, 1024 devices: a whole 8x8x8 slice. The times are simulated.
1024 devices in a mesh: along: 64 (over z, x), across: 16 (over y, core).
Axes of the slice: x: 8, y: 8, z: 8, core: 2. Of those that a mesh axis runs over, the one named last changes fastest.
Arguments:
- features: bfloat16 [1048576, 256], P(('along', 'across')), may hold values from -6 to 6
- adj_tiles: bfloat16 [8192, 4, 128, 128], P(('along', 'across')), may hold values from -0.25 to 0.25
- adj_index: int32 [8192, 4], P(('along', 'across')), may hold values from 0 to 11, as said below
- adj_count: int32 [8192], P(('along', 'across')), may hold values from 2 to 4, as said below
- bnd_index: int32 [131072], P(('along', 'across')), may hold values from 0 to 1023
- pool_index: int32 [1048576], P(('along', 'across')), may hold values from 0 to 63
- w_msg: bfloat16 [256, 256], replicated, may hold values from -0.375 to 0.375
- w_update: bfloat16 [512, 256], replicated, may hold values from -0.25 to 0.25
- w_coarse: bfloat16 [256, 256], replicated, may hold values from -0.375 to 0.375
- cotangent: bfloat16 [1048576, 256], P(('along', 'across')), may hold values from -0.125 to 0.125
Outputs:
- updated: bfloat16 [1048576, 256], P(('along', 'across'))
- weight_grads: float32 [131072], P(('along', 'across'))
Inputs may be any that keep to these rules, and one draw needn't show every extreme that they name: `adj_index`: indices 0 to 7 name the partition's own blocks, 8 to 11 the four boundary tiles in the order of the sources. Slot 0 of every block names the block itself. Slots from adj_count on are ignored. Some block has all 4 slots live.
All inputs are finite; a program needn't handle non-finite values.
Results may differ from a plain program's by a relative error of at most 0.0062.
Values may be sent and summed in bfloat16 or wider, within the bound.
No kernel may reach another device: no remote copies, remote signals or barrier semaphores. Data moves between devices by JAX's collectives and lax.ppermute only.
A program may use at most 32 MiB of HBM per device.

v0:
```python
import jax
import jax.numpy as jnp
from jax import lax
from jax.sharding import PartitionSpec as P

NC_DEV = 4


eps = 1e-05


def extended(block, sides, width):
    for axis, dim in sides:
        count = lax.axis_size(axis)
        forward = [(i, i + 1) for i in range(count - 1)]
        backward = [(target, source) for source, target in forward]
        low = lax.ppermute(
            lax.slice_in_dim(block, block.shape[dim] - width, None, axis=dim), axis, forward
        )
        high = lax.ppermute(lax.slice_in_dim(block, 0, width, axis=dim), axis, backward)
        block = jnp.concatenate([low, block, high], axis=dim)
    return block


def normalize(values):
    center = values - jnp.mean(values, axis=-1, keepdims=True)
    inverse = lax.rsqrt(jnp.mean(center * center, axis=-1, keepdims=True) + eps)
    return (center * inverse, inverse)


def silu_slope(values):
    logistic = jax.nn.sigmoid(values)
    return logistic * (1.0 + values * (1.0 - logistic))


def transposed_times(operand, second, precision=None):
    return lax.dot_general(
        operand,
        second,
        (((0,), (0,)), ((), ())),
        precision=precision,
        preferred_element_type=jnp.float32,
    )


def times_transposed(operand, second):
    return lax.dot_general(
        operand, second, (((1,), (1,)), ((), ())), preferred_element_type=jnp.float32
    )


def coarse_forward(pooled, w_coarse):
    coarse_norm, inverse = normalize(pooled)
    coarse = coarse_norm.astype(jnp.bfloat16)
    coarse_pre = jnp.dot(coarse, w_coarse, preferred_element_type=jnp.float32)
    return (coarse_norm, inverse, coarse, coarse_pre, jax.nn.silu(coarse_pre).astype(jnp.bfloat16))


def coarse_backward(coarse_cot, coarse_norm, inverse, coarse_pre, w_coarse):
    coarse_delta = (coarse_cot * silu_slope(coarse_pre)).astype(jnp.bfloat16)
    coarse_back = times_transposed(coarse_delta, w_coarse)
    mean_one = jnp.mean(coarse_back, axis=-1, keepdims=True)
    mean_two = jnp.mean(coarse_back * coarse_norm, axis=-1, keepdims=True)
    return (coarse_delta, inverse * (coarse_back - mean_one - coarse_norm * mean_two))


def local(
    features,
    adj_tiles,
    adj_index,
    adj_count,
    bnd_index,
    pool_index,
    w_msg,
    w_update,
    w_coarse,
    cotangent,
):
    feature_count = features.shape[1]
    blocks = adj_tiles.shape[0]
    slot_count = adj_tiles.shape[1]
    tile_rows = adj_tiles.shape[2]
    inputs = features.astype(jnp.float32)
    normed, _ = normalize(inputs)
    scaled = normed.astype(jnp.bfloat16)
    rim_rows = scaled[bnd_index]
    padded = extended(rim_rows[None, None], (("along", 0), ("across", 1)), 1)
    halo_tiles = jnp.stack([padded[0, 1], padded[2, 1], padded[1, 0], padded[1, 2]])
    sources = jnp.concatenate(
        [scaled.reshape(blocks, tile_rows, feature_count), halo_tiles], axis=0
    )
    messages = jnp.dot(
        sources.reshape(-1, feature_count), w_msg, preferred_element_type=jnp.float32
    )
    messages = messages.astype(jnp.bfloat16).reshape(sources.shape)
    live_slots = jnp.arange(slot_count)[None, :] < adj_count[:, None]
    masked_tiles = jnp.where(live_slots[:, :, None, None], adj_tiles, jnp.zeros((), jnp.bfloat16))
    aggregated = jnp.einsum(
        "bkij,bkjh->bih", masked_tiles, messages[adj_index], preferred_element_type=jnp.float32
    )
    aggregated = aggregated.astype(jnp.bfloat16).reshape(-1, feature_count)
    summed_scaled = jnp.einsum(
        "bkij,bkjh->bih", masked_tiles, sources[adj_index], preferred_element_type=jnp.float32
    )
    summed_scaled = summed_scaled.astype(jnp.bfloat16).reshape(-1, feature_count)
    w_first = w_update[:feature_count]
    w_second = w_update[feature_count:]
    update_pre = jnp.dot(scaled, w_first, preferred_element_type=jnp.float32) + jnp.dot(
        aggregated, w_second, preferred_element_type=jnp.float32
    )
    hidden_one = inputs + jax.nn.silu(update_pre)
    coarse_count = NC_DEV * lax.axis_size("across")
    assign_float = (pool_index[:, None] == jnp.arange(coarse_count)[None, :]).astype(jnp.float32)
    assign_bits = assign_float.astype(jnp.bfloat16)
    pooled_part = transposed_times(assign_float, hidden_one, lax.Precision.HIGHEST)
    cot_part = transposed_times(assign_bits, cotangent)
    pooled, coarse_cot = lax.psum((pooled_part, cot_part), "across")
    coarse_norm, inverse, coarse, coarse_pre, coarse_out = coarse_forward(pooled, w_coarse)
    hidden_two = hidden_one + jnp.dot(assign_bits, coarse_out, preferred_element_type=jnp.float32)
    coarse_delta, pooled_delta = coarse_backward(
        coarse_cot, coarse_norm, inverse, coarse_pre, w_coarse
    )
    start = lax.axis_index("across") * NC_DEV
    own_coarse = lax.dynamic_slice_in_dim(coarse, start, NC_DEV, 0)
    own_coarse_delta = lax.dynamic_slice_in_dim(coarse_delta, start, NC_DEV, 0)
    coarse_grad = transposed_times(own_coarse, own_coarse_delta)
    hidden_delta = cotangent.astype(jnp.float32) + jnp.dot(
        assign_float,
        pooled_delta,
        precision=lax.Precision.HIGHEST,
        preferred_element_type=jnp.float32,
    )
    update_delta = (hidden_delta * silu_slope(update_pre)).astype(jnp.bfloat16)
    aggregated_delta = times_transposed(update_delta, w_second).astype(jnp.bfloat16)
    message_grad = transposed_times(summed_scaled, aggregated_delta)
    grad_terms = jnp.concatenate([message_grad.reshape(-1), coarse_grad.reshape(-1)])
    partial_grads = lax.psum_scatter(grad_terms, "along", scatter_dimension=0, tiled=True)
    weight_grads = lax.psum_scatter(partial_grads, "across", scatter_dimension=0, tiled=True)
    return (hidden_two.astype(jnp.bfloat16), weight_grads)


def solution(mesh):
    return jax.shard_map(
        local,
        mesh=mesh,
        in_specs=(
            P(("along", "across"), None),
            P(("along", "across"), None, None, None),
            P(("along", "across"), None),
            P(("along", "across")),
            P(("along", "across")),
            P(("along", "across")),
            P(),
            P(),
            P(),
            P(("along", "across"), None),
        ),
        out_specs=(P(("along", "across"), None), P(("along", "across"))),
        check_vma=False,
    )
```

profile of v0, /device:TPU:1, one launch (start us, length us, event | category | flops | bytes accessed | tf_op | source)
XLA Modules:
  0.0 388.5 jit_solution(2341022200515996538)
XLA Ops:
  7.2 0.0 copy-start
  7.2 0.0 copy-start.10
  7.2 0.0 copy-start.9
  7.2 0.0 copy-start.11
  7.2 0.0 copy-start.7
  7.2 0.0 all-reduce.8.cloned.1.call-start
  7.3 1.3 convert_reduce_fusion
  8.6 1.4 fusion.9
  10.0 0.0 copy-start.5
  10.0 0.0 copy-start.8
  10.1 1.4 fusion.10
  11.5 0.0 copy-done.10
  11.5 0.8 gather_fusion
  12.4 3.9 %collective-permute-start = (bf16[1,1,128,256]{3,2,1,0:T(8,128)(2,1)S(1)}, bf16[1,1,128,256]{3,2,1,0:T(8,128)(2,1)S(1)}, u32[]{:S(2)}, u32[]{:S(2)}) collective-permute-start(bf16[1,1,128,256]{3,2,1,0:T(8,128)(2,1)S(1)} %bitcast.59), channel_id=1, source_target_pairs={{0,16},{16,32},{32,48},{48,64},{64,80},{80,96},{96,112},{112,128},... | collective-permute-start | bytes 196616 | tf_op jit(solution)/shard_map/ppermute | solution.py:17
  16.3 1.3 collective-permute-start.1
  17.7 0.0 copy-done.9
  17.7 0.1 copy.14
  17.8 0.1 reshape.96
  17.9 0.0 copy-done.11
  17.9 0.1 iota_compare_fusion.3
  17.9 0.0 copy-done.7
  17.9 0.3 fusion.19
  18.2 0.0 copy-done.5
  18.3 0.0 copy-done.8
  18.3 1.1 fusion.14
  19.3 0.0 collective-permute-done
  19.4 2.0 collective-permute-done.1
  21.4 5.3 %collective-permute-start.2 = (bf16[3,1,128,256]{3,2,1,0:T(8,128)(2,1)S(1)}, bf16[3,1,128,256]{3,2,1,0:T(8,128)(2,1)S(1)}, u32[]{:S(2)}, u32[]{:S(2)}) collective-permute-start(bf16[3,1,128,256]{3,2,1,0:T(8,128)(2,1)S(1)} %pad_maximum_fusion.1), channel_id=1, source_target_pairs={{0,1},{1,2},{2,3},{3,4},{4,5},{5,6},{6,7},{7,8},{8,9},{9,10},{10,1... | collective-permute-start | bytes 589832 | tf_op jit(solution)/shard_map/ppermute | solution.py:17
  26.7 10.6 %collective-permute-start.3 = (bf16[3,1,128,256]{3,2,1,0:T(8,128)(2,1)S(1)}, bf16[3,1,128,256]{3,2,1,0:T(8,128)(2,1)S(1)}, u32[]{:S(2)}, u32[]{:S(2)}) collective-permute-start(bf16[3,1,128,256]{3,2,1,0:T(8,128)(2,1)S(1)} %pad_maximum_fusion.1), channel_id=1, source_target_pairs={{1,0},{2,1},{3,2},{4,3},{5,4},{6,5},{7,6},{8,7},{9,8},{10,9},{11,1... | collective-permute-start | bytes 589832 | tf_op jit(solution)/shard_map/ppermute | solution.py:20
  37.3 0.0 collective-permute-done.2
  37.3 1.0 collective-permute-done.3
  38.3 2.0 gather_fusion.2
  40.3 0.0 copy-done
  40.3 0.4 convolution_convert_fusion
  40.7 2.0 gather_fusion.1
  42.7 2.4 fusion.3
  45.1 0.3 convolution_add_fusion.1
  45.4 1.0 copy-done.3
  46.4 1.6 fusion.11
  48.0 0.0 all-reduce.8.cloned.1.call-update
  48.0 0.0 all-reduce.6.cloned.1.call-start
  48.1 0.0 copy-start.6
  48.1 2.6 fusion.4
  50.7 123.0 %all-reduce.8.cloned.1.call-done = (f32[64,256]{1,0:T(8,128)}, f32[64,256]{1,0:T(8,128)}) async-done(((f32[64,256]{1,0:T(8,128)}, f32[64,256]{1,0:T(8,128)}), (f32[64,256]{1,0:T(8,128)}, f32[64,256]{1,0:T(8,128)})) %all-reduce.8.cloned.1.call-update) | async-done | bytes 131088 | tf_op jit(solution)/shard_map/psum | solution.py:117
  173.6 0.9 reduce_sum.56
  174.6 1.0 multiply_reduce_fusion.1
  175.6 0.9 fusion.30
  176.6 1.1 multiply_convert_fusion
  177.7 1.2 fusion.42
  178.9 0.0 copy-start.12
  178.9 2.9 fusion.2
  181.9 1.8 fusion.8
  183.6 0.1 copy.17
  183.8 0.2 convolution_bitcast_fusion.2
  184.0 0.1 copy.18
  184.2 0.8 pad_maximum_fusion
  185.0 0.0 all-reduce.6.cloned.1.call-update
  185.0 1.3 dynamic-slice
  186.3 1.3 dynamic-slice.2
  188.9 1.3 fusion.1
  190.1 161.5 %all-reduce.6.cloned.1.call-done = f32[131072]{0:T(1024)} async-done(((f32[131072]{0:T(1024)}), f32[131072]{0:T(1024)}) %all-reduce.6.cloned.1.call-update) | async-done | bytes 524304
  351.6 0.7 dynamic-slice.1
  352.3 28.7 %all-reduce.1 = f32[2048]{0:T(1024)S(1)} all-reduce(f32[2048]{0:T(1024)S(1)} %dynamic-slice.1), channel_id=3, replica_groups=mesh['along'=64,'across'=16] {'across'}, use_global_device_ids=true, to_apply=%region_9.10.clone | all-reduce | flops 2048 | bytes 16384
  381.0 0.6 dynamic-slice.3
  (24 shorter events, 0.1 us)
Async XLA Ops:
  7.2 33.2 %copy-start = (bf16[256,256]{1,0:T(8,128)(2,1)S(1)}, bf16[256,256]{1,0:T(8,128)(2,1)}, u32[]{:S(2)}) copy-start(bf16[256,256]{1,0:T(8,128)(2,1)} %param.16) | copy-start | bytes 393220
  7.2 4.3 %copy-start.10 = (s32[128]{0:T(128)S(1)}, s32[128]{0:T(128)}, u32[]{:S(2)}) copy-start(s32[128]{0:T(128)} %param.14) | copy-start | bytes 1540
  7.2 10.5 %copy-start.9 = (s32[8,4]{0,1:T(4,128)S(1)}, s32[8,4]{0,1:T(4,128)}, u32[]{:S(2)}) copy-start(s32[8,4]{0,1:T(4,128)} %param.12) | copy-start | bytes 388
  7.2 10.7 %copy-start.11 = (s32[8]{0:T(128)S(1)}, s32[8]{0:T(128)}, u32[]{:S(2)}) copy-start(s32[8]{0:T(128)} %param.13) | copy-start | bytes 100
  7.2 10.7 %copy-start.7 = (bf16[512,256]{1,0:T(8,128)(2,1)S(1)}, bf16[512,256]{1,0:T(8,128)(2,1)}, u32[]{:S(2)}) copy-start(bf16[512,256]{1,0:T(8,128)(2,1)} %param.17) | copy-start | bytes 786436
  7.2 166.4 %all-reduce.8.cloned.1.call-start = ((), (), s32[]{:S(2)}) async-start(), calls=%async_computation.1 | async-start | bytes 262144 | tf_op jit(solution)/shard_map/psum | solution.py:117
  10.0 8.2 %copy-start.5 = (bf16[1024,256]{1,0:T(8,128)(2,1)S(1)}, bf16[1024,256]{1,0:T(8,128)(2,1)}, u32[]{:S(2)}) copy-start(bf16[1024,256]{1,0:T(8,128)(2,1)} %param.19) | copy-start | bytes 1572868
  10.0 8.2 %copy-start.8 = (s32[1024]{0:T(1024)S(1)}, s32[1024]{0:T(1024)}, u32[]{:S(2)}) copy-start(s32[1024]{0:T(1024)} %param.15) | copy-start | bytes 12292
  12.4 7.0 %collective-permute-start = (bf16[1,1,128,256]{3,2,1,0:T(8,128)(2,1)S(1)}, bf16[1,1,128,256]{3,2,1,0:T(8,128)(2,1)S(1)}, u32[]{:S(2)}, u32[]{:S(2)}) collective-permute-start(bf16[1,1,128,256]{3,2,1,0:T(8,128)(2,1)S(1)} %bitcast.59), channel_id=1, source_target_pairs={{0,16},{16,32},{32,48},{48,64},{64,80},{80,96},{96,112},{112,128},... | collective-permute-start | bytes 196616 | tf_op jit(solution)/shard_map/ppermute | solution.py:17
  16.3 5.0 %collective-permute-start.1 = (bf16[1,1,128,256]{3,2,1,0:T(8,128)(2,1)S(1)}, bf16[1,1,128,256]{3,2,1,0:T(8,128)(2,1)S(1)}, u32[]{:S(2)}, u32[]{:S(2)}) collective-permute-start(bf16[1,1,128,256]{3,2,1,0:T(8,128)(2,1)S(1)} %bitcast.60), channel_id=1, source_target_pairs={{16,0},{32,16},{48,32},{64,48},{80,64},{96,80},{112,96},{128,112},... | collective-permute-start | bytes 196616 | tf_op jit(solution)/shard_map/ppermute | solution.py:20
  21.4 15.9 %collective-permute-start.2 = (bf16[3,1,128,256]{3,2,1,0:T(8,128)(2,1)S(1)}, bf16[3,1,128,256]{3,2,1,0:T(8,128)(2,1)S(1)}, u32[]{:S(2)}, u32[]{:S(2)}) collective-permute-start(bf16[3,1,128,256]{3,2,1,0:T(8,128)(2,1)S(1)} %pad_maximum_fusion.1), channel_id=1, source_target_pairs={{0,1},{1,2},{2,3},{3,4},{4,5},{5,6},{6,7},{7,8},{8,9},{9,10},{10,1... | collective-permute-start | bytes 589832 | tf_op jit(solution)/shard_map/ppermute | solution.py:17
  26.7 11.6 %collective-permute-start.3 = (bf16[3,1,128,256]{3,2,1,0:T(8,128)(2,1)S(1)}, bf16[3,1,128,256]{3,2,1,0:T(8,128)(2,1)S(1)}, u32[]{:S(2)}, u32[]{:S(2)}) collective-permute-start(bf16[3,1,128,256]{3,2,1,0:T(8,128)(2,1)S(1)} %pad_maximum_fusion.1), channel_id=1, source_target_pairs={{1,0},{2,1},{3,2},{4,3},{5,4},{6,5},{7,6},{8,7},{9,8},{10,9},{11,1... | collective-permute-start | bytes 589832 | tf_op jit(solution)/shard_map/ppermute | solution.py:20
  45.1 1.3 copy-start.1
  45.4 1.0 copy-start.3
  46.4 1.7 copy-start.2
  48.0 303.6 %all-reduce.6.cloned.1.call-start = ((), (), s32[]{:S(2)}) async-start(), calls=%async_computation | async-start | bytes 1048576
  48.1 130.8 %copy-start.6 = (bf16[1024,256]{1,0:T(8,128)(2,1)S(1)}, bf16[1024,256]{1,0:T(8,128)(2,1)}, u32[]{:S(2)}) copy-start(bf16[1024,256]{1,0:T(8,128)(2,1)} %param.19) | copy-start | bytes 1572868
  178.9 3.0 copy-start.12
  181.9 7.0 %copy-start.4 = (f32[1024,256]{1,0:T(8,128)S(1)}, f32[1024,256]{1,0:T(8,128)}, u32[]{:S(2)}) copy-start(f32[1024,256]{1,0:T(8,128)} %copy-done.3) | copy-start | bytes 3145732
Sparse Core Ops, SparseCore 0:
  48.1 125.4 all-reduce.7
  185.1 166.4 all-reduce.5
where the time goes:
time: 389 us; the launch traced here: 388 us
  waiting for transfers between devices  287 us (74%)
  blocking collectives  28.7 us (7%)
  starting transfers between devices  21.2 us (5%)
  matrix products  17.1 us (4%)
  between operations  15.7 us (4%)
  local copies, waits for them, and re-layouts  10.2 us (3%)
  other arithmetic  8.03 us (2%)
    unnamed x3, waiting for transfers between devices  161 us
    psum x1, waiting for transfers between devices, local(): pooled, coarse_cot = lax.psum((pooled_part, cot_part), 'across')  123 us
    unnamed x1, blocking collectives  28.7 us
    ppermute x2, starting transfers between devices, extended(): lax.ppermute(lax.slice_in_dim(block, 0, width, axis=dim), axis, backward)  11.8 us
    ppermute x2, starting transfers between devices, extended(): lax.ppermute(lax.slice_in_dim(block, block.shape[dim] - width, None, axis...  9.26 us
  transfers between devices with their start and end apart: 6, of which 4 were waited for; matrix products, arithmetic and copies ran while one was open for 2% of the time, Pallas kernels for 0%

commit v1 on v0

--- a/solution.py
+++ b/solution.py
@@ -9,17 +9,47 @@
 eps = 1e-05
 
 
-def extended(block, sides, width):
-    for axis, dim in sides:
+def partner_pairs(count, distance):
+    return [(i, i ^ distance) for i in range(count)]
+
+
+def butterfly_sum(values, axis):
+    count = lax.axis_size(axis)
+    distance = 1
+    while distance < count:
+        values = values + lax.ppermute(values, axis, partner_pairs(count, distance))
+        distance *= 2
+    return values
+
+
+def halving_scatter(values, axes):
+    steps = []
+    for axis in reversed(axes):
+        count = lax.axis_size(axis)
+        distance = 1
+        while distance < count:
+            steps.append((axis, count, distance))
+            distance *= 2
+    chunk = values.shape[0] // (1 << len(steps))
+    values = values.reshape(-1, chunk)
+    for axis, count, distance in steps:
+        bit = (lax.axis_index(axis) // distance) % 2
+        pairs = values.reshape(-1, 2, chunk)
+        keep = jnp.where(bit == 0, pairs[:, 0], pairs[:, 1])
+        send = jnp.where(bit == 0, pairs[:, 1], pairs[:, 0])
+        values = keep + lax.ppermute(send, axis, partner_pairs(count, distance))
+    return values.reshape(-1)
+
+
+def neighbour_tiles(tile):
+    tiles = []
+    for axis in ("along", "across"):
         count = lax.axis_size(axis)
         forward = [(i, i + 1) for i in range(count - 1)]
-        backward = [(target, source) for source, target in forward]
-        low = lax.ppermute(
-            lax.slice_in_dim(block, block.shape[dim] - width, None, axis=dim), axis, forward
-        )
-        high = lax.ppermute(lax.slice_in_dim(block, 0, width, axis=dim), axis, backward)
-        block = jnp.concatenate([low, block, high], axis=dim)
-    return block
+        backward = [(i + 1, i) for i in range(count - 1)]
+        tiles.append(lax.ppermute(tile, axis, forward))
+        tiles.append(lax.ppermute(tile, axis, backward))
+    return jnp.stack(tiles)
 
 
 def normalize(values):
@@ -84,8 +114,7 @@
     normed, _ = normalize(inputs)
     scaled = normed.astype(jnp.bfloat16)
     rim_rows = scaled[bnd_index]
-    padded = extended(rim_rows[None, None], (("along", 0), ("across", 1)), 1)
-    halo_tiles = jnp.stack([padded[0, 1], padded[2, 1], padded[1, 0], padded[1, 2]])
+    halo_tiles = neighbour_tiles(rim_rows)
     sources = jnp.concatenate(
         [scaled.reshape(blocks, tile_rows, feature_count), halo_tiles], axis=0
     )
@@ -114,7 +143,7 @@
     assign_bits = assign_float.astype(jnp.bfloat16)
     pooled_part = transposed_times(assign_float, hidden_one, lax.Precision.HIGHEST)
     cot_part = transposed_times(assign_bits, cotangent)
-    pooled, coarse_cot = lax.psum((pooled_part, cot_part), "across")
+    pooled, coarse_cot = butterfly_sum(jnp.stack([pooled_part, cot_part]), "across")
     coarse_norm, inverse, coarse, coarse_pre, coarse_out = coarse_forward(pooled, w_coarse)
     hidden_two = hidden_one + jnp.dot(assign_bits, coarse_out, preferred_element_type=jnp.float32)
     coarse_delta, pooled_delta = coarse_backward(
@@ -134,8 +163,7 @@
     aggregated_delta = times_transposed(update_delta, w_second).astype(jnp.bfloat16)
     message_grad = transposed_times(summed_scaled, aggregated_delta)
     grad_terms = jnp.concatenate([message_grad.reshape(-1), coarse_grad.reshape(-1)])
-    partial_grads = lax.psum_scatter(grad_terms, "along", scatter_dimension=0, tiled=True)
-    weight_grads = lax.psum_scatter(partial_grads, "across", scatter_dimension=0, tiled=True)
+    weight_grads = halving_scatter(grad_terms, ("along", "across"))
     return (hidden_two.astype(jnp.bfloat16), weight_grads)
 
 

time: 389 us -> 154 us (0.40)
  the two profiles are of different devices: /device:TPU:1 before, /device:TPU:8 now
where the time goes in v1:
time: 154 us; the launch traced here: 153 us
  starting transfers between devices  72.3 us (47%)
  waiting for transfers between devices  54.2 us (35%)
  matrix products  11 us (7%)
  other arithmetic  7.28 us (5%)
  local copies, waits for them, and re-layouts  6.79 us (4%)
    ppermute x10, starting transfers between devices, halving_scatter(): values = keep + lax.ppermute(send, axis, partner_pairs(count, distance))  42.4 us
    ppermute x10, waiting for transfers between devices, halving_scatter(): values = keep + lax.ppermute(send, axis, partner_pairs(count, distance))  35.6 us
    ppermute x4, starting transfers between devices, butterfly_sum(): values = values + lax.ppermute(values, axis, partner_pairs(count, distance))  20.3 us
    ppermute x4, waiting for transfers between devices, butterfly_sum(): values = values + lax.ppermute(values, axis, partner_pairs(count, distance))  16.7 us
    ppermute x2, starting transfers between devices, neighbour_tiles(): tiles.append(lax.ppermute(tile, axis, backward))  5.84 us
    ppermute x2, starting transfers between devices, neighbour_tiles(): tiles.append(lax.ppermute(tile, axis, forward))  3.78 us
  transfers between devices with their start and end apart: 18, of which 15 were waited for; matrix products, arithmetic and copies ran while one was open for 4% of the time, Pallas kernels for 0%

profile of v1, /device:TPU:8, one launch (start us, length us, event | category | flops | bytes accessed | tf_op | source)
XLA Modules:
  0.0 153.2 jit_solution(16093494421873966662)
XLA Ops:
  0.7 1.3 convert_reduce_fusion
  2.0 1.4 fusion.7
  3.5 1.4 fusion.8
  4.9 1.5 gather_fusion
  6.4 2.5 %collective-permute-start = (bf16[128,256]{1,0:T(8,128)(2,1)}, bf16[128,256]{1,0:T(8,128)(2,1)}, u32[]{:S(2)}, u32[]{:S(2)}) collective-permute-start(bf16[128,256]{1,0:T(8,128)(2,1)} %gather_fusion), channel_id=1, source_target_pairs={{0,16},{16,32},{32,48},{48,64},{64,80},{80,96},{96,112},{112,128},... | collective-permute-start | bytes 196616 | tf_op jit(solution)/shard_map/ppermute | solution.py:50
  8.9 4.6 %collective-permute-start.1 = (bf16[128,256]{1,0:T(8,128)(2,1)}, bf16[128,256]{1,0:T(8,128)(2,1)S(1)}, u32[]{:S(2)}, u32[]{:S(2)}) collective-permute-start(bf16[128,256]{1,0:T(8,128)(2,1)} %gather_fusion), channel_id=1, source_target_pairs={{16,0},{32,16},{48,32},{64,48},{80,64},{96,80},{112,96},{128,112},... | collective-permute-start | bytes 196616 | tf_op jit(solution)/shard_map/ppermute | solution.py:51
  13.5 1.3 collective-permute-start.2
  14.8 1.3 collective-permute-start.3
  16.4 0.3 fusion.16
  16.7 0.4 convolution_bitcast_fusion.2
  17.2 0.8 bitcast_dynamic-update-slice_fusion.3
  18.1 2.0 %collective-permute-done.3 = bf16[128,256]{1,0:T(8,128)(2,1)S(1)} collective-permute-done((bf16[128,256]{1,0:T(8,128)(2,1)}, bf16[128,256]{1,0:T(8,128)(2,1)S(1)}, u32[]{:S(2)}, u32[]{:S(2)}) %collective-permute-start.3) | collective-permute-done | bytes 65568 | tf_op jit(solution)/shard_map/ppermute | solution.py:51
  20.1 0.4 convolution_convert_fusion
  20.4 2.0 %gather_fusion.1 = bf16[32,128,256]{2,1,0:T(8,128)(2,1)} fusion(bf16[12,128,256]{2,1,0:T(8,128)(2,1)S(1)} %bitcast.150, s32[1024]{0:T(1024)S(1)} %pad_clamp_fusion), kind=kCustom, calls=%fused_computation.1 | custom fusion | bytes 4194432 | tf_op jit(solution)/shard_map/gather | solution.py:128
  22.4 2.5 %fusion.3 = bf16[8,128,256]{2,1,0:T(8,128)(2,1)S(1)} fusion(bf16[8,4,128,256]{3,2,1,0:T(8,128)(2,1)} %bitcast.153, bf16[8,4,128,128]{3,2,1,0:T(8,128)(2,1)} %param.11, pred[8,4]{1,0:T(8,128)(4,1)S(1)} %iota_compare_fusion.3), kind=kOutput, calls=%fused_computation.16 | convolution fusion | flops 269221888 | bytes 3670048 | tf_op jit(solution)/shard_map/bkij,bkjh->bih/dot_general | solution.py:127
  24.9 0.3 convolution_add_fusion.1
  25.2 0.7 copy-done.1
  26.0 1.0 convolution_bitcast_fusion.3
  27.0 4.8 %collective-permute-start.4 = (f32[2,64,256]{2,1,0:T(8,128)S(1)}, f32[2,64,256]{2,1,0:T(8,128)S(1)}, u32[]{:S(2)}, u32[]{:S(2)}) collective-permute-start(f32[2,64,256]{2,1,0:T(8,128)S(1)} %pad_maximum_fusion.1), channel_id=1, source_target_pairs={{0,1},{1,0},{2,3},{3,2},{4,5},{5,4},{6,7},{7,6},{8,9},{9,8},{10,11... | collective-permute-start | bytes 393224 | tf_op jit(solution)/shard_map/ppermute | solution.py:20
  31.8 1.0 collective-permute-done.4
  32.8 3.6 %collective-permute-start.5 = (f32[2,64,256]{2,1,0:T(8,128)S(1)}, f32[2,64,256]{2,1,0:T(8,128)S(1)}, u32[]{:S(2)}, u32[]{:S(2)}) collective-permute-start(f32[2,64,256]{2,1,0:T(8,128)S(1)} %fusion.46), channel_id=1, source_target_pairs={{0,2},{1,3},{2,0},{3,1},{4,6},{5,7},{6,4},{7,5},{8,10},{9,11},{10,... | collective-permute-start | bytes 393224 | tf_op jit(solution)/shard_map/ppermute | solution.py:20
  36.4 4.0 %collective-permute-done.5 = f32[2,64,256]{2,1,0:T(8,128)S(1)} collective-permute-done((f32[2,64,256]{2,1,0:T(8,128)S(1)}, f32[2,64,256]{2,1,0:T(8,128)S(1)}, u32[]{:S(2)}, u32[]{:S(2)}) %collective-permute-start.5) | collective-permute-done | bytes 131104 | tf_op jit(solution)/shard_map/ppermute | solution.py:20
  40.5 0.7 fusion.71
  41.2 7.1 %collective-permute-start.6 = (f32[2,64,256]{2,1,0:T(8,128)}, f32[2,64,256]{2,1,0:T(8,128)}, u32[]{:S(2)}, u32[]{:S(2)}) collective-permute-start(f32[2,64,256]{2,1,0:T(8,128)} %fusion.71), channel_id=1, source_target_pairs={{0,4},{1,5},{2,6},{3,7},{4,0},{5,1},{6,2},{7,3},{8,12},{9,13},{10,... | collective-permute-start | bytes 393224 | tf_op jit(solution)/shard_map/ppermute | solution.py:20
  48.3 0.7 gather_fusion.2
  48.9 5.9 %collective-permute-done.6 = f32[2,64,256]{2,1,0:T(8,128)} collective-permute-done((f32[2,64,256]{2,1,0:T(8,128)}, f32[2,64,256]{2,1,0:T(8,128)}, u32[]{:S(2)}, u32[]{:S(2)}) %collective-permute-start.6) | collective-permute-done | bytes 131104 | tf_op jit(solution)/shard_map/ppermute | solution.py:20
  54.8 1.0 add.157
  55.8 4.7 %collective-permute-start.7 = (f32[2,64,256]{2,1,0:T(8,128)S(1)}, f32[2,64,256]{2,1,0:T(8,128)S(1)}, u32[]{:S(2)}, u32[]{:S(2)}) collective-permute-start(f32[2,64,256]{2,1,0:T(8,128)S(1)} %add.157), channel_id=1, source_target_pairs={{0,8},{1,9},{2,10},{3,11},{4,12},{5,13},{6,14},{7,15},{8,0},{9,1},... | collective-permute-start | bytes 393224 | tf_op jit(solution)/shard_map/ppermute | solution.py:20
  60.6 2.7 %fusion.4 = bf16[8,128,256]{2,1,0:T(8,128)(2,1)} fusion(bf16[8,4,128,256]{3,2,1,0:T(8,128)(2,1)S(1)} %bitcast.152, bf16[8,4,128,128]{3,2,1,0:T(8,128)(2,1)} %param.11, pred[8,4]{1,0:T(8,128)(4,1)S(1)} %iota_compare_fusion.3), kind=kOutput, calls=%fused_computation.17 | convolution fusion | flops 269221888 | bytes 3670048 | tf_op jit(solution)/shard_map/bkij,bkjh->bih/dot_general | solution.py:131
  63.2 5.8 %collective-permute-done.7 = f32[2,64,256]{2,1,0:T(8,128)S(1)} collective-permute-done((f32[2,64,256]{2,1,0:T(8,128)S(1)}, f32[2,64,256]{2,1,0:T(8,128)S(1)}, u32[]{:S(2)}, u32[]{:S(2)}) %collective-permute-start.7) | collective-permute-done | bytes 131104 | tf_op jit(solution)/shard_map/ppermute | solution.py:20
  69.0 0.1 slice_reduce_fusion
  69.2 0.2 multiply_reduce_fusion.1
  69.5 0.2 fusion.21
  69.7 0.3 fusion.47
  70.0 0.9 fusion.2
  70.9 0.3 convolution_convert_fusion.1
  71.3 0.2 fusion.34
  71.5 0.1 copy.230
  71.7 0.3 copy-done.10
  72.0 0.3 fusion.56
  72.4 2.1 %collective-permute-start.8 = (f32[512,128]{1,0:T(8,128)S(1)}, f32[512,128]{1,0:T(8,128)S(1)}, u32[]{:S(2)}, u32[]{:S(2)}) collective-permute-start(f32[512,128]{1,0:T(8,128)S(1)} %select_bitcast_fusion), channel_id=1, source_target_pairs={{0,1},{1,0},{2,3},{3,2},{4,5},{5,4},{6,7},{7,6},{8,9},{9,8},{10,11... | collective-permute-start | bytes 786440 | tf_op jit(solution)/shard_map/ppermute | solution.py:40
  74.5 1.5 collective-permute-done.8
  76.0 0.2 fusion.48
  76.2 1.9 %collective-permute-start.9 = (f32[256,128]{1,0:T(8,128)S(1)}, f32[256,128]{1,0:T(8,128)S(1)}, u32[]{:S(2)}, u32[]{:S(2)}) collective-permute-start(f32[256,128]{1,0:T(8,128)S(1)} %select_bitcast_fusion.1), channel_id=1, source_target_pairs={{0,2},{1,3},{2,0},{3,1},{4,6},{5,7},{6,4},{7,5},{8,10},{9,11},{10,... | collective-permute-start | bytes 393224 | tf_op jit(solution)/shard_map/ppermute | solution.py:40
  78.2 5.5 %collective-permute-done.9 = f32[256,128]{1,0:T(8,128)S(1)} collective-permute-done((f32[256,128]{1,0:T(8,128)S(1)}, f32[256,128]{1,0:T(8,128)S(1)}, u32[]{:S(2)}, u32[]{:S(2)}) %collective-permute-start.9) | collective-permute-done | bytes 131104 | tf_op jit(solution)/shard_map/ppermute | solution.py:40
  83.7 0.1 fusion.49
  83.8 2.3 %collective-permute-start.10 = (f32[128,128]{1,0:T(8,128)S(1)}, f32[128,128]{1,0:T(8,128)S(1)}, u32[]{:S(2)}, u32[]{:S(2)}) collective-permute-start(f32[128,128]{1,0:T(8,128)S(1)} %bitcast.170), channel_id=1, source_target_pairs={{0,4},{1,5},{2,6},{3,7},{4,0},{5,1},{6,2},{7,3},{8,12},{9,13},{10,... | collective-permute-start | bytes 196616 | tf_op jit(solution)/shard_map/ppermute | solution.py:40
  86.1 5.2 %collective-permute-done.10 = f32[128,128]{1,0:T(8,128)S(1)} collective-permute-done((f32[128,128]{1,0:T(8,128)S(1)}, f32[128,128]{1,0:T(8,128)S(1)}, u32[]{:S(2)}, u32[]{:S(2)}) %collective-permute-start.10) | collective-permute-done | bytes 65568 | tf_op jit(solution)/shard_map/ppermute | solution.py:40
  91.4 4.5 %collective-permute-start.11 = (f32[64,128]{1,0:T(8,128)S(1)}, f32[64,128]{1,0:T(8,128)S(1)}, u32[]{:S(2)}, u32[]{:S(2)}) collective-permute-start(f32[64,128]{1,0:T(8,128)S(1)} %bitcast.174), channel_id=1, source_target_pairs={{0,8},{1,9},{2,10},{3,11},{4,12},{5,13},{6,14},{7,15},{8,0},{9,1},... | collective-permute-start | bytes 98312 | tf_op jit(solution)/shard_map/ppermute | solution.py:40
  95.9 5.6 %collective-permute-done.11 = f32[64,128]{1,0:T(8,128)S(1)} collective-permute-done((f32[64,128]{1,0:T(8,128)S(1)}, f32[64,128]{1,0:T(8,128)S(1)}, u32[]{:S(2)}, u32[]{:S(2)}) %collective-permute-start.11) | collective-permute-done | bytes 32800 | tf_op jit(solution)/shard_map/ppermute | solution.py:40
  101.5 1.9 %collective-permute-start.12 = (f32[32,128]{1,0:T(8,128)S(1)}, f32[32,128]{1,0:T(8,128)S(1)}, u32[]{:S(2)}, u32[]{:S(2)}) collective-permute-start(f32[32,128]{1,0:T(8,128)S(1)} %bitcast.178), channel_id=1, source_target_pairs={{0,16},{16,0},{32,48},{48,32},{64,80},{80,64},{96,112},{112,96},{1... | collective-permute-start | bytes 49160 | tf_op jit(solution)/shard_map/ppermute | solution.py:40
  103.5 3.7 %collective-permute-done.12 = f32[32,128]{1,0:T(8,128)S(1)} collective-permute-done((f32[32,128]{1,0:T(8,128)S(1)}, f32[32,128]{1,0:T(8,128)S(1)}, u32[]{:S(2)}, u32[]{:S(2)}) %collective-permute-start.12) | collective-permute-done | bytes 16416 | tf_op jit(solution)/shard_map/ppermute | solution.py:40
  107.2 1.9 %collective-permute-start.13 = (f32[16,128]{1,0:T(8,128)S(1)}, f32[16,128]{1,0:T(8,128)S(1)}, u32[]{:S(2)}, u32[]{:S(2)}) collective-permute-start(f32[16,128]{1,0:T(8,128)S(1)} %bitcast.185), channel_id=1, source_target_pairs={{0,32},{16,48},{32,0},{48,16},{64,96},{80,112},{96,64},{112,80},{1... | collective-permute-start | bytes 24584 | tf_op jit(solution)/shard_map/ppermute | solution.py:40
  109.1 4.5 %collective-permute-done.13 = f32[16,128]{1,0:T(8,128)S(1)} collective-permute-done((f32[16,128]{1,0:T(8,128)S(1)}, f32[16,128]{1,0:T(8,128)S(1)}, u32[]{:S(2)}, u32[]{:S(2)}) %collective-permute-start.13) | collective-permute-done | bytes 8224 | tf_op jit(solution)/shard_map/ppermute | solution.py:40
  113.6 2.9 %collective-permute-start.14 = (f32[8,128]{1,0:T(8,128)S(1)}, f32[8,128]{1,0:T(8,128)S(1)}, u32[]{:S(2)}, u32[]{:S(2)}) collective-permute-start(f32[8,128]{1,0:T(8,128)S(1)} %bitcast.186), channel_id=1, source_target_pairs={{0,64},{16,80},{32,96},{48,112},{64,0},{80,16},{96,32},{112,48},{1... | collective-permute-start | bytes 12296 | tf_op jit(solution)/shard_map/ppermute | solution.py:40
  116.6 6.5 %collective-permute-done.14 = f32[8,128]{1,0:T(8,128)S(1)} collective-permute-done((f32[8,128]{1,0:T(8,128)S(1)}, f32[8,128]{1,0:T(8,128)S(1)}, u32[]{:S(2)}, u32[]{:S(2)}) %collective-permute-start.14) | collective-permute-done | bytes 4128 | tf_op jit(solution)/shard_map/ppermute | solution.py:40
  123.1 5.2 %collective-permute-start.15 = (f32[4,128]{1,0:T(4,128)S(1)}, f32[4,128]{1,0:T(4,128)S(1)}, u32[]{:S(2)}, u32[]{:S(2)}) collective-permute-start(f32[4,128]{1,0:T(4,128)S(1)} %bitcast.189), channel_id=1, source_target_pairs={{0,128},{16,144},{32,160},{48,176},{64,192},{80,208},{96,224},{112... | collective-permute-start | bytes 6152 | tf_op jit(solution)/shard_map/ppermute | solution.py:40
  128.3 1.5 collective-permute-done.15
  129.8 7.9 %collective-permute-start.16 = (f32[2,128]{1,0:T(2,128)S(1)}, f32[2,128]{1,0:T(2,128)S(1)}, u32[]{:S(2)}, u32[]{:S(2)}) collective-permute-start(f32[2,128]{1,0:T(2,128)S(1)} %bitcast.190), channel_id=1, source_target_pairs={{0,256},{16,272},{32,288},{48,304},{64,320},{80,336},{96,352},{112... | collective-permute-start | bytes 3080 | tf_op jit(solution)/shard_map/ppermute | solution.py:40
  137.8 1.5 collective-permute-done.16
  139.3 11.9 %collective-permute-start.17 = (f32[1,128]{1,0:T(1,128)S(1)}, f32[1,128]{1,0:T(1,128)S(1)}, u32[]{:S(2)}, u32[]{:S(2)}) collective-permute-start(f32[1,128]{1,0:T(1,128)S(1)} %fusion.41), channel_id=1, source_target_pairs={{0,512},{16,528},{32,544},{48,560},{64,576},{80,592},{96,608},{112... | collective-permute-start | bytes 1544 | tf_op jit(solution)/shard_map/ppermute | solution.py:40
  151.2 1.3 fusion.1
  152.4 0.2 collective-permute-done.17
  152.7 0.5 fusion.40
  (71 shorter events, 1.0 us)
Async XLA Ops:
  0.6 19.4 %copy-start = (bf16[256,256]{1,0:T(8,128)(2,1)S(1)}, bf16[256,256]{1,0:T(8,128)(2,1)}, u32[]{:S(2)}) copy-start(bf16[256,256]{1,0:T(8,128)(2,1)} %param.16) | copy-start | bytes 393220
  0.6 4.3 %copy-start.14 = (s32[128]{0:T(128)S(1)}, s32[128]{0:T(128)}, u32[]{:S(2)}) copy-start(s32[128]{0:T(128)} %param.14) | copy-start | bytes 1540
  0.7 15.5 %copy-start.13 = (s32[8,4]{0,1:T(4,128)S(1)}, s32[8,4]{0,1:T(4,128)}, u32[]{:S(2)}) copy-start(s32[8,4]{0,1:T(4,128)} %param.12) | copy-start | bytes 388
  0.7 15.6 %copy-start.15 = (s32[8]{0:T(128)S(1)}, s32[8]{0:T(128)}, u32[]{:S(2)}) copy-start(s32[8]{0:T(128)} %param.13) | copy-start | bytes 100
  0.7 15.7 %copy-start.5 = (bf16[512,256]{1,0:T(8,128)(2,1)S(1)}, bf16[512,256]{1,0:T(8,128)(2,1)}, u32[]{:S(2)}) copy-start(bf16[512,256]{1,0:T(8,128)(2,1)} %param.17) | copy-start | bytes 786436
  3.4 13.2 %copy-start.8 = (bf16[1024,256]{1,0:T(8,128)(2,1)S(1)}, bf16[1024,256]{1,0:T(8,128)(2,1)}, u32[]{:S(2)}) copy-start(bf16[1024,256]{1,0:T(8,128)(2,1)} %param.19) | copy-start | bytes 1572868
  3.4 13.2 %copy-start.12 = (s32[1024]{0:T(1024)S(1)}, s32[1024]{0:T(1024)}, u32[]{:S(2)}) copy-start(s32[1024]{0:T(1024)} %param.15) | copy-start | bytes 12292
  6.4 10.8 %collective-permute-start = (bf16[128,256]{1,0:T(8,128)(2,1)}, bf16[128,256]{1,0:T(8,128)(2,1)}, u32[]{:S(2)}, u32[]{:S(2)}) collective-permute-start(bf16[128,256]{1,0:T(8,128)(2,1)} %gather_fusion), channel_id=1, source_target_pairs={{0,16},{16,32},{32,48},{48,64},{64,80},{80,96},{96,112},{112,128},... | collective-permute-start | bytes 196616 | tf_op jit(solution)/shard_map/ppermute | solution.py:50
  8.9 9.1 %collective-permute-start.1 = (bf16[128,256]{1,0:T(8,128)(2,1)}, bf16[128,256]{1,0:T(8,128)(2,1)S(1)}, u32[]{:S(2)}, u32[]{:S(2)}) collective-permute-start(bf16[128,256]{1,0:T(8,128)(2,1)} %gather_fusion), channel_id=1, source_target_pairs={{16,0},{32,16},{48,32},{64,48},{80,64},{96,80},{112,96},{128,112},... | collective-permute-start | bytes 196616 | tf_op jit(solution)/shard_map/ppermute | solution.py:51
  13.5 4.6 %collective-permute-start.2 = (bf16[128,256]{1,0:T(8,128)(2,1)}, bf16[128,256]{1,0:T(8,128)(2,1)S(1)}, u32[]{:S(2)}, u32[]{:S(2)}) collective-permute-start(bf16[128,256]{1,0:T(8,128)(2,1)} %gather_fusion), channel_id=1, source_target_pairs={{0,1},{1,2},{2,3},{3,4},{4,5},{5,6},{6,7},{7,8},{8,9},{9,10},{10,1... | collective-permute-start | bytes 196616 | tf_op jit(solution)/shard_map/ppermute | solution.py:50
  14.8 5.3 %collective-permute-start.3 = (bf16[128,256]{1,0:T(8,128)(2,1)}, bf16[128,256]{1,0:T(8,128)(2,1)S(1)}, u32[]{:S(2)}, u32[]{:S(2)}) collective-permute-start(bf16[128,256]{1,0:T(8,128)(2,1)} %gather_fusion), channel_id=1, source_target_pairs={{1,0},{2,1},{3,2},{4,3},{5,4},{6,5},{7,6},{8,7},{9,8},{10,9},{11,1... | collective-permute-start | bytes 196616 | tf_op jit(solution)/shard_map/ppermute | solution.py:51
  22.4 2.5 %copy-start.6 = (bf16[512,256]{1,0:T(8,128)(2,1)S(1)}, bf16[512,256]{1,0:T(8,128)(2,1)}, u32[]{:S(2)}) copy-start(bf16[512,256]{1,0:T(8,128)(2,1)} %param.17) | copy-start | bytes 786436
  24.9 1.0 copy-start.1
  26.0 1.0 copy-start.2
  27.0 5.8 %collective-permute-start.4 = (f32[2,64,256]{2,1,0:T(8,128)S(1)}, f32[2,64,256]{2,1,0:T(8,128)S(1)}, u32[]{:S(2)}, u32[]{:S(2)}) collective-permute-start(f32[2,64,256]{2,1,0:T(8,128)S(1)} %pad_maximum_fusion.1), channel_id=1, source_target_pairs={{0,1},{1,0},{2,3},{3,2},{4,5},{5,4},{6,7},{7,6},{8,9},{9,8},{10,11... | collective-permute-start | bytes 393224 | tf_op jit(solution)/shard_map/ppermute | solution.py:20
  32.8 7.7 %collective-permute-start.5 = (f32[2,64,256]{2,1,0:T(8,128)S(1)}, f32[2,64,256]{2,1,0:T(8,128)S(1)}, u32[]{:S(2)}, u32[]{:S(2)}) collective-permute-start(f32[2,64,256]{2,1,0:T(8,128)S(1)} %fusion.46), channel_id=1, source_target_pairs={{0,2},{1,3},{2,0},{3,1},{4,6},{5,7},{6,4},{7,5},{8,10},{9,11},{10,... | collective-permute-start | bytes 393224 | tf_op jit(solution)/shard_map/ppermute | solution.py:20
  41.2 13.6 %collective-permute-start.6 = (f32[2,64,256]{2,1,0:T(8,128)}, f32[2,64,256]{2,1,0:T(8,128)}, u32[]{:S(2)}, u32[]{:S(2)}) collective-permute-start(f32[2,64,256]{2,1,0:T(8,128)} %fusion.71), channel_id=1, source_target_pairs={{0,4},{1,5},{2,6},{3,7},{4,0},{5,1},{6,2},{7,3},{8,12},{9,13},{10,... | collective-permute-start | bytes 393224 | tf_op jit(solution)/shard_map/ppermute | solution.py:20
  55.8 13.2 %collective-permute-start.7 = (f32[2,64,256]{2,1,0:T(8,128)S(1)}, f32[2,64,256]{2,1,0:T(8,128)S(1)}, u32[]{:S(2)}, u32[]{:S(2)}) collective-permute-start(f32[2,64,256]{2,1,0:T(8,128)S(1)} %add.157), channel_id=1, source_target_pairs={{0,8},{1,9},{2,10},{3,11},{4,12},{5,13},{6,14},{7,15},{8,0},{9,1},... | collective-permute-start | bytes 393224 | tf_op jit(solution)/shard_map/ppermute | solution.py:20
  60.5 8.9 %copy-start.11 = (bf16[256,256]{1,0:T(8,128)(2,1)S(1)}, bf16[256,256]{1,0:T(8,128)(2,1)}, u32[]{:S(2)}) copy-start(bf16[256,256]{1,0:T(8,128)(2,1)} %param.18) | copy-start | bytes 393220
  60.5 9.4 %copy-start.3 = (f32[1024,256]{1,0:T(8,128)S(1)}, f32[1024,256]{1,0:T(8,128)}, u32[]{:S(2)}) copy-start(f32[1024,256]{1,0:T(8,128)} %copy-done.2) | copy-start | bytes 3145732
  60.6 9.4 %copy-start.9 = (bf16[1024,256]{1,0:T(8,128)(2,1)S(1)}, bf16[1024,256]{1,0:T(8,128)(2,1)}, u32[]{:S(2)}) copy-start(bf16[1024,256]{1,0:T(8,128)(2,1)} %param.19) | copy-start | bytes 1572868
  70.0 1.0 copy-start.7
  70.9 1.0 copy-start.10
  72.4 78.8 %copy-start.4 = (f32[1024,256]{1,0:T(8,128)S(1)}, f32[1024,256]{1,0:T(8,128)}, u32[]{:S(2)}) copy-start(f32[1024,256]{1,0:T(8,128)} %copy-done.2) | copy-start | bytes 3145732
  72.4 3.6 %collective-permute-start.8 = (f32[512,128]{1,0:T(8,128)S(1)}, f32[512,128]{1,0:T(8,128)S(1)}, u32[]{:S(2)}, u32[]{:S(2)}) collective-permute-start(f32[512,128]{1,0:T(8,128)S(1)} %select_bitcast_fusion), channel_id=1, source_target_pairs={{0,1},{1,0},{2,3},{3,2},{4,5},{5,4},{6,7},{7,6},{8,9},{9,8},{10,11... | collective-permute-start | bytes 786440 | tf_op jit(solution)/shard_map/ppermute | solution.py:40
  76.2 7.4 %collective-permute-start.9 = (f32[256,128]{1,0:T(8,128)S(1)}, f32[256,128]{1,0:T(8,128)S(1)}, u32[]{:S(2)}, u32[]{:S(2)}) collective-permute-start(f32[256,128]{1,0:T(8,128)S(1)} %select_bitcast_fusion.1), channel_id=1, source_target_pairs={{0,2},{1,3},{2,0},{3,1},{4,6},{5,7},{6,4},{7,5},{8,10},{9,11},{10,... | collective-permute-start | bytes 393224 | tf_op jit(solution)/shard_map/ppermute | solution.py:40
  83.8 7.5 %collective-permute-start.10 = (f32[128,128]{1,0:T(8,128)S(1)}, f32[128,128]{1,0:T(8,128)S(1)}, u32[]{:S(2)}, u32[]{:S(2)}) collective-permute-start(f32[128,128]{1,0:T(8,128)S(1)} %bitcast.170), channel_id=1, source_target_pairs={{0,4},{1,5},{2,6},{3,7},{4,0},{5,1},{6,2},{7,3},{8,12},{9,13},{10,... | collective-permute-start | bytes 196616 | tf_op jit(solution)/shard_map/ppermute | solution.py:40
  91.4 10.1 %collective-permute-start.11 = (f32[64,128]{1,0:T(8,128)S(1)}, f32[64,128]{1,0:T(8,128)S(1)}, u32[]{:S(2)}, u32[]{:S(2)}) collective-permute-start(f32[64,128]{1,0:T(8,128)S(1)} %bitcast.174), channel_id=1, source_target_pairs={{0,8},{1,9},{2,10},{3,11},{4,12},{5,13},{6,14},{7,15},{8,0},{9,1},... | collective-permute-start | bytes 98312 | tf_op jit(solution)/shard_map/ppermute | solution.py:40
  101.5 5.6 %collective-permute-start.12 = (f32[32,128]{1,0:T(8,128)S(1)}, f32[32,128]{1,0:T(8,128)S(1)}, u32[]{:S(2)}, u32[]{:S(2)}) collective-permute-start(f32[32,128]{1,0:T(8,128)S(1)} %bitcast.178), channel_id=1, source_target_pairs={{0,16},{16,0},{32,48},{48,32},{64,80},{80,64},{96,112},{112,96},{1... | collective-permute-start | bytes 49160 | tf_op jit(solution)/shard_map/ppermute | solution.py:40
  107.2 6.4 %collective-permute-start.13 = (f32[16,128]{1,0:T(8,128)S(1)}, f32[16,128]{1,0:T(8,128)S(1)}, u32[]{:S(2)}, u32[]{:S(2)}) collective-permute-start(f32[16,128]{1,0:T(8,128)S(1)} %bitcast.185), channel_id=1, source_target_pairs={{0,32},{16,48},{32,0},{48,16},{64,96},{80,112},{96,64},{112,80},{1... | collective-permute-start | bytes 24584 | tf_op jit(solution)/shard_map/ppermute | solution.py:40
  113.6 9.4 %collective-permute-start.14 = (f32[8,128]{1,0:T(8,128)S(1)}, f32[8,128]{1,0:T(8,128)S(1)}, u32[]{:S(2)}, u32[]{:S(2)}) collective-permute-start(f32[8,128]{1,0:T(8,128)S(1)} %bitcast.186), channel_id=1, source_target_pairs={{0,64},{16,80},{32,96},{48,112},{64,0},{80,16},{96,32},{112,48},{1... | collective-permute-start | bytes 12296 | tf_op jit(solution)/shard_map/ppermute | solution.py:40
  123.1 6.8 %collective-permute-start.15 = (f32[4,128]{1,0:T(4,128)S(1)}, f32[4,128]{1,0:T(4,128)S(1)}, u32[]{:S(2)}, u32[]{:S(2)}) collective-permute-start(f32[4,128]{1,0:T(4,128)S(1)} %bitcast.189), channel_id=1, source_target_pairs={{0,128},{16,144},{32,160},{48,176},{64,192},{80,208},{96,224},{112... | collective-permute-start | bytes 6152 | tf_op jit(solution)/shard_map/ppermute | solution.py:40
  129.8 9.4 %collective-permute-start.16 = (f32[2,128]{1,0:T(2,128)S(1)}, f32[2,128]{1,0:T(2,128)S(1)}, u32[]{:S(2)}, u32[]{:S(2)}) collective-permute-start(f32[2,128]{1,0:T(2,128)S(1)} %bitcast.190), channel_id=1, source_target_pairs={{0,256},{16,272},{32,288},{48,304},{64,320},{80,336},{96,352},{112... | collective-permute-start | bytes 3080 | tf_op jit(solution)/shard_map/ppermute | solution.py:40
  139.3 13.4 %collective-permute-start.17 = (f32[1,128]{1,0:T(1,128)S(1)}, f32[1,128]{1,0:T(1,128)S(1)}, u32[]{:S(2)}, u32[]{:S(2)}) collective-permute-start(f32[1,128]{1,0:T(1,128)S(1)} %fusion.41), channel_id=1, source_target_pairs={{0,512},{16,528},{32,544},{48,560},{64,576},{80,592},{96,608},{112... | collective-permute-start | bytes 1544 | tf_op jit(solution)/shard_map/ppermute | solution.py:40

commit v2 on v0

--- a/solution.py
+++ b/solution.py
@@ -9,17 +9,26 @@
 eps = 1e-05
 
 
-def extended(block, sides, width):
-    for axis, dim in sides:
+def scatter_sum(pieces, axes):
+    return lax.all_to_all(pieces, axes, 0, 0, tiled=False).sum(0)
+
+
+def all_sum(values, axis):
+    count = lax.axis_size(axis)
+    mine = scatter_sum(values.reshape(count, -1), axis)
+    gathered = lax.all_to_all(jnp.broadcast_to(mine, (count,) + mine.shape), axis, 0, 0, tiled=False)
+    return gathered.reshape(values.shape)
+
+
+def neighbour_tiles(tile):
+    tiles = []
+    for axis in ("along", "across"):
         count = lax.axis_size(axis)
         forward = [(i, i + 1) for i in range(count - 1)]
-        backward = [(target, source) for source, target in forward]
-        low = lax.ppermute(
-            lax.slice_in_dim(block, block.shape[dim] - width, None, axis=dim), axis, forward
-        )
-        high = lax.ppermute(lax.slice_in_dim(block, 0, width, axis=dim), axis, backward)
-        block = jnp.concatenate([low, block, high], axis=dim)
-    return block
+        backward = [(i + 1, i) for i in range(count - 1)]
+        tiles.append(lax.ppermute(tile, axis, forward))
+        tiles.append(lax.ppermute(tile, axis, backward))
+    return jnp.stack(tiles)
 
 
 def normalize(values):
@@ -84,8 +93,7 @@
     normed, _ = normalize(inputs)
     scaled = normed.astype(jnp.bfloat16)
     rim_rows = scaled[bnd_index]
-    padded = extended(rim_rows[None, None], (("along", 0), ("across", 1)), 1)
-    halo_tiles = jnp.stack([padded[0, 1], padded[2, 1], padded[1, 0], padded[1, 2]])
+    halo_tiles = neighbour_tiles(rim_rows)
     sources = jnp.concatenate(
         [scaled.reshape(blocks, tile_rows, feature_count), halo_tiles], axis=0
     )
@@ -114,16 +122,25 @@
     assign_bits = assign_float.astype(jnp.bfloat16)
     pooled_part = transposed_times(assign_float, hidden_one, lax.Precision.HIGHEST)
     cot_part = transposed_times(assign_bits, cotangent)
-    pooled, coarse_cot = lax.psum((pooled_part, cot_part), "across")
+    pooled, coarse_cot = all_sum(jnp.stack([pooled_part, cot_part]), "across")
     coarse_norm, inverse, coarse, coarse_pre, coarse_out = coarse_forward(pooled, w_coarse)
     hidden_two = hidden_one + jnp.dot(assign_bits, coarse_out, preferred_element_type=jnp.float32)
     coarse_delta, pooled_delta = coarse_backward(
         coarse_cot, coarse_norm, inverse, coarse_pre, w_coarse
     )
-    start = lax.axis_index("across") * NC_DEV
-    own_coarse = lax.dynamic_slice_in_dim(coarse, start, NC_DEV, 0)
-    own_coarse_delta = lax.dynamic_slice_in_dim(coarse_delta, start, NC_DEV, 0)
-    coarse_grad = transposed_times(own_coarse, own_coarse_delta)
+    along_count = lax.axis_size("along")
+    across_count = lax.axis_size("across")
+    chunk = (feature_count * feature_count) // (along_count * across_count // 2)
+    halves = feature_count // chunk
+    rows_per_step = across_count // halves
+    member = lax.axis_index("across")
+    picked_rows = lax.dynamic_index_in_dim(
+        coarse.reshape(coarse_count, -1, rows_per_step), member // halves, 2, keepdims=False
+    )
+    picked_cols = lax.dynamic_index_in_dim(
+        coarse_delta.reshape(coarse_count, halves, chunk), member % halves, 1, keepdims=False
+    )
+    coarse_grad = transposed_times(picked_rows, picked_cols)
     hidden_delta = cotangent.astype(jnp.float32) + jnp.dot(
         assign_float,
         pooled_delta,
@@ -133,9 +150,10 @@
     update_delta = (hidden_delta * silu_slope(update_pre)).astype(jnp.bfloat16)
     aggregated_delta = times_transposed(update_delta, w_second).astype(jnp.bfloat16)
     message_grad = transposed_times(summed_scaled, aggregated_delta)
-    grad_terms = jnp.concatenate([message_grad.reshape(-1), coarse_grad.reshape(-1)])
-    partial_grads = lax.psum_scatter(grad_terms, "along", scatter_dimension=0, tiled=True)
-    weight_grads = lax.psum_scatter(partial_grads, "across", scatter_dimension=0, tiled=True)
+    message_pieces = message_grad.reshape(-1, across_count, chunk).transpose(1, 0, 2)
+    message_part = scatter_sum(message_pieces, "across")
+    grad_pieces = jnp.concatenate([message_part, coarse_grad], axis=0)
+    weight_grads = scatter_sum(grad_pieces, "along")
     return (hidden_two.astype(jnp.bfloat16), weight_grads)
 
 

time: 389 us -> 123 us (0.32)
  waiting for transfers between devices: 287 us -> 32.5 us
  starting transfers between devices: 21.2 us -> 53.5 us
  blocking collectives: 28.7 us -> 0 us
  between operations: 15.7 us -> 1.07 us
    unnamed x3 -> x0, waiting for transfers between devices: 161 us -> none
    psum x1 -> x0, waiting for transfers between devices: 123 us -> none  [local(): pooled, coarse_cot = lax.psum((pooled_part, cot_part), 'across')]
    all_to_all x0 -> x4, starting transfers between devices: none -> 33 us  [the longest x3 28.9 us: scatter_sum(): return lax.all_to_all(pieces, axes, 0, 0, tiled=False).sum(0)]
    all_to_all x0 -> x4, waiting for transfers between devices: none -> 32.5 us  [the longest x3 25.9 us: scatter_sum(): return lax.all_to_all(pieces, axes, 0, 0, tiled=False).sum(0)]
    unnamed x1 -> x0, blocking collectives: 28.7 us -> none
  transfers between devices with their start and end apart: 6 -> 8, of which waited for: 4 -> 4; matrix products, arithmetic and copies ran while one was open for 2% -> 8% of each run, Pallas kernels for 0% -> 0%
where the time goes in v2:
time: 123 us
  starting transfers between devices  53.5 us (43%)
  waiting for transfers between devices  32.5 us (26%)
  matrix products  16 us (13%)
  local copies, waits for them, and re-layouts  12.2 us (10%)
  other arithmetic  7.25 us (6%)
    all_to_all x3, starting transfers between devices, scatter_sum(): return lax.all_to_all(pieces, axes, 0, 0, tiled=False).sum(0)  28.9 us
    all_to_all x3, waiting for transfers between devices, scatter_sum(): return lax.all_to_all(pieces, axes, 0, 0, tiled=False).sum(0)  25.9 us
    ppermute x2, starting transfers between devices, neighbour_tiles(): tiles.append(lax.ppermute(tile, axis, backward))  11.8 us
    ppermute x2, starting transfers between devices, neighbour_tiles(): tiles.append(lax.ppermute(tile, axis, forward))  8.71 us
    all_to_all x1, waiting for transfers between devices, all_sum(): lax.all_to_all(jnp.broadcast_to(mine, (count,) + mine.shape), axis, 0, 0,...  6.56 us
    all_to_all x1, starting transfers between devices, all_sum(): lax.all_to_all(jnp.broadcast_to(mine, (count,) + mine.shape), axis, 0, 0,...  4.06 us
    dot_general x4, matrix products, transposed_times(): lax.dot_general(operand, second, (((0,), (0,)), ((), ())), precision=prec...  3.38 us
    dot_general x1, matrix products, local(): jnp.einsum('bkij,bkjh->bih', masked_tiles, sources[adj_index], preferred_...  2.53 us
  transfers between devices with their start and end apart: 8, of which 4 were waited for; matrix products, arithmetic and copies ran while one was open for 8% of the time, Pallas kernels for 0%

profile of v2, /device:TPU:1, one launch (start us, length us, event | category | flops | bytes accessed | tf_op | source)
XLA Modules:
  0.0 122.5 jit_solution(3884227482175645479)
XLA Ops:
  0.6 0.0 copy-start
  0.6 0.0 copy-start.10
  0.7 0.0 copy-start.9
  0.7 0.0 copy-start.6
  0.7 1.3 %convert_reduce_fusion = f32[1024]{0:T(1024)S(1)} fusion(bf16[1024,256]{1,0:T(8,128)(2,1)} %param.10), kind=kLoop, calls=%fused_computation.6 | loop fusion | flops 523264 | bytes 528384 | tf_op jit(solution)/shard_map/reduce_sum | solution.py:35
  2.0 1.4 %fusion.8 = f32[1024]{0:T(1024)S(1)} fusion(bf16[1024,256]{1,0:T(8,128)(2,1)} %param.10, f32[1024]{0:T(1024)S(1)} %broadcast_multiply_fusion), kind=kLoop, calls=%fused_computation.23 | loop fusion | flops 1047552 | bytes 532480 | tf_op jit(solution)/shard_map/reduce_sum | solution.py:36
  3.4 0.0 copy-start.4
  3.4 0.0 copy-start.8
  3.5 1.4 %fusion.9 = bf16[1024,256]{1,0:T(8,128)(2,1)S(1)} fusion(bf16[1024,256]{1,0:T(8,128)(2,1)} %param.10, f32[1024]{0:T(1024)S(1)} %add_rsqrt_fusion, f32[1024]{0:T(1024)S(1)} %broadcast_multiply_fusion), kind=kLoop, calls=%fused_computation.24 | loop fusion | flops 1048576 | bytes 1056768 | tf_op jit(solution)/shard_map/convert_element_type | solution.py:94
  4.9 0.0 copy-done.10
  4.9 1.5 %gather_fusion = bf16[128,256]{1,0:T(8,128)(2,1)} fusion(bf16[1024,256]{1,0:T(8,128)(2,1)S(1)} %fusion.9, s32[1024]{0:T(1024)S(1)} %pad_clamp_fusion.1), kind=kCustom, calls=%fused_computation | custom fusion | bytes 131584 | tf_op jit(solution)/shard_map/gather | solution.py:95
  6.4 4.6 %collective-permute-start = (bf16[128,256]{1,0:T(8,128)(2,1)}, bf16[128,256]{1,0:T(8,128)(2,1)}, u32[]{:S(2)}, u32[]{:S(2)}) collective-permute-start(bf16[128,256]{1,0:T(8,128)(2,1)} %gather_fusion), channel_id=1, source_target_pairs={{0,16},{16,32},{32,48},{48,64},{64,80},{80,96},{96,112},{112,128},... | collective-permute-start | bytes 196616 | tf_op jit(solution)/shard_map/ppermute | solution.py:29
  11.0 1.3 %collective-permute-start.1 = (bf16[128,256]{1,0:T(8,128)(2,1)}, bf16[128,256]{1,0:T(8,128)(2,1)S(1)}, u32[]{:S(2)}, u32[]{:S(2)}) collective-permute-start(bf16[128,256]{1,0:T(8,128)(2,1)} %gather_fusion), channel_id=1, source_target_pairs={{16,0},{32,16},{48,32},{64,48},{80,64},{96,80},{112,96},{128,112},... | collective-permute-start | bytes 196616 | tf_op jit(solution)/shard_map/ppermute | solution.py:30
  12.3 4.2 %collective-permute-start.2 = (bf16[128,256]{1,0:T(8,128)(2,1)}, bf16[128,256]{1,0:T(8,128)(2,1)S(1)}, u32[]{:S(2)}, u32[]{:S(2)}) collective-permute-start(bf16[128,256]{1,0:T(8,128)(2,1)} %gather_fusion), channel_id=1, source_target_pairs={{0,1},{1,2},{2,3},{3,4},{4,5},{5,6},{6,7},{7,8},{8,9},{9,10},{10,1... | collective-permute-start | bytes 196616 | tf_op jit(solution)/shard_map/ppermute | solution.py:29
  16.4 10.5 %collective-permute-start.3 = (bf16[128,256]{1,0:T(8,128)(2,1)}, bf16[128,256]{1,0:T(8,128)(2,1)S(1)}, u32[]{:S(2)}, u32[]{:S(2)}) collective-permute-start(bf16[128,256]{1,0:T(8,128)(2,1)} %gather_fusion), channel_id=1, source_target_pairs={{1,0},{2,1},{3,2},{4,3},{5,4},{6,5},{7,6},{8,7},{9,8},{10,9},{11,1... | collective-permute-start | bytes 196616 | tf_op jit(solution)/shard_map/ppermute | solution.py:30
  27.0 0.1 copy.16
  27.1 0.1 reshape.128
  27.2 0.1 iota_compare_fusion.3
  27.3 0.0 copy-done.6
  27.3 0.3 fusion.18
  27.6 0.4 convolution_bitcast_fusion.2
  28.1 0.0 collective-permute-done
  28.1 0.8 bitcast_dynamic-update-slice_fusion.3
  28.9 0.0 collective-permute-done.1
  28.9 0.0 collective-permute-done.2
  29.0 0.0 collective-permute-done.3
  29.0 0.4 convolution_convert_fusion
  29.4 2.0 %gather_fusion.1 = bf16[32,128,256]{2,1,0:T(8,128)(2,1)} fusion(bf16[12,128,256]{2,1,0:T(8,128)(2,1)S(1)} %bitcast.54, s32[1024]{0:T(1024)S(1)} %pad_clamp_fusion), kind=kCustom, calls=%fused_computation.1 | custom fusion | bytes 4194432 | tf_op jit(solution)/shard_map/gather | solution.py:107
  31.4 2.5 %fusion.3 = bf16[8,128,256]{2,1,0:T(8,128)(2,1)S(1)} fusion(bf16[8,4,128,256]{3,2,1,0:T(8,128)(2,1)} %bitcast.57, bf16[8,4,128,128]{3,2,1,0:T(8,128)(2,1)} %param.11, pred[8,4]{1,0:T(8,128)(4,1)S(1)} %iota_compare_fusion.3), kind=kOutput, calls=%fused_computation.16 | convolution fusion | flops 269221888 | bytes 3670048 | tf_op jit(solution)/shard_map/bkij,bkjh->bih/dot_general | solution.py:106
  33.9 0.0 copy-done.7
  33.9 0.3 convolution_add_fusion.1
  34.2 0.7 copy-done.1
  34.9 1.0 convolution_bitcast_fusion.3
  35.9 0.0 copy-done.2
  35.9 0.8 all_to_all.25
  36.7 4.1 %all-to-all-start = ((f32[16,1,2048]{2,1,0:T(1,128)}), f32[16,1,2048]{2,1,0:T(1,128)}, u32[]{:S(2)}, u32[]{:S(2)}) async-start(f32[16,1,2048]{2,1,0:T(1,128)} %all_to_all.25), calls=%async_computation | async-start | bytes 262144 | tf_op jit(solution)/shard_map/all_to_all | solution.py:13
  40.8 0.7 gather_fusion.2
  41.5 8.0 %all-to-all-done = f32[16,1,2048]{2,1,0:T(1,128)} async-done(((f32[16,1,2048]{2,1,0:T(1,128)}), f32[16,1,2048]{2,1,0:T(1,128)}, u32[]{:S(2)}, u32[]{:S(2)}) %all-to-all-start) | async-done | bytes 131104 | tf_op jit(solution)/shard_map/all_to_all | solution.py:13
  49.4 1.0 reduce_sum.83
  50.4 0.7 broadcast_in_dim.22
  51.2 4.1 %all-to-all-start.1 = ((f32[16,1,2048]{2,1,0:T(1,128)}), f32[16,1,2048]{2,1,0:T(1,128)}, u32[]{:S(2)}, u32[]{:S(2)}) async-start(f32[16,1,2048]{2,1,0:T(1,128)} %broadcast_in_dim.22), calls=%async_computation.1 | async-start | bytes 262144 | tf_op jit(solution)/shard_map/all_to_all | solution.py:19
  55.2 2.5 %fusion.4 = bf16[8,128,256]{2,1,0:T(8,128)(2,1)} fusion(bf16[8,4,128,256]{3,2,1,0:T(8,128)(2,1)S(1)} %bitcast.56, bf16[8,4,128,128]{3,2,1,0:T(8,128)(2,1)} %param.11, pred[8,4]{1,0:T(8,128)(4,1)S(1)} %iota_compare_fusion.3), kind=kOutput, calls=%fused_computation.17 | convolution fusion | flops 269221888 | bytes 3670048 | tf_op jit(solution)/shard_map/bkij,bkjh->bih/dot_general | solution.py:110
  57.8 6.6 %all-to-all-done.1 = f32[16,1,2048]{2,1,0:T(1,128)} async-done(((f32[16,1,2048]{2,1,0:T(1,128)}), f32[16,1,2048]{2,1,0:T(1,128)}, u32[]{:S(2)}, u32[]{:S(2)}) %all-to-all-start.1) | async-done | bytes 131104 | tf_op jit(solution)/shard_map/all_to_all | solution.py:19
  64.3 1.2 slice_reduce_fusion
  65.6 0.6 unstack.18
  66.2 0.1 reduce_sum.84
  66.3 0.2 multiply_reduce_fusion.1
  66.5 1.7 %multiply_convert_fusion = (bf16[64,256]{1,0:T(8,128)(2,1)S(1)}, f32[64,256]{1,0:T(8,128)}) fusion(f32[64,256]{1,0:T(8,128)S(1)} %unstack.17, bf16[256,256]{1,0:T(8,128)(2,1)} %param.18, f32[64,256]{1,0:T(8,128)S(1)} %unstack.15, f32[64]{0:T(128)S(1)} %add_rsqrt_fusion.1, f32[64]{0:T(128)S(1)} %broadcast_multiply_fusion.3), kind=kOutput, calls=%fused_computation.55 | convolution fusion | flops 8585216 | bytes 360960 | tf_op jit(solution)/shard_map/dot_general | solution.py:64
  68.2 1.2 fusion.42
  69.4 0.6 reshape.117
  70.1 1.6 %fusion.2 = bf16[1024,256]{1,0:T(8,128)(2,1)} fusion(f32[1024,256]{1,0:T(8,128)S(1)} %copy-done.3, bf16[1024,256]{1,0:T(8,128)(2,1)S(1)} %copy-done.5, s32[1024]{0:T(1024)S(1)} %copy-done.8, f32[64,256]{1,0:T(8,128)S(1)} %get-tuple-element.8, f32[64,256]{1,0:T(8,128)S(1)} %unstack.15, f32[64]{0:T(128)S(1)} %get-tuple-element.9, ...), kind=kOutput, calls=%fused_computation.15 | convolution fusion | flops 204374016 | bytes 2233344 | tf_op jit(solution)/shard_map/dot_general | solution.py:144
  71.7 1.8 %fusion.7 = f32[256,256]{1,0:T(8,128)S(1)} fusion(bf16[1024,256]{1,0:T(8,128)(2,1)} %bitcast.59, bf16[1024,256]{1,0:T(8,128)(2,1)} %fusion.2, bf16[512,256]{1,0:T(8,128)(2,1)} %param.17), kind=kOutput, calls=%fused_computation.20 | convolution fusion | flops 268697600 | bytes 1441792 | tf_op jit(solution)/shard_map/dot_general | solution.py:46
  73.6 0.8 copy.28
  74.4 3.4 %all-to-all-start.2 = ((f32[16,32,128]{2,1,0:T(8,128)}), f32[16,32,128]{2,1,0:T(8,128)S(1)}, u32[]{:S(2)}, u32[]{:S(2)}) async-start(f32[16,32,128]{2,1,0:T(8,128)} %bitcast.52), calls=%async_computation.2 | async-start | bytes 524288 | tf_op jit(solution)/shard_map/all_to_all | solution.py:13
  77.8 0.5 fusion.11
  78.3 0.6 copy.19
  78.9 0.8 constant_dynamic-slice_fusion
  79.7 0.1 fusion.37
  79.9 9.2 %all-to-all-done.2 = f32[16,32,128]{2,1,0:T(8,128)S(1)} async-done(((f32[16,32,128]{2,1,0:T(8,128)}), f32[16,32,128]{2,1,0:T(8,128)S(1)}, u32[]{:S(2)}, u32[]{:S(2)}) %all-to-all-start.2) | async-done | bytes 262176 | tf_op jit(solution)/shard_map/all_to_all | solution.py:13
  89.1 0.6 pad_maximum_fusion.1
  89.7 21.4 %all-to-all-start.3 = ((f32[64,1,128]{2,1,0:T(1,128)}), f32[64,1,128]{2,1,0:T(1,128)S(1)}, u32[]{:S(2)}, u32[]{:S(2)}) async-start(f32[64,1,128]{2,1,0:T(1,128)} %bitcast.21), calls=%async_computation.3 | async-start | bytes 65536 | tf_op jit(solution)/shard_map/all_to_all | solution.py:13
  111.1 2.1 %fusion.1 = bf16[1024,256]{1,0:T(8,128)(2,1)} fusion(s32[1024]{0:T(1024)S(1)} %copy-done.8, f32[64,256]{1,0:T(8,128)} %get-tuple-element.7, f32[1024,256]{1,0:T(8,128)S(1)} %copy-done.3, bf16[1024,256]{1,0:T(8,128)(2,1)S(1)} %copy-done.1), kind=kOutput, calls=%fused_computation.14 | convolution fusion | flops 35930112 | bytes 2166784 | tf_op jit(solution)/shard_map/dot_general | solution.py:127
  113.2 8.7 %all-to-all-done.3 = f32[64,1,128]{2,1,0:T(1,128)S(1)} async-done(((f32[64,1,128]{2,1,0:T(1,128)}), f32[64,1,128]{2,1,0:T(1,128)S(1)}, u32[]{:S(2)}, u32[]{:S(2)}) %all-to-all-start.3) | async-done | bytes 32800 | tf_op jit(solution)/shard_map/all_to_all | solution.py:13
  121.9 0.6 reduce_sum.89
  (31 shorter events, 0.2 us)
Async XLA Ops:
  0.6 28.4 %copy-start = (bf16[256,256]{1,0:T(8,128)(2,1)S(1)}, bf16[256,256]{1,0:T(8,128)(2,1)}, u32[]{:S(2)}) copy-start(bf16[256,256]{1,0:T(8,128)(2,1)} %param.16) | copy-start | bytes 393220
  0.6 4.3 %copy-start.10 = (s32[128]{0:T(128)S(1)}, s32[128]{0:T(128)}, u32[]{:S(2)}) copy-start(s32[128]{0:T(128)} %param.14) | copy-start | bytes 1540
  0.7 26.4 %copy-start.9 = (s32[8,4]{0,1:T(4,128)S(1)}, s32[8,4]{0,1:T(4,128)}, u32[]{:S(2)}) copy-start(s32[8,4]{0,1:T(4,128)} %param.12) | copy-start | bytes 388
  0.7 26.5 %copy-start.11 = (s32[8]{0:T(128)S(1)}, s32[8]{0:T(128)}, u32[]{:S(2)}) copy-start(s32[8]{0:T(128)} %param.13) | copy-start | bytes 100
  0.7 26.6 %copy-start.6 = (bf16[512,256]{1,0:T(8,128)(2,1)S(1)}, bf16[512,256]{1,0:T(8,128)(2,1)}, u32[]{:S(2)}) copy-start(bf16[512,256]{1,0:T(8,128)(2,1)} %param.17) | copy-start | bytes 786436
  3.4 24.1 %copy-start.4 = (bf16[1024,256]{1,0:T(8,128)(2,1)S(1)}, bf16[1024,256]{1,0:T(8,128)(2,1)}, u32[]{:S(2)}) copy-start(bf16[1024,256]{1,0:T(8,128)(2,1)} %param.19) | copy-start | bytes 1572868
  3.4 24.1 %copy-start.8 = (s32[1024]{0:T(1024)S(1)}, s32[1024]{0:T(1024)}, u32[]{:S(2)}) copy-start(s32[1024]{0:T(1024)} %param.15) | copy-start | bytes 12292
  6.4 21.7 %collective-permute-start = (bf16[128,256]{1,0:T(8,128)(2,1)}, bf16[128,256]{1,0:T(8,128)(2,1)}, u32[]{:S(2)}, u32[]{:S(2)}) collective-permute-start(bf16[128,256]{1,0:T(8,128)(2,1)} %gather_fusion), channel_id=1, source_target_pairs={{0,16},{16,32},{32,48},{48,64},{64,80},{80,96},{96,112},{112,128},... | collective-permute-start | bytes 196616 | tf_op jit(solution)/shard_map/ppermute | solution.py:29
  11.0 18.0 %collective-permute-start.1 = (bf16[128,256]{1,0:T(8,128)(2,1)}, bf16[128,256]{1,0:T(8,128)(2,1)S(1)}, u32[]{:S(2)}, u32[]{:S(2)}) collective-permute-start(bf16[128,256]{1,0:T(8,128)(2,1)} %gather_fusion), channel_id=1, source_target_pairs={{16,0},{32,16},{48,32},{64,48},{80,64},{96,80},{112,96},{128,112},... | collective-permute-start | bytes 196616 | tf_op jit(solution)/shard_map/ppermute | solution.py:30
  12.3 16.7 %collective-permute-start.2 = (bf16[128,256]{1,0:T(8,128)(2,1)}, bf16[128,256]{1,0:T(8,128)(2,1)S(1)}, u32[]{:S(2)}, u32[]{:S(2)}) collective-permute-start(bf16[128,256]{1,0:T(8,128)(2,1)} %gather_fusion), channel_id=1, source_target_pairs={{0,1},{1,2},{2,3},{3,4},{4,5},{5,6},{6,7},{7,8},{8,9},{9,10},{10,1... | collective-permute-start | bytes 196616 | tf_op jit(solution)/shard_map/ppermute | solution.py:29
  16.4 12.5 %collective-permute-start.3 = (bf16[128,256]{1,0:T(8,128)(2,1)}, bf16[128,256]{1,0:T(8,128)(2,1)S(1)}, u32[]{:S(2)}, u32[]{:S(2)}) collective-permute-start(bf16[128,256]{1,0:T(8,128)(2,1)} %gather_fusion), channel_id=1, source_target_pairs={{1,0},{2,1},{3,2},{4,3},{5,4},{6,5},{7,6},{8,7},{9,8},{10,9},{11,1... | collective-permute-start | bytes 196616 | tf_op jit(solution)/shard_map/ppermute | solution.py:30
  31.4 2.5 %copy-start.7 = (bf16[512,256]{1,0:T(8,128)(2,1)S(1)}, bf16[512,256]{1,0:T(8,128)(2,1)}, u32[]{:S(2)}) copy-start(bf16[512,256]{1,0:T(8,128)(2,1)} %param.17) | copy-start | bytes 786436
  33.8 1.0 copy-start.1
  34.9 1.0 copy-start.2
  36.7 12.8 %all-to-all-start = ((f32[16,1,2048]{2,1,0:T(1,128)}), f32[16,1,2048]{2,1,0:T(1,128)}, u32[]{:S(2)}, u32[]{:S(2)}) async-start(f32[16,1,2048]{2,1,0:T(1,128)} %all_to_all.25), calls=%async_computation | async-start | bytes 262144 | tf_op jit(solution)/shard_map/all_to_all | solution.py:13
  51.2 13.2 %all-to-all-start.1 = ((f32[16,1,2048]{2,1,0:T(1,128)}), f32[16,1,2048]{2,1,0:T(1,128)}, u32[]{:S(2)}, u32[]{:S(2)}) async-start(f32[16,1,2048]{2,1,0:T(1,128)} %broadcast_in_dim.22), calls=%async_computation.1 | async-start | bytes 262144 | tf_op jit(solution)/shard_map/all_to_all | solution.py:19
  57.8 12.3 %copy-start.3 = (f32[1024,256]{1,0:T(8,128)S(1)}, f32[1024,256]{1,0:T(8,128)}, u32[]{:S(2)}) copy-start(f32[1024,256]{1,0:T(8,128)} %copy-done.2) | copy-start | bytes 3145732
  57.8 12.3 %copy-start.5 = (bf16[1024,256]{1,0:T(8,128)(2,1)S(1)}, bf16[1024,256]{1,0:T(8,128)(2,1)}, u32[]{:S(2)}) copy-start(bf16[1024,256]{1,0:T(8,128)(2,1)} %param.19) | copy-start | bytes 1572868
  74.4 14.7 %all-to-all-start.2 = ((f32[16,32,128]{2,1,0:T(8,128)}), f32[16,32,128]{2,1,0:T(8,128)S(1)}, u32[]{:S(2)}, u32[]{:S(2)}) async-start(f32[16,32,128]{2,1,0:T(8,128)} %bitcast.52), calls=%async_computation.2 | async-start | bytes 524288 | tf_op jit(solution)/shard_map/all_to_all | solution.py:13
  89.7 32.2 %all-to-all-start.3 = ((f32[64,1,128]{2,1,0:T(1,128)}), f32[64,1,128]{2,1,0:T(1,128)S(1)}, u32[]{:S(2)}, u32[]{:S(2)}) async-start(f32[64,1,128]{2,1,0:T(1,128)} %bitcast.21), calls=%async_computation.3 | async-start | bytes 65536 | tf_op jit(solution)/shard_map/all_to_all | solution.py:13

commit v3 on v2

--- a/solution.py
+++ b/solution.py
@@ -9,13 +9,14 @@
 eps = 1e-05
 
 
-def scatter_sum(pieces, axes):
-    return lax.all_to_all(pieces, axes, 0, 0, tiled=False).sum(0)
+def scatter_sum(pieces, axes, dim=0):
+    return lax.all_to_all(pieces, axes, dim, dim, tiled=False).sum(dim)
 
 
 def all_sum(values, axis):
     count = lax.axis_size(axis)
-    mine = scatter_sum(values.reshape(count, -1), axis)
+    width = values.shape[-1]
+    mine = scatter_sum(values.reshape(count, -1, width), axis)
     gathered = lax.all_to_all(jnp.broadcast_to(mine, (count,) + mine.shape), axis, 0, 0, tiled=False)
     return gathered.reshape(values.shape)
 
@@ -150,8 +151,7 @@
     update_delta = (hidden_delta * silu_slope(update_pre)).astype(jnp.bfloat16)
     aggregated_delta = times_transposed(update_delta, w_second).astype(jnp.bfloat16)
     message_grad = transposed_times(summed_scaled, aggregated_delta)
-    message_pieces = message_grad.reshape(-1, across_count, chunk).transpose(1, 0, 2)
-    message_part = scatter_sum(message_pieces, "across")
+    message_part = scatter_sum(message_grad.reshape(-1, across_count, chunk), "across", 1)
     grad_pieces = jnp.concatenate([message_part, coarse_grad], axis=0)
     weight_grads = scatter_sum(grad_pieces, "along")
     return (hidden_two.astype(jnp.bfloat16), weight_grads)

time: 123 us -> 118 us (0.959)
  matrix products: 16 us -> 13.5 us
  local copies, waits for them, and re-layouts: 12.2 us -> 10.3 us
    another operation x4 -> x1, local copies, waits for them, and re-layouts: 1.83 us -> 0.58 us  [local(): pooled, coarse_cot = all_sum(jnp.stack([pooled_part, cot_part]), 'across')]
where the time goes in v3:
time: 118 us
  starting transfers between devices  53 us (45%)
  waiting for transfers between devices  31.8 us (27%)
  matrix products  13.5 us (11%)
  local copies, waits for them, and re-layouts  10.3 us (9%)
  other arithmetic  7.81 us (7%)
    all_to_all x3, starting transfers between devices, scatter_sum(): return lax.all_to_all(pieces, axes, dim, dim, tiled=False).sum(dim)  29 us
    all_to_all x3, waiting for transfers between devices, scatter_sum(): return lax.all_to_all(pieces, axes, dim, dim, tiled=False).sum(dim)  25.4 us
    ppermute x2, starting transfers between devices, neighbour_tiles(): tiles.append(lax.ppermute(tile, axis, backward))  11.8 us
    ppermute x2, starting transfers between devices, neighbour_tiles(): tiles.append(lax.ppermute(tile, axis, forward))  8.71 us
    all_to_all x1, waiting for transfers between devices, all_sum(): lax.all_to_all(jnp.broadcast_to(mine, (count,) + mine.shape), axis, 0, 0,...  6.44 us
    all_to_all x1, starting transfers between devices, all_sum(): lax.all_to_all(jnp.broadcast_to(mine, (count,) + mine.shape), axis, 0, 0,...  3.41 us
    dot_general x1, matrix products, local(): jnp.einsum('bkij,bkjh->bih', masked_tiles, sources[adj_index], preferred_...  2.59 us
    dot_general x1, matrix products, local(): jnp.einsum('bkij,bkjh->bih', masked_tiles, messages[adj_index], preferred...  2.46 us
  transfers between devices with their start and end apart: 8, of which 4 were waited for; matrix products, arithmetic and copies ran while one was open for 8% of the time, Pallas kernels for 0%

profile of v3, /device:TPU:1, one launch (start us, length us, event | category | flops | bytes accessed | tf_op | source)
XLA Modules:
  0.0 117.5 jit_solution(2738001412325636834)
XLA Ops:
  0.6 0.0 copy-start
  0.7 0.0 copy-start.6
  0.7 1.3 %convert_reduce_fusion = f32[1024]{0:T(1024)S(1)} fusion(bf16[1024,256]{1,0:T(8,128)(2,1)} %param.10), kind=kLoop, calls=%fused_computation.6 | loop fusion | flops 523264 | bytes 528384 | tf_op jit(solution)/shard_map/reduce_sum | solution.py:36
  2.0 1.4 %fusion.8 = f32[1024]{0:T(1024)S(1)} fusion(bf16[1024,256]{1,0:T(8,128)(2,1)} %param.10, f32[1024]{0:T(1024)S(1)} %broadcast_multiply_fusion.1), kind=kLoop, calls=%fused_computation.23 | loop fusion | flops 1047552 | bytes 532480 | tf_op jit(solution)/shard_map/reduce_sum | solution.py:37
  3.4 0.0 copy-start.4
  3.4 0.0 copy-start.10
  3.5 1.4 %fusion.9 = bf16[1024,256]{1,0:T(8,128)(2,1)S(1)} fusion(bf16[1024,256]{1,0:T(8,128)(2,1)} %param.10, f32[1024]{0:T(1024)S(1)} %add_rsqrt_fusion.1, f32[1024]{0:T(1024)S(1)} %broadcast_multiply_fusion.1), kind=kLoop, calls=%fused_computation.24 | loop fusion | flops 1048576 | bytes 1056768 | tf_op jit(solution)/shard_map/convert_element_type | solution.py:95
  4.9 0.0 copy-done.12
  4.9 1.5 %gather_fusion = bf16[128,256]{1,0:T(8,128)(2,1)} fusion(bf16[1024,256]{1,0:T(8,128)(2,1)S(1)} %fusion.9, s32[1024]{0:T(1024)S(1)} %pad_clamp_fusion.1), kind=kCustom, calls=%fused_computation | custom fusion | bytes 131584 | tf_op jit(solution)/shard_map/gather | solution.py:96
  6.4 4.6 %collective-permute-start = (bf16[128,256]{1,0:T(8,128)(2,1)}, bf16[128,256]{1,0:T(8,128)(2,1)}, u32[]{:S(2)}, u32[]{:S(2)}) collective-permute-start(bf16[128,256]{1,0:T(8,128)(2,1)} %gather_fusion), channel_id=1, source_target_pairs={{0,16},{16,32},{32,48},{48,64},{64,80},{80,96},{96,112},{112,128},... | collective-permute-start | bytes 196616 | tf_op jit(solution)/shard_map/ppermute | solution.py:30
  11.0 1.3 %collective-permute-start.1 = (bf16[128,256]{1,0:T(8,128)(2,1)}, bf16[128,256]{1,0:T(8,128)(2,1)S(1)}, u32[]{:S(2)}, u32[]{:S(2)}) collective-permute-start(bf16[128,256]{1,0:T(8,128)(2,1)} %gather_fusion), channel_id=1, source_target_pairs={{16,0},{32,16},{48,32},{64,48},{80,64},{96,80},{112,96},{128,112},... | collective-permute-start | bytes 196616 | tf_op jit(solution)/shard_map/ppermute | solution.py:31
  12.3 4.2 %collective-permute-start.2 = (bf16[128,256]{1,0:T(8,128)(2,1)}, bf16[128,256]{1,0:T(8,128)(2,1)S(1)}, u32[]{:S(2)}, u32[]{:S(2)}) collective-permute-start(bf16[128,256]{1,0:T(8,128)(2,1)} %gather_fusion), channel_id=1, source_target_pairs={{0,1},{1,2},{2,3},{3,4},{4,5},{5,6},{6,7},{7,8},{8,9},{9,10},{10,1... | collective-permute-start | bytes 196616 | tf_op jit(solution)/shard_map/ppermute | solution.py:30
  16.4 10.5 %collective-permute-start.3 = (bf16[128,256]{1,0:T(8,128)(2,1)}, bf16[128,256]{1,0:T(8,128)(2,1)S(1)}, u32[]{:S(2)}, u32[]{:S(2)}) collective-permute-start(bf16[128,256]{1,0:T(8,128)(2,1)} %gather_fusion), channel_id=1, source_target_pairs={{1,0},{2,1},{3,2},{4,3},{5,4},{6,5},{7,6},{8,7},{9,8},{10,9},{11,1... | collective-permute-start | bytes 196616 | tf_op jit(solution)/shard_map/ppermute | solution.py:31
  27.0 0.1 copy.16
  27.1 0.1 reshape.139
  27.2 0.1 iota_compare_fusion.3
  27.3 0.3 fusion.18
  27.6 0.4 convolution_bitcast_fusion.2
  28.1 0.0 collective-permute-done
  28.1 0.8 bitcast_dynamic-update-slice_fusion.3
  28.9 0.0 collective-permute-done.1
  28.9 0.0 collective-permute-done.2
  29.0 0.0 collective-permute-done.3
  29.0 0.4 convolution_convert_fusion
  29.4 2.0 %gather_fusion.1 = bf16[32,128,256]{2,1,0:T(8,128)(2,1)} fusion(bf16[12,128,256]{2,1,0:T(8,128)(2,1)S(1)} %bitcast.72, s32[1024]{0:T(1024)S(1)} %pad_clamp_fusion), kind=kCustom, calls=%fused_computation.1 | custom fusion | bytes 4194432 | tf_op jit(solution)/shard_map/gather | solution.py:108
  31.4 2.5 %fusion.3 = bf16[8,128,256]{2,1,0:T(8,128)(2,1)S(1)} fusion(bf16[8,4,128,256]{3,2,1,0:T(8,128)(2,1)} %bitcast.75, bf16[8,4,128,128]{3,2,1,0:T(8,128)(2,1)} %param.11, pred[8,4]{1,0:T(8,128)(4,1)S(1)} %iota_compare_fusion.3), kind=kOutput, calls=%fused_computation.16 | convolution fusion | flops 269221888 | bytes 3670048 | tf_op jit(solution)/shard_map/bkij,bkjh->bih/dot_general | solution.py:107
  33.8 0.3 convolution_add_fusion.1
  34.1 0.7 copy-done.1
  34.9 1.0 convolution_bitcast_fusion.3
  35.9 0.7 pad_maximum_fusion
  36.5 4.1 %all-to-all-start = ((f32[16,8,256]{2,1,0:T(8,128)}), f32[16,8,256]{2,1,0:T(8,128)}, u32[]{:S(2)}, u32[]{:S(2)}) async-start(f32[16,8,256]{2,1,0:T(8,128)} %bitcast.13), calls=%async_computation | async-start | bytes 262144 | tf_op jit(solution)/shard_map/all_to_all | solution.py:13
  40.6 0.7 gather_fusion.2
  41.3 8.0 %all-to-all-done = f32[16,8,256]{2,1,0:T(8,128)} async-done(((f32[16,8,256]{2,1,0:T(8,128)}), f32[16,8,256]{2,1,0:T(8,128)}, u32[]{:S(2)}, u32[]{:S(2)}) %all-to-all-start) | async-done | bytes 131104 | tf_op jit(solution)/shard_map/all_to_all | solution.py:13
  49.3 0.9 reduce_sum.83
  50.2 0.7 broadcast_in_dim.22
  50.9 3.4 %all-to-all-start.1 = ((f32[16,8,256]{2,1,0:T(8,128)}), f32[16,8,256]{2,1,0:T(8,128)S(1)}, u32[]{:S(2)}, u32[]{:S(2)}) async-start(f32[16,8,256]{2,1,0:T(8,128)} %broadcast_in_dim.22), calls=%async_computation.1 | async-start | bytes 262144 | tf_op jit(solution)/shard_map/all_to_all | solution.py:20
  54.3 0.0 copy-start.9
  54.3 0.0 copy-start.5
  54.3 2.6 %fusion.4 = bf16[8,128,256]{2,1,0:T(8,128)(2,1)} fusion(bf16[8,4,128,256]{3,2,1,0:T(8,128)(2,1)S(1)} %bitcast.74, bf16[8,4,128,128]{3,2,1,0:T(8,128)(2,1)} %param.11, pred[8,4]{1,0:T(8,128)(4,1)S(1)} %iota_compare_fusion.3), kind=kOutput, calls=%fused_computation.17 | convolution fusion | flops 269221888 | bytes 3670048 | tf_op jit(solution)/shard_map/bkij,bkjh->bih/dot_general | solution.py:111
  56.9 6.4 %all-to-all-done.1 = f32[16,8,256]{2,1,0:T(8,128)S(1)} async-done(((f32[16,8,256]{2,1,0:T(8,128)}), f32[16,8,256]{2,1,0:T(8,128)S(1)}, u32[]{:S(2)}, u32[]{:S(2)}) %all-to-all-start.1) | async-done | bytes 131104 | tf_op jit(solution)/shard_map/all_to_all | solution.py:20
  63.3 0.1 fusion.49
  63.4 0.1 div.42
  63.5 0.2 multiply_reduce_fusion.1
  63.7 0.1 rsqrt.21
  63.8 0.8 fusion.24
  64.6 0.6 reshape.128
  65.2 0.3 fusion.48
  65.5 0.0 copy-start.8
  65.6 0.0 copy-start.14
  65.6 2.1 %fusion.2 = bf16[1024,256]{1,0:T(8,128)(2,1)S(1)} fusion(f32[1024,256]{1,0:T(8,128)} %copy-done.2, bf16[1024,256]{1,0:T(8,128)(2,1)S(1)} %copy-done.5, s32[1024]{0:T(1024)S(1)} %copy-done.10, f32[64,256]{1,0:T(8,128)S(1)} %get-tuple-element.8, f32[64]{0:T(128)S(1)} %get-tuple-element.9, f32[64]{0:T(128)S(1)} %get-tuple-element.10, f32[64]{0:T(128)S(1)} %rsqrt.21, ...), kind=kOutput, calls=%fused_computation.15 | convolution fusion | flops 204374016 | bytes 2234368 | tf_op jit(solution)/shard_map/dot_general | solution.py:145
  67.7 0.6 fusion.7
  68.4 0.8 copy.17
  69.2 3.6 %all-to-all-start.2 = ((f32[32,16,128]{2,0,1:T(8,128)}), f32[32,16,128]{2,0,1:T(8,128)S(1)}, u32[]{:S(2)}, u32[]{:S(2)}) async-start(f32[32,16,128]{2,0,1:T(8,128)} %copy.17), calls=%async_computation.2 | async-start | bytes 524288 | tf_op jit(solution)/shard_map/all_to_all | solution.py:13
  72.8 0.6 unstack.18
  73.3 0.5 fusion.11
  73.8 0.6 copy.18
  74.5 0.8 constant_dynamic-slice_fusion
  75.3 0.1 fusion.41
  75.4 8.6 %all-to-all-done.2 = f32[32,16,128]{2,0,1:T(8,128)S(1)} async-done(((f32[32,16,128]{2,0,1:T(8,128)}), f32[32,16,128]{2,0,1:T(8,128)S(1)}, u32[]{:S(2)}, u32[]{:S(2)}) %all-to-all-start.2) | async-done | bytes 262176 | tf_op jit(solution)/shard_map/all_to_all | solution.py:13
  84.0 0.6 pad_maximum_fusion.1
  84.6 21.4 %all-to-all-start.3 = ((f32[64,1,128]{2,1,0:T(1,128)}), f32[64,1,128]{2,1,0:T(1,128)S(1)}, u32[]{:S(2)}, u32[]{:S(2)}) async-start(f32[64,1,128]{2,1,0:T(1,128)} %bitcast.23), calls=%async_computation.3 | async-start | bytes 65536 | tf_op jit(solution)/shard_map/all_to_all | solution.py:13
  106.1 2.1 %fusion.1 = bf16[1024,256]{1,0:T(8,128)(2,1)} fusion(s32[1024]{0:T(1024)S(1)} %copy-done.10, f32[64,256]{1,0:T(8,128)} %get-tuple-element.7, f32[1024,256]{1,0:T(8,128)S(1)} %copy-done.3, bf16[1024,256]{1,0:T(8,128)(2,1)S(1)} %copy-done.1), kind=kOutput, calls=%fused_computation.14 | convolution fusion | flops 35930112 | bytes 2166784 | tf_op jit(solution)/shard_map/dot_general | solution.py:128
  108.2 8.7 %all-to-all-done.3 = f32[64,1,128]{2,1,0:T(1,128)S(1)} async-done(((f32[64,1,128]{2,1,0:T(1,128)}), f32[64,1,128]{2,1,0:T(1,128)S(1)}, u32[]{:S(2)}, u32[]{:S(2)}) %all-to-all-start.3) | async-done | bytes 32800 | tf_op jit(solution)/shard_map/all_to_all | solution.py:13
  116.9 0.6 reduce_sum.89
  (35 shorter events, 0.2 us)
Async XLA Ops:
  0.6 28.4 %copy-start = (bf16[256,256]{1,0:T(8,128)(2,1)S(1)}, bf16[256,256]{1,0:T(8,128)(2,1)}, u32[]{:S(2)}) copy-start(bf16[256,256]{1,0:T(8,128)(2,1)} %param.16) | copy-start | bytes 393220
  0.6 4.3 %copy-start.12 = (s32[128]{0:T(128)S(1)}, s32[128]{0:T(128)}, u32[]{:S(2)}) copy-start(s32[128]{0:T(128)} %param.14) | copy-start | bytes 1540
  0.7 26.4 %copy-start.11 = (s32[8,4]{0,1:T(4,128)S(1)}, s32[8,4]{0,1:T(4,128)}, u32[]{:S(2)}) copy-start(s32[8,4]{0,1:T(4,128)} %param.12) | copy-start | bytes 388
  0.7 26.5 %copy-start.13 = (s32[8]{0:T(128)S(1)}, s32[8]{0:T(128)}, u32[]{:S(2)}) copy-start(s32[8]{0:T(128)} %param.13) | copy-start | bytes 100
  0.7 26.6 %copy-start.6 = (bf16[512,256]{1,0:T(8,128)(2,1)S(1)}, bf16[512,256]{1,0:T(8,128)(2,1)}, u32[]{:S(2)}) copy-start(bf16[512,256]{1,0:T(8,128)(2,1)} %param.17) | copy-start | bytes 786436
  3.4 24.1 %copy-start.4 = (bf16[1024,256]{1,0:T(8,128)(2,1)S(1)}, bf16[1024,256]{1,0:T(8,128)(2,1)}, u32[]{:S(2)}) copy-start(bf16[1024,256]{1,0:T(8,128)(2,1)} %param.19) | copy-start | bytes 1572868
  3.4 24.1 %copy-start.10 = (s32[1024]{0:T(1024)S(1)}, s32[1024]{0:T(1024)}, u32[]{:S(2)}) copy-start(s32[1024]{0:T(1024)} %param.15) | copy-start | bytes 12292
  6.4 21.7 %collective-permute-start = (bf16[128,256]{1,0:T(8,128)(2,1)}, bf16[128,256]{1,0:T(8,128)(2,1)}, u32[]{:S(2)}, u32[]{:S(2)}) collective-permute-start(bf16[128,256]{1,0:T(8,128)(2,1)} %gather_fusion), channel_id=1, source_target_pairs={{0,16},{16,32},{32,48},{48,64},{64,80},{80,96},{96,112},{112,128},... | collective-permute-start | bytes 196616 | tf_op jit(solution)/shard_map/ppermute | solution.py:30
  11.0 18.0 %collective-permute-start.1 = (bf16[128,256]{1,0:T(8,128)(2,1)}, bf16[128,256]{1,0:T(8,128)(2,1)S(1)}, u32[]{:S(2)}, u32[]{:S(2)}) collective-permute-start(bf16[128,256]{1,0:T(8,128)(2,1)} %gather_fusion), channel_id=1, source_target_pairs={{16,0},{32,16},{48,32},{64,48},{80,64},{96,80},{112,96},{128,112},... | collective-permute-start | bytes 196616 | tf_op jit(solution)/shard_map/ppermute | solution.py:31
  12.3 16.7 %collective-permute-start.2 = (bf16[128,256]{1,0:T(8,128)(2,1)}, bf16[128,256]{1,0:T(8,128)(2,1)S(1)}, u32[]{:S(2)}, u32[]{:S(2)}) collective-permute-start(bf16[128,256]{1,0:T(8,128)(2,1)} %gather_fusion), channel_id=1, source_target_pairs={{0,1},{1,2},{2,3},{3,4},{4,5},{5,6},{6,7},{7,8},{8,9},{9,10},{10,1... | collective-permute-start | bytes 196616 | tf_op jit(solution)/shard_map/ppermute | solution.py:30
  16.4 12.5 %collective-permute-start.3 = (bf16[128,256]{1,0:T(8,128)(2,1)}, bf16[128,256]{1,0:T(8,128)(2,1)S(1)}, u32[]{:S(2)}, u32[]{:S(2)}) collective-permute-start(bf16[128,256]{1,0:T(8,128)(2,1)} %gather_fusion), channel_id=1, source_target_pairs={{1,0},{2,1},{3,2},{4,3},{5,4},{6,5},{7,6},{8,7},{9,8},{10,9},{11,1... | collective-permute-start | bytes 196616 | tf_op jit(solution)/shard_map/ppermute | solution.py:31
  31.4 2.5 %copy-start.7 = (bf16[512,256]{1,0:T(8,128)(2,1)S(1)}, bf16[512,256]{1,0:T(8,128)(2,1)}, u32[]{:S(2)}) copy-start(bf16[512,256]{1,0:T(8,128)(2,1)} %param.17) | copy-start | bytes 786436
  33.8 1.0 copy-start.1
  34.9 1.0 copy-start.2
  36.5 12.8 %all-to-all-start = ((f32[16,8,256]{2,1,0:T(8,128)}), f32[16,8,256]{2,1,0:T(8,128)}, u32[]{:S(2)}, u32[]{:S(2)}) async-start(f32[16,8,256]{2,1,0:T(8,128)} %bitcast.13), calls=%async_computation | async-start | bytes 262144 | tf_op jit(solution)/shard_map/all_to_all | solution.py:13
  50.9 12.5 %all-to-all-start.1 = ((f32[16,8,256]{2,1,0:T(8,128)}), f32[16,8,256]{2,1,0:T(8,128)S(1)}, u32[]{:S(2)}, u32[]{:S(2)}) async-start(f32[16,8,256]{2,1,0:T(8,128)} %broadcast_in_dim.22), calls=%async_computation.1 | async-start | bytes 262144 | tf_op jit(solution)/shard_map/all_to_all | solution.py:20
  54.3 9.5 %copy-start.9 = (bf16[256,256]{1,0:T(8,128)(2,1)S(1)}, bf16[256,256]{1,0:T(8,128)(2,1)}, u32[]{:S(2)}) copy-start(bf16[256,256]{1,0:T(8,128)(2,1)} %param.18) | copy-start | bytes 393220
  54.3 11.2 %copy-start.5 = (bf16[1024,256]{1,0:T(8,128)(2,1)S(1)}, bf16[1024,256]{1,0:T(8,128)(2,1)}, u32[]{:S(2)}) copy-start(bf16[1024,256]{1,0:T(8,128)(2,1)} %param.19) | copy-start | bytes 1572868
  65.5 2.2 %copy-start.8 = (bf16[512,256]{1,0:T(8,128)(2,1)S(1)}, bf16[512,256]{1,0:T(8,128)(2,1)}, u32[]{:S(2)}) copy-start(bf16[512,256]{1,0:T(8,128)(2,1)} %param.17) | copy-start | bytes 786436
  65.6 2.2 %copy-start.14 = (bf16[8,128,256]{2,1,0:T(8,128)(2,1)S(1)}, bf16[8,128,256]{2,1,0:T(8,128)(2,1)}, u32[]{:S(2)}) copy-start(bf16[8,128,256]{2,1,0:T(8,128)(2,1)} %fusion.4) | copy-start | bytes 1572868
  69.2 36.9 %copy-start.3 = (f32[1024,256]{1,0:T(8,128)S(1)}, f32[1024,256]{1,0:T(8,128)}, u32[]{:S(2)}) copy-start(f32[1024,256]{1,0:T(8,128)} %copy-done.2) | copy-start | bytes 3145732
  69.2 14.8 %all-to-all-start.2 = ((f32[32,16,128]{2,0,1:T(8,128)}), f32[32,16,128]{2,0,1:T(8,128)S(1)}, u32[]{:S(2)}, u32[]{:S(2)}) async-start(f32[32,16,128]{2,0,1:T(8,128)} %copy.17), calls=%async_computation.2 | async-start | bytes 524288 | tf_op jit(solution)/shard_map/all_to_all | solution.py:13
  84.6 32.3 %all-to-all-start.3 = ((f32[64,1,128]{2,1,0:T(1,128)}), f32[64,1,128]{2,1,0:T(1,128)S(1)}, u32[]{:S(2)}, u32[]{:S(2)}) async-start(f32[64,1,128]{2,1,0:T(1,128)} %bitcast.23), calls=%async_computation.3 | async-start | bytes 65536 | tf_op jit(solution)/shard_map/all_to_all | solution.py:13

commit v4 on v3

--- a/solution.py
+++ b/solution.py
@@ -1,6 +1,8 @@
 import jax
 import jax.numpy as jnp
 from jax import lax
+from jax.experimental import pallas as pl
+from jax.experimental.pallas import tpu as pltpu
 from jax.sharding import PartitionSpec as P
 
 NC_DEV = 4
@@ -31,6 +33,43 @@
         tiles.append(lax.ppermute(tile, axis, backward))
     return jnp.stack(tiles)
 
+
+def aggregate_kernel(index_ref, count_ref, tiles_ref, messages_ref, sources_ref, agg_ref, summed_ref):
+    block = pl.program_id(0)
+    slots = tiles_ref.shape[1]
+    last = messages_ref.shape[0] - 1
+    agg = jnp.zeros(agg_ref.shape[1:], jnp.float32)
+    summed = jnp.zeros(summed_ref.shape[1:], jnp.float32)
+    for slot in range(slots):
+        source = jnp.clip(index_ref[block, slot], 0, last)
+        tile = tiles_ref[0, slot]
+        tile = jnp.where(slot < count_ref[block], tile, jnp.zeros_like(tile))
+        agg = agg + jnp.dot(tile, messages_ref[source], preferred_element_type=jnp.float32)
+        summed = summed + jnp.dot(tile, sources_ref[source], preferred_element_type=jnp.float32)
+    agg_ref[0] = agg.astype(agg_ref.dtype)
+    summed_ref[0] = summed.astype(summed_ref.dtype)
+
+def aggregate(adj_tiles, adj_index, adj_count, messages, sources):
+    blocks, slots, rows, _ = adj_tiles.shape
+    count, _, width = messages.shape
+    out = jax.ShapeDtypeStruct((blocks, rows, width), jnp.bfloat16)
+    return pl.pallas_call(
+        aggregate_kernel,
+        grid_spec=pltpu.PrefetchScalarGridSpec(
+            num_scalar_prefetch=2,
+            grid=(blocks,),
+            in_specs=[
+                pl.BlockSpec((1, slots, rows, rows), lambda b, i, c: (b, 0, 0, 0)),
+                pl.BlockSpec((count, rows, width), lambda b, i, c: (0, 0, 0)),
+                pl.BlockSpec((count, rows, width), lambda b, i, c: (0, 0, 0)),
+            ],
+            out_specs=[
+                pl.BlockSpec((1, rows, width), lambda b, i, c: (b, 0, 0)),
+                pl.BlockSpec((1, rows, width), lambda b, i, c: (b, 0, 0)),
+            ],
+        ),
+        out_shape=(out, out),
+    )(adj_index, adj_count, adj_tiles, messages, sources)
 
 def normalize(values):
     center = values - jnp.mean(values, axis=-1, keepdims=True)
@@ -102,16 +141,9 @@
         sources.reshape(-1, feature_count), w_msg, preferred_element_type=jnp.float32
     )
     messages = messages.astype(jnp.bfloat16).reshape(sources.shape)
-    live_slots = jnp.arange(slot_count)[None, :] < adj_count[:, None]
-    masked_tiles = jnp.where(live_slots[:, :, None, None], adj_tiles, jnp.zeros((), jnp.bfloat16))
-    aggregated = jnp.einsum(
-        "bkij,bkjh->bih", masked_tiles, messages[adj_index], preferred_element_type=jnp.float32
-    )
-    aggregated = aggregated.astype(jnp.bfloat16).reshape(-1, feature_count)
-    summed_scaled = jnp.einsum(
-        "bkij,bkjh->bih", masked_tiles, sources[adj_index], preferred_element_type=jnp.float32
-    )
-    summed_scaled = summed_scaled.astype(jnp.bfloat16).reshape(-1, feature_count)
+    aggregated, summed_scaled = aggregate(adj_tiles, adj_index, adj_count, messages, sources)
+    aggregated = aggregated.reshape(-1, feature_count)
+    summed_scaled = summed_scaled.reshape(-1, feature_count)
     w_first = w_update[:feature_count]
     w_second = w_update[feature_count:]
     update_pre = jnp.dot(scaled, w_first, preferred_element_type=jnp.float32) + jnp.dot(

time: 118 us -> 123 us (1.042)
  blocking collectives: 0 us -> 10.9 us
  Pallas kernels: 0 us -> 7.51 us
  waiting for transfers between devices: 31.8 us -> 27.3 us
  starting transfers between devices: 53 us -> 49.9 us
  matrix products: 13.5 us -> 10.7 us
  other arithmetic: 7.81 us -> 5.11 us
    all_to_all x0 -> x1, blocking collectives: none -> 10.9 us  [scatter_sum(): return lax.all_to_all(pieces, axes, dim, dim, tiled=False).sum(dim)]
    pallas_call x0 -> x1, Pallas kernels: none -> 7.51 us  [aggregate(): pl.pallas_call(aggregate_kernel, grid_spec=pltpu.PrefetchScalarGridSpec(n...]
    all_to_all x3 -> x2, waiting for transfers between devices: 25.4 us -> 18.6 us  [scatter_sum(): return lax.all_to_all(pieces, axes, dim, dim, tiled=False).sum(dim)]
    dot_general x2 -> x0, matrix products: 5.05 us -> none  [the longest x1 2.59 us: local(): jnp.einsum('bkij,bkjh->bih', masked_tiles, sources[adj_index], preferred_...]
    all_to_all x3 -> x2, starting transfers between devices: 29 us -> 25.4 us  [scatter_sum(): return lax.all_to_all(pieces, axes, dim, dim, tiled=False).sum(dim)]
    gather x2 -> x0, local copies, waits for them, and re-layouts: 2.69 us -> none  [the longest x1 2.01 us: local(): messages[adj_index]]
    all_to_all x1, waiting for transfers between devices: 6.44 us -> 8.7 us  [all_sum(): lax.all_to_all(jnp.broadcast_to(mine, (count,) + mine.shape), axis, 0, 0,...]
    dot_general x4, matrix products: 2.17 us -> 3.82 us  [transposed_times(): lax.dot_general(operand, second, (((0,), (0,)), ((), ())), precision=prec...]
  transfers between devices with their start and end apart: 8 -> 7, of which waited for: 4 -> 3; matrix products, arithmetic and copies ran while one was open for 8% -> 7% of each run, Pallas kernels for 0% -> 0%
where the time goes in v4:
time: 123 us; the launch traced here: 122 us
  starting transfers between devices  49.9 us (41%)
  waiting for transfers between devices  27.3 us (22%)
  blocking collectives  10.9 us (9%)
  matrix products  10.7 us (9%)
  local copies, waits for them, and re-layouts  9.89 us (8%)
  Pallas kernels  7.51 us (6%)
  other arithmetic  5.11 us (4%)
    all_to_all x2, starting transfers between devices, scatter_sum(): return lax.all_to_all(pieces, axes, dim, dim, tiled=False).sum(dim)  25.4 us
    all_to_all x2, waiting for transfers between devices, scatter_sum(): return lax.all_to_all(pieces, axes, dim, dim, tiled=False).sum(dim)  18.6 us
    ppermute x2, starting transfers between devices, neighbour_tiles(): tiles.append(lax.ppermute(tile, axis, backward))  12.4 us
    all_to_all x1, blocking collectives, scatter_sum(): return lax.all_to_all(pieces, axes, dim, dim, tiled=False).sum(dim)  10.9 us
    ppermute x2, starting transfers between devices, neighbour_tiles(): tiles.append(lax.ppermute(tile, axis, forward))  8.71 us
    all_to_all x1, waiting for transfers between devices, all_sum(): lax.all_to_all(jnp.broadcast_to(mine, (count,) + mine.shape), axis, 0, 0,...  8.7 us
    pallas_call x1, Pallas kernels, aggregate(): pl.pallas_call(aggregate_kernel, grid_spec=pltpu.PrefetchScalarGridSpec(n...  7.51 us
    dot_general x4, matrix products, transposed_times(): lax.dot_general(operand, second, (((0,), (0,)), ((), ())), precision=prec...  3.82 us
  transfers between devices with their start and end apart: 7, of which 3 were waited for; matrix products, arithmetic and copies ran while one was open for 7% of the time, Pallas kernels for 0%

profile of v4, /device:TPU:1, one launch (start us, length us, event | category | flops | bytes accessed | tf_op | source)
XLA Modules:
  0.0 122.4 jit_solution(5365364556913103383)
XLA Ops:
  0.6 0.0 copy-start
  0.6 0.0 copy-start.2
  0.7 0.0 copy-start.13
  0.7 1.3 %convert_reduce_fusion = f32[1024]{0:T(1024)S(1)} fusion(bf16[1024,256]{1,0:T(8,128)(2,1)} %param.10), kind=kLoop, calls=%fused_computation.4 | loop fusion | flops 523264 | bytes 528384 | tf_op jit(solution)/shard_map/reduce_sum | solution.py:75
  2.0 0.0 copy-start.11
  2.0 0.0 copy-start.7
  2.0 1.4 %fusion.6 = f32[1024]{0:T(1024)S(1)} fusion(bf16[1024,256]{1,0:T(8,128)(2,1)} %param.10, f32[1024]{0:T(1024)S(1)} %broadcast_multiply_fusion.1), kind=kLoop, calls=%fused_computation.17 | loop fusion | flops 1047552 | bytes 532480 | tf_op jit(solution)/shard_map/reduce_sum | solution.py:76
  3.5 0.0 copy-done.2
  3.5 0.3 fusion.7
  3.8 0.0 copy-done.13
  3.9 0.0 copy-start.5
  3.9 0.0 copy-start.10
  3.9 1.5 %gather_fusion = bf16[128,256]{1,0:T(8,128)(2,1)} fusion(bf16[1024,256]{1,0:T(8,128)(2,1)S(1)} %fusion.7, s32[1024]{0:T(1024)S(1)} %pad_clamp_fusion), kind=kCustom, calls=%fused_computation | custom fusion | bytes 131584 | tf_op jit(solution)/shard_map/gather | solution.py:135
  5.4 4.6 %collective-permute-start = (bf16[128,256]{1,0:T(8,128)(2,1)}, bf16[128,256]{1,0:T(8,128)(2,1)}, u32[]{:S(2)}, u32[]{:S(2)}) collective-permute-start(bf16[128,256]{1,0:T(8,128)(2,1)} %gather_fusion), channel_id=1, source_target_pairs={{0,16},{16,32},{32,48},{48,64},{64,80},{80,96},{96,112},{112,128},... | collective-permute-start | bytes 196616 | tf_op jit(solution)/shard_map/ppermute | solution.py:32
  9.9 1.3 %collective-permute-start.1 = (bf16[128,256]{1,0:T(8,128)(2,1)}, bf16[128,256]{1,0:T(8,128)(2,1)}, u32[]{:S(2)}, u32[]{:S(2)}) collective-permute-start(bf16[128,256]{1,0:T(8,128)(2,1)} %gather_fusion), channel_id=1, source_target_pairs={{16,0},{32,16},{48,32},{64,48},{80,64},{96,80},{112,96},{128,112},... | collective-permute-start | bytes 196616 | tf_op jit(solution)/shard_map/ppermute | solution.py:33
  11.2 4.2 %collective-permute-start.2 = (bf16[128,256]{1,0:T(8,128)(2,1)}, bf16[128,256]{1,0:T(8,128)(2,1)}, u32[]{:S(2)}, u32[]{:S(2)}) collective-permute-start(bf16[128,256]{1,0:T(8,128)(2,1)} %gather_fusion), channel_id=1, source_target_pairs={{0,1},{1,2},{2,3},{3,4},{4,5},{5,6},{6,7},{7,8},{8,9},{9,10},{10,1... | collective-permute-start | bytes 196616 | tf_op jit(solution)/shard_map/ppermute | solution.py:32
  15.4 11.1 %collective-permute-start.3 = (bf16[128,256]{1,0:T(8,128)(2,1)}, bf16[128,256]{1,0:T(8,128)(2,1)}, u32[]{:S(2)}, u32[]{:S(2)}) collective-permute-start(bf16[128,256]{1,0:T(8,128)(2,1)} %gather_fusion), channel_id=1, source_target_pairs={{1,0},{2,1},{3,2},{4,3},{5,4},{6,5},{7,6},{8,7},{9,8},{10,9},{11,1... | collective-permute-start | bytes 196616 | tf_op jit(solution)/shard_map/ppermute | solution.py:33
  26.5 0.7 copy.16.index_ref
  27.2 0.3 fusion.14
  27.5 1.1 convolution_bitcast_fusion
  28.6 0.0 collective-permute-done
  28.6 0.8 bitcast_dynamic-update-slice_fusion.3
  29.5 0.0 collective-permute-done.1
  29.5 0.8 bitcast_dynamic-update-slice_fusion.2
  30.3 0.0 collective-permute-done.2
  30.3 0.8 bitcast_dynamic-update-slice_fusion.1
  31.2 0.0 collective-permute-done.3
  31.2 0.8 bitcast_dynamic-update-slice_fusion.sources_ref
  32.0 1.3 %convolution_convert_fusion = bf16[1536,256]{1,0:T(8,128)(2,1)} fusion(bf16[1536,256]{1,0:T(8,128)(2,1)S(1)} %bitcast.58, bf16[256,256]{1,0:T(8,128)(2,1)S(1)} %copy-done), kind=kOutput, calls=%fused_computation.1 | convolution fusion | flops 201719808 | bytes 1703936 | tf_op jit(solution)/shard_map/dot_general | solution.py:140
  33.3 0.0 copy-done.1
  33.3 7.5 %shard_map.113 = (bf16[8,128,256]{2,1,0:T(8,128)(2,1)}, bf16[8,128,256]{2,1,0:T(8,128)(2,1)}) custom-call(s32[8,4]{1,0:T(8,128)} %copy.16.index_ref, s32[8]{0:T(128)} %count_ref.1, bf16[8,4,128,128]{3,2,1,0:T(8,128)(2,1)} %tiles_ref.1, bf16[12,128,256]{2,1,0:T(8,128)(2,1)} %bitcast.59, bf16[12,128,256]{2,1,0:T(8,128)(2,1)} %copy-done.1), custom_call_target="tpu_custom_call" | custom-call | tf_op jit(solution)/shard_map/pallas_call | solution.py:56
  40.8 1.4 %convolution_add_fusion.1 = f32[1024,256]{1,0:T(8,128)S(1)} fusion(f32[1024,256]{1,0:T(8,128)S(1)} %fusion.14, bf16[1024,256]{1,0:T(8,128)(2,1)} %bitcast.61, bf16[512,256]{1,0:T(8,128)(2,1)} %param.17), kind=kOutput, calls=%fused_computation.6 | convolution fusion | flops 134479872 | bytes 2752512 | tf_op jit(solution)/shard_map/dot_general | solution.py:149
  42.2 0.0 copy-start.3
  42.2 0.0 copy-start.6
  42.2 1.0 convolution_bitcast_fusion.1
  43.2 0.0 copy-start.9
  43.2 10.9 %all_to_all.24 = f32[16,8,256]{2,1,0:T(8,128)S(1)} all-to-all(f32[16,8,256]{2,1,0:T(8,128)S(1)} %bitcast.60), channel_id=1, replica_groups=mesh['along'=64,'across'=16] {'across'}, dimensions={0} | all-to-all | bytes 262144 | tf_op jit(solution)/shard_map/all_to_all | solution.py:15
  54.1 0.7 broadcast_in_dim.5
  54.8 3.4 %all-to-all-start.1 = ((f32[16,8,256]{2,1,0:T(8,128)}), f32[16,8,256]{2,1,0:T(8,128)S(1)}, u32[]{:S(2)}, u32[]{:S(2)}) async-start(f32[16,8,256]{2,1,0:T(8,128)} %broadcast_in_dim.5), calls=%async_computation.1 | async-start | bytes 262144 | tf_op jit(solution)/shard_map/all_to_all | solution.py:22
  58.2 8.7 %all-to-all-done.1 = f32[16,8,256]{2,1,0:T(8,128)S(1)} async-done(((f32[16,8,256]{2,1,0:T(8,128)}), f32[16,8,256]{2,1,0:T(8,128)S(1)}, u32[]{:S(2)}, u32[]{:S(2)}) %all-to-all-start.1) | async-done | bytes 131104 | tf_op jit(solution)/shard_map/all_to_all | solution.py:22
  66.9 0.1 fusion.43
  67.0 0.1 div.42
  67.1 0.2 multiply_reduce_fusion.1
  67.2 0.1 rsqrt.21
  67.3 0.8 fusion.20
  68.2 0.6 reshape.107
  68.8 0.3 fusion.42
  69.1 0.0 copy-start.8
  69.1 1.6 %fusion.2 = bf16[1024,256]{1,0:T(8,128)(2,1)} fusion(f32[1024,256]{1,0:T(8,128)S(1)} %convolution_add_fusion.1, bf16[1024,256]{1,0:T(8,128)(2,1)S(1)} %copy-done.5, s32[1024]{0:T(1024)S(1)} %copy-done.10, f32[64,256]{1,0:T(8,128)S(1)} %get-tuple-element.12, f32[64]{0:T(128)S(1)} %get-tuple-element.13, f32[64]{0:T(128)S(1)} %get-tuple-element.14, ...), kind=kOutput, calls=%fused_computation.11 | convolution fusion | flops 204374016 | bytes 2234368 | tf_op jit(solution)/shard_map/dot_general | solution.py:177
  70.8 1.7 %fusion.5 = f32[256,256]{1,0:T(8,128)S(1)} fusion(bf16[1024,256]{1,0:T(8,128)(2,1)S(1)} %bitcast.62, bf16[1024,256]{1,0:T(8,128)(2,1)} %fusion.2, bf16[512,256]{1,0:T(8,128)(2,1)S(1)} %copy-done.8), kind=kOutput, calls=%fused_computation.14 | convolution fusion | flops 268697600 | bytes 1441792 | tf_op jit(solution)/shard_map/dot_general | solution.py:86
  72.5 0.8 copy.17
  73.2 3.4 %all-to-all-start.2 = ((f32[32,16,128]{2,0,1:T(8,128)}), f32[32,16,128]{2,0,1:T(8,128)S(1)}, u32[]{:S(2)}, u32[]{:S(2)}) async-start(f32[32,16,128]{2,0,1:T(8,128)} %copy.17), calls=%async_computation.2 | async-start | bytes 524288 | tf_op jit(solution)/shard_map/all_to_all | solution.py:15
  76.7 0.6 unstack.18
  77.3 0.5 fusion.9
  77.8 0.0 copy-start.14
  77.8 0.6 copy.18
  78.4 0.8 constant_dynamic-slice_fusion
  79.2 0.1 fusion.37
  79.3 9.1 %all-to-all-done.2 = f32[32,16,128]{2,0,1:T(8,128)S(1)} async-done(((f32[32,16,128]{2,0,1:T(8,128)}), f32[32,16,128]{2,0,1:T(8,128)S(1)}, u32[]{:S(2)}, u32[]{:S(2)}) %all-to-all-start.2) | async-done | bytes 262176 | tf_op jit(solution)/shard_map/all_to_all | solution.py:15
  88.4 0.6 pad_maximum_fusion.1
  89.0 21.9 %all-to-all-start.3 = ((f32[64,1,128]{2,1,0:T(1,128)}), f32[64,1,128]{2,1,0:T(1,128)S(1)}, u32[]{:S(2)}, u32[]{:S(2)}) async-start(f32[64,1,128]{2,1,0:T(1,128)} %bitcast.17), calls=%async_computation.3 | async-start | bytes 65536 | tf_op jit(solution)/shard_map/all_to_all | solution.py:15
  111.0 1.3 %fusion.1 = bf16[1024,256]{1,0:T(8,128)(2,1)} fusion(s32[1024]{0:T(1024)S(1)} %copy-done.10, f32[64,256]{1,0:T(8,128)S(1)} %copy-done.14, f32[1024,256]{1,0:T(8,128)S(1)} %copy-done.4, bf16[1024,256]{1,0:T(8,128)(2,1)S(1)} %copy-done.2), kind=kOutput, calls=%fused_computation.10 | convolution fusion | flops 35930112 | bytes 2166784 | tf_op jit(solution)/shard_map/dot_general | solution.py:160
  112.3 9.5 %all-to-all-done.3 = f32[64,1,128]{2,1,0:T(1,128)S(1)} async-done(((f32[64,1,128]{2,1,0:T(1,128)}), f32[64,1,128]{2,1,0:T(1,128)S(1)}, u32[]{:S(2)}, u32[]{:S(2)}) %all-to-all-start.3) | async-done | bytes 32800 | tf_op jit(solution)/shard_map/all_to_all | solution.py:15
  121.8 0.6 reduce_sum.89
  (27 shorter events, 0.2 us)
Async XLA Ops:
  0.6 31.4 %copy-start = (bf16[256,256]{1,0:T(8,128)(2,1)S(1)}, bf16[256,256]{1,0:T(8,128)(2,1)}, u32[]{:S(2)}) copy-start(bf16[256,256]{1,0:T(8,128)(2,1)} %param.16) | copy-start | bytes 393220
  0.6 2.8 %copy-start.2 = (bf16[1024,256]{1,0:T(8,128)(2,1)S(1)}, bf16[1024,256]{1,0:T(8,128)(2,1)}, u32[]{:S(2)}) copy-start(bf16[1024,256]{1,0:T(8,128)(2,1)} %param.10) | copy-start | bytes 1572868
  0.7 3.2 %copy-start.13 = (s32[128]{0:T(128)S(1)}, s32[128]{0:T(128)}, u32[]{:S(2)}) copy-start(s32[128]{0:T(128)} %param.14) | copy-start | bytes 1540
  2.0 24.5 %copy-start.11 = (s32[8,4]{0,1:T(4,128)S(1)}, s32[8,4]{0,1:T(4,128)}, u32[]{:S(2)}) copy-start(s32[8,4]{0,1:T(4,128)} %param.12) | copy-start | bytes 388
  2.0 25.2 %copy-start.7 = (bf16[512,256]{1,0:T(8,128)(2,1)S(1)}, bf16[512,256]{1,0:T(8,128)(2,1)}, u32[]{:S(2)}) copy-start(bf16[512,256]{1,0:T(8,128)(2,1)} %param.17) | copy-start | bytes 786436
  3.9 23.6 %copy-start.5 = (bf16[1024,256]{1,0:T(8,128)(2,1)S(1)}, bf16[1024,256]{1,0:T(8,128)(2,1)}, u32[]{:S(2)}) copy-start(bf16[1024,256]{1,0:T(8,128)(2,1)} %param.19) | copy-start | bytes 1572868
  3.9 23.6 %copy-start.10 = (s32[1024]{0:T(1024)S(1)}, s32[1024]{0:T(1024)}, u32[]{:S(2)}) copy-start(s32[1024]{0:T(1024)} %param.15) | copy-start | bytes 12292
  5.4 23.3 %collective-permute-start = (bf16[128,256]{1,0:T(8,128)(2,1)}, bf16[128,256]{1,0:T(8,128)(2,1)}, u32[]{:S(2)}, u32[]{:S(2)}) collective-permute-start(bf16[128,256]{1,0:T(8,128)(2,1)} %gather_fusion), channel_id=1, source_target_pairs={{0,16},{16,32},{32,48},{48,64},{64,80},{80,96},{96,112},{112,128},... | collective-permute-start | bytes 196616 | tf_op jit(solution)/shard_map/ppermute | solution.py:32
  9.9 19.6 %collective-permute-start.1 = (bf16[128,256]{1,0:T(8,128)(2,1)}, bf16[128,256]{1,0:T(8,128)(2,1)}, u32[]{:S(2)}, u32[]{:S(2)}) collective-permute-start(bf16[128,256]{1,0:T(8,128)(2,1)} %gather_fusion), channel_id=1, source_target_pairs={{16,0},{32,16},{48,32},{64,48},{80,64},{96,80},{112,96},{128,112},... | collective-permute-start | bytes 196616 | tf_op jit(solution)/shard_map/ppermute | solution.py:33
  11.2 19.1 %collective-permute-start.2 = (bf16[128,256]{1,0:T(8,128)(2,1)}, bf16[128,256]{1,0:T(8,128)(2,1)}, u32[]{:S(2)}, u32[]{:S(2)}) collective-permute-start(bf16[128,256]{1,0:T(8,128)(2,1)} %gather_fusion), channel_id=1, source_target_pairs={{0,1},{1,2},{2,3},{3,4},{4,5},{5,6},{6,7},{7,8},{8,9},{9,10},{10,1... | collective-permute-start | bytes 196616 | tf_op jit(solution)/shard_map/ppermute | solution.py:32
  15.4 15.8 %collective-permute-start.3 = (bf16[128,256]{1,0:T(8,128)(2,1)}, bf16[128,256]{1,0:T(8,128)(2,1)}, u32[]{:S(2)}, u32[]{:S(2)}) collective-permute-start(bf16[128,256]{1,0:T(8,128)(2,1)} %gather_fusion), channel_id=1, source_target_pairs={{1,0},{2,1},{3,2},{4,3},{5,4},{6,5},{7,6},{8,7},{9,8},{10,9},{11,1... | collective-permute-start | bytes 196616 | tf_op jit(solution)/shard_map/ppermute | solution.py:33
  32.0 1.3 %copy-start.1 = (bf16[12,128,256]{2,1,0:T(8,128)(2,1)}, bf16[12,128,256]{2,1,0:T(8,128)(2,1)S(1)}, u32[]{:S(2)}) copy-start(bf16[12,128,256]{2,1,0:T(8,128)(2,1)S(1)} %bitcast_dynamic-update-slice_fusion.sources_ref) | copy-start | bytes 2359300
  42.2 26.9 %copy-start.3 = (f32[1024,256]{1,0:T(8,128)}, f32[1024,256]{1,0:T(8,128)S(1)}, u32[]{:S(2)}) copy-start(f32[1024,256]{1,0:T(8,128)S(1)} %convolution_add_fusion.1) | copy-start | bytes 3145732
  42.2 1.0 copy-start.6
  43.2 24.2 %copy-start.9 = (bf16[256,256]{1,0:T(8,128)(2,1)S(1)}, bf16[256,256]{1,0:T(8,128)(2,1)}, u32[]{:S(2)}) copy-start(bf16[256,256]{1,0:T(8,128)(2,1)} %param.18) | copy-start | bytes 393220
  54.8 12.1 %all-to-all-start.1 = ((f32[16,8,256]{2,1,0:T(8,128)}), f32[16,8,256]{2,1,0:T(8,128)S(1)}, u32[]{:S(2)}, u32[]{:S(2)}) async-start(f32[16,8,256]{2,1,0:T(8,128)} %broadcast_in_dim.5), calls=%async_computation.1 | async-start | bytes 262144 | tf_op jit(solution)/shard_map/all_to_all | solution.py:22
  69.1 1.7 %copy-start.8 = (bf16[512,256]{1,0:T(8,128)(2,1)S(1)}, bf16[512,256]{1,0:T(8,128)(2,1)}, u32[]{:S(2)}) copy-start(bf16[512,256]{1,0:T(8,128)(2,1)} %param.17) | copy-start | bytes 786436
  69.1 1.7 %copy-start.12 = (bf16[8,128,256]{2,1,0:T(8,128)(2,1)S(1)}, bf16[8,128,256]{2,1,0:T(8,128)(2,1)}, u32[]{:S(2)}) copy-start(bf16[8,128,256]{2,1,0:T(8,128)(2,1)} %get-tuple-element.5) | copy-start | bytes 1572868
  73.2 15.2 %all-to-all-start.2 = ((f32[32,16,128]{2,0,1:T(8,128)}), f32[32,16,128]{2,0,1:T(8,128)S(1)}, u32[]{:S(2)}, u32[]{:S(2)}) async-start(f32[32,16,128]{2,0,1:T(8,128)} %copy.17), calls=%async_computation.2 | async-start | bytes 524288 | tf_op jit(solution)/shard_map/all_to_all | solution.py:15
  77.3 33.7 %copy-start.4 = (f32[1024,256]{1,0:T(8,128)S(1)}, f32[1024,256]{1,0:T(8,128)}, u32[]{:S(2)}) copy-start(f32[1024,256]{1,0:T(8,128)} %copy-done.3) | copy-start | bytes 3145732
  77.8 33.3 %copy-start.14 = (f32[64,256]{1,0:T(8,128)S(1)}, f32[64,256]{1,0:T(8,128)}, u32[]{:S(2)}) copy-start(f32[64,256]{1,0:T(8,128)} %get-tuple-element.11) | copy-start | bytes 196612
  89.0 32.8 %all-to-all-start.3 = ((f32[64,1,128]{2,1,0:T(1,128)}), f32[64,1,128]{2,1,0:T(1,128)S(1)}, u32[]{:S(2)}, u32[]{:S(2)}) async-start(f32[64,1,128]{2,1,0:T(1,128)} %bitcast.17), calls=%async_computation.3 | async-start | bytes 65536 | tf_op jit(solution)/shard_map/all_to_all | solution.py:15

commit v5 on v3

--- a/solution.py
+++ b/solution.py
@@ -4,6 +4,10 @@
 from jax.sharding import PartitionSpec as P
 
 NC_DEV = 4
+ALONG = ("z", "x")
+ACROSS = ("y", "core")
+CHIP_X = 8
+CHIP_CORES = 2
 
 
 eps = 1e-05
@@ -23,7 +27,7 @@
 
 def neighbour_tiles(tile):
     tiles = []
-    for axis in ("along", "across"):
+    for axis in (ALONG, ACROSS):
         count = lax.axis_size(axis)
         forward = [(i, i + 1) for i in range(count - 1)]
         backward = [(i + 1, i) for i in range(count - 1)]
@@ -118,23 +122,23 @@
         aggregated, w_second, preferred_element_type=jnp.float32
     )
     hidden_one = inputs + jax.nn.silu(update_pre)
-    coarse_count = NC_DEV * lax.axis_size("across")
+    coarse_count = NC_DEV * lax.axis_size(ACROSS)
     assign_float = (pool_index[:, None] == jnp.arange(coarse_count)[None, :]).astype(jnp.float32)
     assign_bits = assign_float.astype(jnp.bfloat16)
     pooled_part = transposed_times(assign_float, hidden_one, lax.Precision.HIGHEST)
     cot_part = transposed_times(assign_bits, cotangent)
-    pooled, coarse_cot = all_sum(jnp.stack([pooled_part, cot_part]), "across")
+    pooled, coarse_cot = all_sum(jnp.stack([pooled_part, cot_part]), ACROSS)
     coarse_norm, inverse, coarse, coarse_pre, coarse_out = coarse_forward(pooled, w_coarse)
     hidden_two = hidden_one + jnp.dot(assign_bits, coarse_out, preferred_element_type=jnp.float32)
     coarse_delta, pooled_delta = coarse_backward(
         coarse_cot, coarse_norm, inverse, coarse_pre, w_coarse
     )
-    along_count = lax.axis_size("along")
-    across_count = lax.axis_size("across")
+    along_count = lax.axis_size(ALONG)
+    across_count = lax.axis_size(ACROSS)
     chunk = (feature_count * feature_count) // (along_count * across_count // 2)
     halves = feature_count // chunk
     rows_per_step = across_count // halves
-    member = lax.axis_index("across")
+    member = lax.axis_index(ACROSS)
     picked_rows = lax.dynamic_index_in_dim(
         coarse.reshape(coarse_count, -1, rows_per_step), member // halves, 2, keepdims=False
     )
@@ -151,28 +155,35 @@
     update_delta = (hidden_delta * silu_slope(update_pre)).astype(jnp.bfloat16)
     aggregated_delta = times_transposed(update_delta, w_second).astype(jnp.bfloat16)
     message_grad = transposed_times(summed_scaled, aggregated_delta)
-    message_part = scatter_sum(message_grad.reshape(-1, across_count, chunk), "across", 1)
+    message_part = scatter_sum(message_grad.reshape(-1, across_count, chunk), ACROSS, 1)
     grad_pieces = jnp.concatenate([message_part, coarse_grad], axis=0)
-    weight_grads = scatter_sum(grad_pieces, "along")
+    along_pieces = grad_pieces.reshape(-1, lax.axis_size("x"), chunk)
+    weight_grads = scatter_sum(scatter_sum(along_pieces, "x", 1), "z")
     return (hidden_two.astype(jnp.bfloat16), weight_grads)
 
 
 def solution(mesh):
+    along, across = mesh.shape["along"], mesh.shape["across"]
+    chips = jax.sharding.Mesh(
+        mesh.devices.reshape(along // CHIP_X, CHIP_X, across // CHIP_CORES, CHIP_CORES),
+        ("z", "x", "y", "core"),
+    )
+    rows = ALONG + ACROSS
     return jax.shard_map(
         local,
-        mesh=mesh,
+        mesh=chips,
         in_specs=(
-            P(("along", "across"), None),
-            P(("along", "across"), None, None, None),
-            P(("along", "across"), None),
-            P(("along", "across")),
-            P(("along", "across")),
-            P(("along", "across")),
+            P(rows, None),
+            P(rows, None, None, None),
+            P(rows, None),
+            P(rows),
+            P(rows),
+            P(rows),
             P(),
             P(),
             P(),
-            P(("along", "across"), None),
+            P(rows, None),
         ),
-        out_specs=(P(("along", "across"), None), P(("along", "across"))),
+        out_specs=(P(rows, None), P(rows)),
         check_vma=False,
     )

time: 118 us -> 121 us (1.025)
  blocking collectives: 0 us -> 12.4 us
  starting transfers between devices: 53 us -> 47.9 us
  waiting for transfers between devices: 31.8 us -> 27.5 us
    all_to_all x0 -> x1, blocking collectives: none -> 12.4 us  [scatter_sum(): return lax.all_to_all(pieces, axes, dim, dim, tiled=False).sum(dim)]
    all_to_all x3, starting transfers between devices: 29 us -> 24 us  [scatter_sum(): return lax.all_to_all(pieces, axes, dim, dim, tiled=False).sum(dim)]
    all_to_all x3, waiting for transfers between devices: 25.4 us -> 21 us  [scatter_sum(): return lax.all_to_all(pieces, axes, dim, dim, tiled=False).sum(dim)]
where the time goes in v5:
time: 121 us; the launch traced here: 120 us
  starting transfers between devices  47.9 us (40%)
  waiting for transfers between devices  27.5 us (23%)
  matrix products  13.6 us (11%)
  blocking collectives  12.4 us (10%)
  local copies, waits for them, and re-layouts  10.3 us (9%)
  other arithmetic  7.75 us (6%)
    all_to_all x3, starting transfers between devices, scatter_sum(): return lax.all_to_all(pieces, axes, dim, dim, tiled=False).sum(dim)  24 us
    all_to_all x3, waiting for transfers between devices, scatter_sum(): return lax.all_to_all(pieces, axes, dim, dim, tiled=False).sum(dim)  21 us
    all_to_all x1, blocking collectives, scatter_sum(): return lax.all_to_all(pieces, axes, dim, dim, tiled=False).sum(dim)  12.4 us
    ppermute x2, starting transfers between devices, neighbour_tiles(): tiles.append(lax.ppermute(tile, axis, backward))  11.8 us
    ppermute x2, starting transfers between devices, neighbour_tiles(): tiles.append(lax.ppermute(tile, axis, forward))  8.71 us
    all_to_all x1, waiting for transfers between devices, all_sum(): lax.all_to_all(jnp.broadcast_to(mine, (count,) + mine.shape), axis, 0, 0,...  6.43 us
    all_to_all x1, starting transfers between devices, all_sum(): lax.all_to_all(jnp.broadcast_to(mine, (count,) + mine.shape), axis, 0, 0,...  3.41 us
    dot_general x1, matrix products, local(): jnp.einsum('bkij,bkjh->bih', masked_tiles, sources[adj_index], preferred_...  2.59 us
  transfers between devices with their start and end apart: 8, of which 4 were waited for; matrix products, arithmetic and copies ran while one was open for 8% of the time, Pallas kernels for 0%

profile of v5, /device:TPU:1, one launch (start us, length us, event | category | flops | bytes accessed | tf_op | source)
XLA Modules:
  0.0 120.5 jit_solution(1428726069420078102)
XLA Ops:
  0.6 0.0 copy-start
  0.7 0.0 copy-start.6
  0.7 1.3 %convert_reduce_fusion = f32[1024]{0:T(1024)S(1)} fusion(bf16[1024,256]{1,0:T(8,128)(2,1)} %param.10), kind=kLoop, calls=%fused_computation.6 | loop fusion | flops 523264 | bytes 528384 | tf_op jit(solution)/shard_map/reduce_sum | solution.py:40
  2.0 1.4 %fusion.8 = f32[1024]{0:T(1024)S(1)} fusion(bf16[1024,256]{1,0:T(8,128)(2,1)} %param.10, f32[1024]{0:T(1024)S(1)} %broadcast_multiply_fusion.1), kind=kLoop, calls=%fused_computation.23 | loop fusion | flops 1047552 | bytes 532480 | tf_op jit(solution)/shard_map/reduce_sum | solution.py:41
  3.4 0.0 copy-start.4
  3.4 0.0 copy-start.10
  3.5 1.4 %fusion.9 = bf16[1024,256]{1,0:T(8,128)(2,1)S(1)} fusion(bf16[1024,256]{1,0:T(8,128)(2,1)} %param.10, f32[1024]{0:T(1024)S(1)} %add_rsqrt_fusion.1, f32[1024]{0:T(1024)S(1)} %broadcast_multiply_fusion.1), kind=kLoop, calls=%fused_computation.24 | loop fusion | flops 1048576 | bytes 1056768 | tf_op jit(solution)/shard_map/convert_element_type | solution.py:99
  4.9 1.5 %gather_fusion = bf16[128,256]{1,0:T(8,128)(2,1)} fusion(bf16[1024,256]{1,0:T(8,128)(2,1)S(1)} %fusion.9, s32[1024]{0:T(1024)S(1)} %pad_clamp_fusion.1), kind=kCustom, calls=%fused_computation | custom fusion | bytes 131584 | tf_op jit(solution)/shard_map/gather | solution.py:100
  6.4 4.5 %collective-permute-start = (bf16[128,256]{1,0:T(8,128)(2,1)}, bf16[128,256]{1,0:T(8,128)(2,1)}, u32[]{:S(2)}, u32[]{:S(2)}) collective-permute-start(bf16[128,256]{1,0:T(8,128)(2,1)} %gather_fusion), channel_id=1, source_target_pairs={{0,16},{16,32},{32,48},{48,64},{64,80},{80,96},{96,112},{112,128},... | collective-permute-start | bytes 196616 | tf_op jit(solution)/shard_map/ppermute | solution.py:34
  11.0 1.3 %collective-permute-start.1 = (bf16[128,256]{1,0:T(8,128)(2,1)}, bf16[128,256]{1,0:T(8,128)(2,1)S(1)}, u32[]{:S(2)}, u32[]{:S(2)}) collective-permute-start(bf16[128,256]{1,0:T(8,128)(2,1)} %gather_fusion), channel_id=1, source_target_pairs={{16,0},{32,16},{48,32},{64,48},{80,64},{96,80},{112,96},{128,112},... | collective-permute-start | bytes 196616 | tf_op jit(solution)/shard_map/ppermute | solution.py:35
  12.2 4.2 %collective-permute-start.2 = (bf16[128,256]{1,0:T(8,128)(2,1)}, bf16[128,256]{1,0:T(8,128)(2,1)S(1)}, u32[]{:S(2)}, u32[]{:S(2)}) collective-permute-start(bf16[128,256]{1,0:T(8,128)(2,1)} %gather_fusion), channel_id=1, source_target_pairs={{0,1},{1,2},{2,3},{3,4},{4,5},{5,6},{6,7},{7,8},{8,9},{9,10},{10,1... | collective-permute-start | bytes 196616 | tf_op jit(solution)/shard_map/ppermute | solution.py:34
  16.4 10.5 %collective-permute-start.3 = (bf16[128,256]{1,0:T(8,128)(2,1)}, bf16[128,256]{1,0:T(8,128)(2,1)S(1)}, u32[]{:S(2)}, u32[]{:S(2)}) collective-permute-start(bf16[128,256]{1,0:T(8,128)(2,1)} %gather_fusion), channel_id=1, source_target_pairs={{1,0},{2,1},{3,2},{4,3},{5,4},{6,5},{7,6},{8,7},{9,8},{10,9},{11,1... | collective-permute-start | bytes 196616 | tf_op jit(solution)/shard_map/ppermute | solution.py:35
  27.0 0.1 copy.16
  27.1 0.1 reshape.143
  27.2 0.1 iota_compare_fusion.3
  27.3 0.3 fusion.18
  27.6 0.4 convolution_bitcast_fusion.2
  28.1 0.0 collective-permute-done
  28.1 0.8 bitcast_dynamic-update-slice_fusion.3
  28.9 0.0 collective-permute-done.1
  28.9 0.0 collective-permute-done.2
  29.0 0.0 collective-permute-done.3
  29.0 0.4 convolution_convert_fusion
  29.4 2.0 %gather_fusion.1 = bf16[32,128,256]{2,1,0:T(8,128)(2,1)} fusion(bf16[12,128,256]{2,1,0:T(8,128)(2,1)S(1)} %bitcast.72, s32[1024]{0:T(1024)S(1)} %pad_clamp_fusion), kind=kCustom, calls=%fused_computation.1 | custom fusion | bytes 4194432 | tf_op jit(solution)/shard_map/gather | solution.py:112
  31.4 2.5 %fusion.3 = bf16[8,128,256]{2,1,0:T(8,128)(2,1)S(1)} fusion(bf16[8,4,128,256]{3,2,1,0:T(8,128)(2,1)} %bitcast.75, bf16[8,4,128,128]{3,2,1,0:T(8,128)(2,1)} %param.11, pred[8,4]{1,0:T(8,128)(4,1)S(1)} %iota_compare_fusion.3), kind=kOutput, calls=%fused_computation.16 | convolution fusion | flops 269221888 | bytes 3670048 | tf_op jit(solution)/shard_map/bkij,bkjh->bih/dot_general | solution.py:111
  33.9 0.3 convolution_add_fusion.1
  34.2 0.7 copy-done.1
  34.9 1.0 convolution_bitcast_fusion.3
  35.9 0.7 pad_maximum_fusion
  36.5 4.1 %all-to-all-start = ((f32[16,8,256]{2,1,0:T(8,128)}), f32[16,8,256]{2,1,0:T(8,128)}, u32[]{:S(2)}, u32[]{:S(2)}) async-start(f32[16,8,256]{2,1,0:T(8,128)} %bitcast.13), calls=%async_computation | async-start | bytes 262144 | tf_op jit(solution)/shard_map/all_to_all | solution.py:17
  40.6 0.7 gather_fusion.2
  41.3 8.0 %all-to-all-done = f32[16,8,256]{2,1,0:T(8,128)} async-done(((f32[16,8,256]{2,1,0:T(8,128)}), f32[16,8,256]{2,1,0:T(8,128)}, u32[]{:S(2)}, u32[]{:S(2)}) %all-to-all-start) | async-done | bytes 131104 | tf_op jit(solution)/shard_map/all_to_all | solution.py:17
  49.3 0.9 reduce_sum.92
  50.2 0.7 broadcast_in_dim.22
  50.9 3.4 %all-to-all-start.1 = ((f32[16,8,256]{2,1,0:T(8,128)}), f32[16,8,256]{2,1,0:T(8,128)S(1)}, u32[]{:S(2)}, u32[]{:S(2)}) async-start(f32[16,8,256]{2,1,0:T(8,128)} %broadcast_in_dim.22), calls=%async_computation.1 | async-start | bytes 262144 | tf_op jit(solution)/shard_map/all_to_all | solution.py:24
  54.3 0.0 copy-start.9
  54.3 0.0 copy-start.5
  54.3 2.6 %fusion.4 = bf16[8,128,256]{2,1,0:T(8,128)(2,1)} fusion(bf16[8,4,128,256]{3,2,1,0:T(8,128)(2,1)S(1)} %bitcast.74, bf16[8,4,128,128]{3,2,1,0:T(8,128)(2,1)} %param.11, pred[8,4]{1,0:T(8,128)(4,1)S(1)} %iota_compare_fusion.3), kind=kOutput, calls=%fused_computation.17 | convolution fusion | flops 269221888 | bytes 3670048 | tf_op jit(solution)/shard_map/bkij,bkjh->bih/dot_general | solution.py:115
  56.9 6.4 %all-to-all-done.1 = f32[16,8,256]{2,1,0:T(8,128)S(1)} async-done(((f32[16,8,256]{2,1,0:T(8,128)}), f32[16,8,256]{2,1,0:T(8,128)S(1)}, u32[]{:S(2)}, u32[]{:S(2)}) %all-to-all-start.1) | async-done | bytes 131104 | tf_op jit(solution)/shard_map/all_to_all | solution.py:24
  63.3 0.1 fusion.49
  63.4 0.1 div.42
  63.5 0.2 multiply_reduce_fusion.1
  63.7 0.1 rsqrt.21
  63.8 0.8 fusion.24
  64.6 0.6 reshape.131
  65.2 0.3 fusion.48
  65.5 0.0 copy-start.8
  65.6 0.0 copy-start.14
  65.6 2.1 %fusion.2 = bf16[1024,256]{1,0:T(8,128)(2,1)S(1)} fusion(f32[1024,256]{1,0:T(8,128)} %copy-done.2, bf16[1024,256]{1,0:T(8,128)(2,1)S(1)} %copy-done.5, s32[1024]{0:T(1024)S(1)} %copy-done.10, f32[64,256]{1,0:T(8,128)S(1)} %get-tuple-element.8, f32[64]{0:T(128)S(1)} %get-tuple-element.9, f32[64]{0:T(128)S(1)} %get-tuple-element.10, f32[64]{0:T(128)S(1)} %rsqrt.21, ...), kind=kOutput, calls=%fused_computation.15 | convolution fusion | flops 204374016 | bytes 2234368 | tf_op jit(solution)/shard_map/dot_general | solution.py:149
  67.7 0.6 fusion.7
  68.4 0.8 copy.17
  69.2 3.6 %all-to-all-start.2 = ((f32[32,16,128]{2,0,1:T(8,128)}), f32[32,16,128]{2,0,1:T(8,128)S(1)}, u32[]{:S(2)}, u32[]{:S(2)}) async-start(f32[32,16,128]{2,0,1:T(8,128)} %copy.17), calls=%async_computation.2 | async-start | bytes 524288 | tf_op jit(solution)/shard_map/all_to_all | solution.py:17
  72.8 0.6 unstack.18
  73.3 0.5 fusion.11
  73.8 0.6 copy.18
  74.5 0.8 constant_dynamic-slice_fusion
  75.3 0.1 fusion.41
  75.4 8.6 %all-to-all-done.2 = f32[32,16,128]{2,0,1:T(8,128)S(1)} async-done(((f32[32,16,128]{2,0,1:T(8,128)}), f32[32,16,128]{2,0,1:T(8,128)S(1)}, u32[]{:S(2)}, u32[]{:S(2)}) %all-to-all-start.2) | async-done | bytes 262176 | tf_op jit(solution)/shard_map/all_to_all | solution.py:17
  84.1 12.4 %all_to_all.29 = f32[8,8,128]{2,0,1:T(8,128)S(1)} all-to-all(f32[8,8,128]{2,0,1:T(8,128)S(1)} %copy.20), channel_id=1, replica_groups=mesh['z'=8,'x'=8,'y'=8,'core'=2] {'x'}, dimensions={1} | all-to-all | bytes 65536 | tf_op jit(solution)/shard_map/all_to_all | solution.py:17
  96.4 0.6 reduce_sum.98
  97.0 16.3 %all-to-all-start.4 = ((f32[8,1,128]{2,1,0:T(1,128)}), f32[8,1,128]{2,1,0:T(1,128)S(1)}, u32[]{:S(2)}, u32[]{:S(2)}) async-start(f32[8,1,128]{2,1,0:T(1,128)} %bitcast.23), calls=%async_computation.4 | async-start | bytes 8192 | tf_op jit(solution)/shard_map/all_to_all | solution.py:17
  113.4 2.1 %fusion.1 = bf16[1024,256]{1,0:T(8,128)(2,1)} fusion(s32[1024]{0:T(1024)S(1)} %copy-done.10, f32[64,256]{1,0:T(8,128)} %get-tuple-element.7, f32[1024,256]{1,0:T(8,128)S(1)} %copy-done.3, bf16[1024,256]{1,0:T(8,128)(2,1)S(1)} %copy-done.1), kind=kOutput, calls=%fused_computation.14 | convolution fusion | flops 35930112 | bytes 2166784 | tf_op jit(solution)/shard_map/dot_general | solution.py:132
  115.5 4.4 %all-to-all-done.4 = f32[8,1,128]{2,1,0:T(1,128)S(1)} async-done(((f32[8,1,128]{2,1,0:T(1,128)}), f32[8,1,128]{2,1,0:T(1,128)S(1)}, u32[]{:S(2)}, u32[]{:S(2)}) %all-to-all-start.4) | async-done | bytes 4128 | tf_op jit(solution)/shard_map/all_to_all | solution.py:17
  119.9 0.5 reduce_sum.99
  (38 shorter events, 0.2 us)
Async XLA Ops:
  0.6 28.3 %copy-start = (bf16[256,256]{1,0:T(8,128)(2,1)S(1)}, bf16[256,256]{1,0:T(8,128)(2,1)}, u32[]{:S(2)}) copy-start(bf16[256,256]{1,0:T(8,128)(2,1)} %param.16) | copy-start | bytes 393220
  0.6 4.3 %copy-start.12 = (s32[128]{0:T(128)S(1)}, s32[128]{0:T(128)}, u32[]{:S(2)}) copy-start(s32[128]{0:T(128)} %param.14) | copy-start | bytes 1540
  0.7 26.4 %copy-start.11 = (s32[8,4]{0,1:T(4,128)S(1)}, s32[8,4]{0,1:T(4,128)}, u32[]{:S(2)}) copy-start(s32[8,4]{0,1:T(4,128)} %param.12) | copy-start | bytes 388
  0.7 26.5 %copy-start.13 = (s32[8]{0:T(128)S(1)}, s32[8]{0:T(128)}, u32[]{:S(2)}) copy-start(s32[8]{0:T(128)} %param.13) | copy-start | bytes 100
  0.7 26.6 %copy-start.6 = (bf16[512,256]{1,0:T(8,128)(2,1)S(1)}, bf16[512,256]{1,0:T(8,128)(2,1)}, u32[]{:S(2)}) copy-start(bf16[512,256]{1,0:T(8,128)(2,1)} %param.17) | copy-start | bytes 786436
  3.4 24.1 %copy-start.4 = (bf16[1024,256]{1,0:T(8,128)(2,1)S(1)}, bf16[1024,256]{1,0:T(8,128)(2,1)}, u32[]{:S(2)}) copy-start(bf16[1024,256]{1,0:T(8,128)(2,1)} %param.19) | copy-start | bytes 1572868
  3.4 24.1 %copy-start.10 = (s32[1024]{0:T(1024)S(1)}, s32[1024]{0:T(1024)}, u32[]{:S(2)}) copy-start(s32[1024]{0:T(1024)} %param.15) | copy-start | bytes 12292
  6.4 21.6 %collective-permute-start = (bf16[128,256]{1,0:T(8,128)(2,1)}, bf16[128,256]{1,0:T(8,128)(2,1)}, u32[]{:S(2)}, u32[]{:S(2)}) collective-permute-start(bf16[128,256]{1,0:T(8,128)(2,1)} %gather_fusion), channel_id=1, source_target_pairs={{0,16},{16,32},{32,48},{48,64},{64,80},{80,96},{96,112},{112,128},... | collective-permute-start | bytes 196616 | tf_op jit(solution)/shard_map/ppermute | solution.py:34
  11.0 18.0 %collective-permute-start.1 = (bf16[128,256]{1,0:T(8,128)(2,1)}, bf16[128,256]{1,0:T(8,128)(2,1)S(1)}, u32[]{:S(2)}, u32[]{:S(2)}) collective-permute-start(bf16[128,256]{1,0:T(8,128)(2,1)} %gather_fusion), channel_id=1, source_target_pairs={{16,0},{32,16},{48,32},{64,48},{80,64},{96,80},{112,96},{128,112},... | collective-permute-start | bytes 196616 | tf_op jit(solution)/shard_map/ppermute | solution.py:35
  12.2 16.7 %collective-permute-start.2 = (bf16[128,256]{1,0:T(8,128)(2,1)}, bf16[128,256]{1,0:T(8,128)(2,1)S(1)}, u32[]{:S(2)}, u32[]{:S(2)}) collective-permute-start(bf16[128,256]{1,0:T(8,128)(2,1)} %gather_fusion), channel_id=1, source_target_pairs={{0,1},{1,2},{2,3},{3,4},{4,5},{5,6},{6,7},{7,8},{8,9},{9,10},{10,1... | collective-permute-start | bytes 196616 | tf_op jit(solution)/shard_map/ppermute | solution.py:34
  16.4 12.5 %collective-permute-start.3 = (bf16[128,256]{1,0:T(8,128)(2,1)}, bf16[128,256]{1,0:T(8,128)(2,1)S(1)}, u32[]{:S(2)}, u32[]{:S(2)}) collective-permute-start(bf16[128,256]{1,0:T(8,128)(2,1)} %gather_fusion), channel_id=1, source_target_pairs={{1,0},{2,1},{3,2},{4,3},{5,4},{6,5},{7,6},{8,7},{9,8},{10,9},{11,1... | collective-permute-start | bytes 196616 | tf_op jit(solution)/shard_map/ppermute | solution.py:35
  31.4 2.5 %copy-start.7 = (bf16[512,256]{1,0:T(8,128)(2,1)S(1)}, bf16[512,256]{1,0:T(8,128)(2,1)}, u32[]{:S(2)}) copy-start(bf16[512,256]{1,0:T(8,128)(2,1)} %param.17) | copy-start | bytes 786436
  33.8 1.0 copy-start.1
  34.9 1.0 copy-start.2
  36.5 12.8 %all-to-all-start = ((f32[16,8,256]{2,1,0:T(8,128)}), f32[16,8,256]{2,1,0:T(8,128)}, u32[]{:S(2)}, u32[]{:S(2)}) async-start(f32[16,8,256]{2,1,0:T(8,128)} %bitcast.13), calls=%async_computation | async-start | bytes 262144 | tf_op jit(solution)/shard_map/all_to_all | solution.py:17
  50.9 12.5 %all-to-all-start.1 = ((f32[16,8,256]{2,1,0:T(8,128)}), f32[16,8,256]{2,1,0:T(8,128)S(1)}, u32[]{:S(2)}, u32[]{:S(2)}) async-start(f32[16,8,256]{2,1,0:T(8,128)} %broadcast_in_dim.22), calls=%async_computation.1 | async-start | bytes 262144 | tf_op jit(solution)/shard_map/all_to_all | solution.py:24
  54.3 9.5 %copy-start.9 = (bf16[256,256]{1,0:T(8,128)(2,1)S(1)}, bf16[256,256]{1,0:T(8,128)(2,1)}, u32[]{:S(2)}) copy-start(bf16[256,256]{1,0:T(8,128)(2,1)} %param.18) | copy-start | bytes 393220
  54.3 11.2 %copy-start.5 = (bf16[1024,256]{1,0:T(8,128)(2,1)S(1)}, bf16[1024,256]{1,0:T(8,128)(2,1)}, u32[]{:S(2)}) copy-start(bf16[1024,256]{1,0:T(8,128)(2,1)} %param.19) | copy-start | bytes 1572868
  65.5 2.2 %copy-start.8 = (bf16[512,256]{1,0:T(8,128)(2,1)S(1)}, bf16[512,256]{1,0:T(8,128)(2,1)}, u32[]{:S(2)}) copy-start(bf16[512,256]{1,0:T(8,128)(2,1)} %param.17) | copy-start | bytes 786436
  65.6 2.2 %copy-start.14 = (bf16[8,128,256]{2,1,0:T(8,128)(2,1)S(1)}, bf16[8,128,256]{2,1,0:T(8,128)(2,1)}, u32[]{:S(2)}) copy-start(bf16[8,128,256]{2,1,0:T(8,128)(2,1)} %fusion.4) | copy-start | bytes 1572868
  69.2 44.2 %copy-start.3 = (f32[1024,256]{1,0:T(8,128)S(1)}, f32[1024,256]{1,0:T(8,128)}, u32[]{:S(2)}) copy-start(f32[1024,256]{1,0:T(8,128)} %copy-done.2) | copy-start | bytes 3145732
  69.2 14.8 %all-to-all-start.2 = ((f32[32,16,128]{2,0,1:T(8,128)}), f32[32,16,128]{2,0,1:T(8,128)S(1)}, u32[]{:S(2)}, u32[]{:S(2)}) async-start(f32[32,16,128]{2,0,1:T(8,128)} %copy.17), calls=%async_computation.2 | async-start | bytes 524288 | tf_op jit(solution)/shard_map/all_to_all | solution.py:17
  97.0 22.9 %all-to-all-start.4 = ((f32[8,1,128]{2,1,0:T(1,128)}), f32[8,1,128]{2,1,0:T(1,128)S(1)}, u32[]{:S(2)}, u32[]{:S(2)}) async-start(f32[8,1,128]{2,1,0:T(1,128)} %bitcast.23), calls=%async_computation.4 | async-start | bytes 8192 | tf_op jit(solution)/shard_map/all_to_all | solution.py:17

commit v6 on v3

--- a/solution.py
+++ b/solution.py
@@ -93,7 +93,9 @@
     inputs = features.astype(jnp.float32)
     normed, _ = normalize(inputs)
     scaled = normed.astype(jnp.bfloat16)
-    rim_rows = scaled[bnd_index]
+    node_count = scaled.shape[0]
+    pick = (bnd_index[:, None] == jnp.arange(node_count)[None, :]).astype(jnp.bfloat16)
+    rim_rows = jnp.dot(pick, scaled, preferred_element_type=jnp.float32).astype(jnp.bfloat16)
     halo_tiles = neighbour_tiles(rim_rows)
     sources = jnp.concatenate(
         [scaled.reshape(blocks, tile_rows, feature_count), halo_tiles], axis=0

time: 118 us -> 118 us (level)
  local copies, waits for them, and re-layouts: 10.3 us -> 8.8 us
    gather x1 -> x0, local copies, waits for them, and re-layouts: 1.48 us -> none  [local(): rim_rows = scaled[bnd_index]]
where the time goes in v6:
time: 118 us; the launch traced here: 117 us
  starting transfers between devices  52.9 us (45%)
  waiting for transfers between devices  31.8 us (27%)
  matrix products  14.5 us (12%)
  local copies, waits for them, and re-layouts  8.8 us (7%)
  other arithmetic  7.8 us (7%)
    all_to_all x3, starting transfers between devices, scatter_sum(): return lax.all_to_all(pieces, axes, dim, dim, tiled=False).sum(dim)  29 us
    all_to_all x3, waiting for transfers between devices, scatter_sum(): return lax.all_to_all(pieces, axes, dim, dim, tiled=False).sum(dim)  25.3 us
    ppermute x2, starting transfers between devices, neighbour_tiles(): tiles.append(lax.ppermute(tile, axis, backward))  11.8 us
    ppermute x2, starting transfers between devices, neighbour_tiles(): tiles.append(lax.ppermute(tile, axis, forward))  8.71 us
    all_to_all x1, waiting for transfers between devices, all_sum(): lax.all_to_all(jnp.broadcast_to(mine, (count,) + mine.shape), axis, 0, 0,...  6.44 us
    all_to_all x1, starting transfers between devices, all_sum(): lax.all_to_all(jnp.broadcast_to(mine, (count,) + mine.shape), axis, 0, 0,...  3.41 us
    dot_general x1, matrix products, local(): jnp.einsum('bkij,bkjh->bih', masked_tiles, sources[adj_index], preferred_...  2.59 us
    dot_general x1, matrix products, local(): jnp.einsum('bkij,bkjh->bih', masked_tiles, messages[adj_index], preferred...  2.46 us
  transfers between devices with their start and end apart: 8, of which 4 were waited for; matrix products, arithmetic and copies ran while one was open for 8% of the time, Pallas kernels for 0%

profile of v6, /device:TPU:1, one launch (start us, length us, event | category | flops | bytes accessed | tf_op | source)
XLA Modules:
  0.0 116.9 jit_solution(12533882566458365073)
XLA Ops:
  0.6 0.0 copy-start
  0.7 0.0 copy-start.6
  0.7 1.3 %convert_reduce_fusion = f32[1024]{0:T(1024)S(1)} fusion(bf16[1024,256]{1,0:T(8,128)(2,1)} %param.10), kind=kLoop, calls=%fused_computation.5 | loop fusion | flops 523264 | bytes 528384 | tf_op jit(solution)/shard_map/reduce_sum | solution.py:36
  2.0 1.4 %fusion.8 = f32[1024]{0:T(1024)S(1)} fusion(bf16[1024,256]{1,0:T(8,128)(2,1)} %param.10, f32[1024]{0:T(1024)S(1)} %broadcast_multiply_fusion.1), kind=kLoop, calls=%fused_computation.23 | loop fusion | flops 1047552 | bytes 532480 | tf_op jit(solution)/shard_map/reduce_sum | solution.py:37
  3.4 0.0 copy-start.4
  3.4 0.0 copy-start.10
  3.5 1.4 %fusion.9 = bf16[1024,256]{1,0:T(8,128)(2,1)S(1)} fusion(bf16[1024,256]{1,0:T(8,128)(2,1)} %param.10, f32[1024]{0:T(1024)S(1)} %add_rsqrt_fusion.1, f32[1024]{0:T(1024)S(1)} %broadcast_multiply_fusion.1), kind=kLoop, calls=%fused_computation.24 | loop fusion | flops 1048576 | bytes 1056768 | tf_op jit(solution)/shard_map/convert_element_type | solution.py:95
  4.9 0.0 copy-done.12
  4.9 0.9 convolution_convert_fusion.2
  5.8 4.6 %collective-permute-start = (bf16[128,256]{1,0:T(8,128)(2,1)}, bf16[128,256]{1,0:T(8,128)(2,1)}, u32[]{:S(2)}, u32[]{:S(2)}) collective-permute-start(bf16[128,256]{1,0:T(8,128)(2,1)} %convolution_convert_fusion.2), channel_id=1, source_target_pairs={{0,16},{16,32},{32,48},{48,64},{64,80},{80,96},{96,112},{112,128},... | collective-permute-start | bytes 196616 | tf_op jit(solution)/shard_map/ppermute | solution.py:30
  10.4 1.3 %collective-permute-start.1 = (bf16[128,256]{1,0:T(8,128)(2,1)}, bf16[128,256]{1,0:T(8,128)(2,1)S(1)}, u32[]{:S(2)}, u32[]{:S(2)}) collective-permute-start(bf16[128,256]{1,0:T(8,128)(2,1)} %convolution_convert_fusion.2), channel_id=1, source_target_pairs={{16,0},{32,16},{48,32},{64,48},{80,64},{96,80},{112,96},{128,112},... | collective-permute-start | bytes 196616 | tf_op jit(solution)/shard_map/ppermute | solution.py:31
  11.7 4.2 %collective-permute-start.2 = (bf16[128,256]{1,0:T(8,128)(2,1)}, bf16[128,256]{1,0:T(8,128)(2,1)S(1)}, u32[]{:S(2)}, u32[]{:S(2)}) collective-permute-start(bf16[128,256]{1,0:T(8,128)(2,1)} %convolution_convert_fusion.2), channel_id=1, source_target_pairs={{0,1},{1,2},{2,3},{3,4},{4,5},{5,6},{6,7},{7,8},{8,9},{9,10},{10,1... | collective-permute-start | bytes 196616 | tf_op jit(solution)/shard_map/ppermute | solution.py:30
  15.8 10.5 %collective-permute-start.3 = (bf16[128,256]{1,0:T(8,128)(2,1)}, bf16[128,256]{1,0:T(8,128)(2,1)S(1)}, u32[]{:S(2)}, u32[]{:S(2)}) collective-permute-start(bf16[128,256]{1,0:T(8,128)(2,1)} %convolution_convert_fusion.2), channel_id=1, source_target_pairs={{1,0},{2,1},{3,2},{4,3},{5,4},{6,5},{7,6},{8,7},{9,8},{10,9},{11,1... | collective-permute-start | bytes 196616 | tf_op jit(solution)/shard_map/ppermute | solution.py:31
  26.4 0.1 copy.16
  26.5 0.1 reshape.132
  26.6 0.1 iota_compare_fusion.5
  26.7 0.3 fusion.19
  27.0 0.4 convolution_bitcast_fusion.2
  27.5 0.0 collective-permute-done
  27.5 0.8 bitcast_dynamic-update-slice_fusion.3
  28.3 0.0 collective-permute-done.1
  28.3 0.0 collective-permute-done.2
  28.4 0.0 collective-permute-done.3
  28.4 0.4 convolution_convert_fusion
  28.8 2.0 %gather_fusion = bf16[32,128,256]{2,1,0:T(8,128)(2,1)} fusion(bf16[12,128,256]{2,1,0:T(8,128)(2,1)S(1)} %bitcast.73, s32[1024]{0:T(1024)S(1)} %pad_clamp_fusion), kind=kCustom, calls=%fused_computation | custom fusion | bytes 4194432 | tf_op jit(solution)/shard_map/gather | solution.py:110
  30.8 2.5 %fusion.3 = bf16[8,128,256]{2,1,0:T(8,128)(2,1)S(1)} fusion(bf16[8,4,128,256]{3,2,1,0:T(8,128)(2,1)} %bitcast.76, bf16[8,4,128,128]{3,2,1,0:T(8,128)(2,1)} %param.11, pred[8,4]{1,0:T(8,128)(4,1)S(1)} %iota_compare_fusion.5), kind=kOutput, calls=%fused_computation.15 | convolution fusion | flops 269221888 | bytes 3670048 | tf_op jit(solution)/shard_map/bkij,bkjh->bih/dot_general | solution.py:109
  33.3 0.3 convolution_add_fusion.1
  33.6 0.7 copy-done.1
  34.3 1.0 convolution_bitcast_fusion.3
  35.3 0.7 pad_maximum_fusion
  35.9 4.1 %all-to-all-start = ((f32[16,8,256]{2,1,0:T(8,128)}), f32[16,8,256]{2,1,0:T(8,128)}, u32[]{:S(2)}, u32[]{:S(2)}) async-start(f32[16,8,256]{2,1,0:T(8,128)} %bitcast.13), calls=%async_computation | async-start | bytes 262144 | tf_op jit(solution)/shard_map/all_to_all | solution.py:13
  40.0 0.7 gather_fusion.1
  40.7 8.0 %all-to-all-done = f32[16,8,256]{2,1,0:T(8,128)} async-done(((f32[16,8,256]{2,1,0:T(8,128)}), f32[16,8,256]{2,1,0:T(8,128)}, u32[]{:S(2)}, u32[]{:S(2)}) %all-to-all-start) | async-done | bytes 131104 | tf_op jit(solution)/shard_map/all_to_all | solution.py:13
  48.7 0.9 reduce_sum.83
  49.6 0.7 broadcast_in_dim.19
  50.3 3.4 %all-to-all-start.1 = ((f32[16,8,256]{2,1,0:T(8,128)}), f32[16,8,256]{2,1,0:T(8,128)S(1)}, u32[]{:S(2)}, u32[]{:S(2)}) async-start(f32[16,8,256]{2,1,0:T(8,128)} %broadcast_in_dim.19), calls=%async_computation.1 | async-start | bytes 262144 | tf_op jit(solution)/shard_map/all_to_all | solution.py:20
  53.7 0.0 copy-start.9
  53.7 0.0 copy-start.5
  53.7 2.6 %fusion.4 = bf16[8,128,256]{2,1,0:T(8,128)(2,1)} fusion(bf16[8,4,128,256]{3,2,1,0:T(8,128)(2,1)S(1)} %bitcast.75, bf16[8,4,128,128]{3,2,1,0:T(8,128)(2,1)} %param.11, pred[8,4]{1,0:T(8,128)(4,1)S(1)} %iota_compare_fusion.5), kind=kOutput, calls=%fused_computation.16 | convolution fusion | flops 269221888 | bytes 3670048 | tf_op jit(solution)/shard_map/bkij,bkjh->bih/dot_general | solution.py:113
  56.3 6.4 %all-to-all-done.1 = f32[16,8,256]{2,1,0:T(8,128)S(1)} async-done(((f32[16,8,256]{2,1,0:T(8,128)}), f32[16,8,256]{2,1,0:T(8,128)S(1)}, u32[]{:S(2)}, u32[]{:S(2)}) %all-to-all-start.1) | async-done | bytes 131104 | tf_op jit(solution)/shard_map/all_to_all | solution.py:20
  62.8 0.1 fusion.50
  62.9 0.1 div.42
  62.9 0.2 multiply_reduce_fusion.1
  63.1 0.1 rsqrt.21
  63.2 0.8 fusion.25
  64.0 0.6 reshape.129
  64.6 0.3 fusion.49
  65.0 0.0 copy-start.8
  65.0 0.0 copy-start.14
  65.0 2.1 %fusion.2 = bf16[1024,256]{1,0:T(8,128)(2,1)S(1)} fusion(f32[1024,256]{1,0:T(8,128)} %copy-done.2, bf16[1024,256]{1,0:T(8,128)(2,1)S(1)} %copy-done.5, s32[1024]{0:T(1024)S(1)} %copy-done.10, f32[64,256]{1,0:T(8,128)S(1)} %get-tuple-element.8, f32[64]{0:T(128)S(1)} %get-tuple-element.9, f32[64]{0:T(128)S(1)} %get-tuple-element.10, f32[64]{0:T(128)S(1)} %rsqrt.21, ...), kind=kOutput, calls=%fused_computation.14 | convolution fusion | flops 204374016 | bytes 2234368 | tf_op jit(solution)/shard_map/dot_general | solution.py:147
  67.1 0.6 fusion.7
  67.8 0.8 copy.17
  68.6 3.6 %all-to-all-start.2 = ((f32[32,16,128]{2,0,1:T(8,128)}), f32[32,16,128]{2,0,1:T(8,128)S(1)}, u32[]{:S(2)}, u32[]{:S(2)}) async-start(f32[32,16,128]{2,0,1:T(8,128)} %copy.17), calls=%async_computation.2 | async-start | bytes 524288 | tf_op jit(solution)/shard_map/all_to_all | solution.py:13
  72.2 0.6 unstack.18
  72.8 0.5 fusion.11
  73.2 0.6 copy.18
  73.9 0.8 constant_dynamic-slice_fusion
  74.7 0.1 fusion.42
  74.8 8.6 %all-to-all-done.2 = f32[32,16,128]{2,0,1:T(8,128)S(1)} async-done(((f32[32,16,128]{2,0,1:T(8,128)}), f32[32,16,128]{2,0,1:T(8,128)S(1)}, u32[]{:S(2)}, u32[]{:S(2)}) %all-to-all-start.2) | async-done | bytes 262176 | tf_op jit(solution)/shard_map/all_to_all | solution.py:13
  83.5 0.6 pad_maximum_fusion.1
  84.1 21.4 %all-to-all-start.3 = ((f32[64,1,128]{2,1,0:T(1,128)}), f32[64,1,128]{2,1,0:T(1,128)S(1)}, u32[]{:S(2)}, u32[]{:S(2)}) async-start(f32[64,1,128]{2,1,0:T(1,128)} %bitcast.23), calls=%async_computation.3 | async-start | bytes 65536 | tf_op jit(solution)/shard_map/all_to_all | solution.py:13
  105.5 2.1 %fusion.1 = bf16[1024,256]{1,0:T(8,128)(2,1)} fusion(s32[1024]{0:T(1024)S(1)} %copy-done.10, f32[64,256]{1,0:T(8,128)} %get-tuple-element.7, f32[1024,256]{1,0:T(8,128)S(1)} %copy-done.3, bf16[1024,256]{1,0:T(8,128)(2,1)S(1)} %copy-done.1), kind=kOutput, calls=%fused_computation.13 | convolution fusion | flops 35930112 | bytes 2166784 | tf_op jit(solution)/shard_map/dot_general | solution.py:130
  107.6 8.7 %all-to-all-done.3 = f32[64,1,128]{2,1,0:T(1,128)S(1)} async-done(((f32[64,1,128]{2,1,0:T(1,128)}), f32[64,1,128]{2,1,0:T(1,128)S(1)}, u32[]{:S(2)}, u32[]{:S(2)}) %all-to-all-start.3) | async-done | bytes 32800 | tf_op jit(solution)/shard_map/all_to_all | solution.py:13
  116.3 0.6 reduce_sum.89
  (33 shorter events, 0.2 us)
Async XLA Ops:
  0.6 27.8 %copy-start = (bf16[256,256]{1,0:T(8,128)(2,1)S(1)}, bf16[256,256]{1,0:T(8,128)(2,1)}, u32[]{:S(2)}) copy-start(bf16[256,256]{1,0:T(8,128)(2,1)} %param.16) | copy-start | bytes 393220
  0.6 4.3 %copy-start.12 = (s32[128]{0:T(128)S(1)}, s32[128]{0:T(128)}, u32[]{:S(2)}) copy-start(s32[128]{0:T(128)} %param.14) | copy-start | bytes 1540
  0.7 25.8 %copy-start.11 = (s32[8,4]{0,1:T(4,128)S(1)}, s32[8,4]{0,1:T(4,128)}, u32[]{:S(2)}) copy-start(s32[8,4]{0,1:T(4,128)} %param.12) | copy-start | bytes 388
  0.7 25.9 %copy-start.13 = (s32[8]{0:T(128)S(1)}, s32[8]{0:T(128)}, u32[]{:S(2)}) copy-start(s32[8]{0:T(128)} %param.13) | copy-start | bytes 100
  0.7 26.0 %copy-start.6 = (bf16[512,256]{1,0:T(8,128)(2,1)S(1)}, bf16[512,256]{1,0:T(8,128)(2,1)}, u32[]{:S(2)}) copy-start(bf16[512,256]{1,0:T(8,128)(2,1)} %param.17) | copy-start | bytes 786436
  3.4 23.6 %copy-start.4 = (bf16[1024,256]{1,0:T(8,128)(2,1)S(1)}, bf16[1024,256]{1,0:T(8,128)(2,1)}, u32[]{:S(2)}) copy-start(bf16[1024,256]{1,0:T(8,128)(2,1)} %param.19) | copy-start | bytes 1572868
  3.4 23.6 %copy-start.10 = (s32[1024]{0:T(1024)S(1)}, s32[1024]{0:T(1024)}, u32[]{:S(2)}) copy-start(s32[1024]{0:T(1024)} %param.15) | copy-start | bytes 12292
  5.8 21.7 %collective-permute-start = (bf16[128,256]{1,0:T(8,128)(2,1)}, bf16[128,256]{1,0:T(8,128)(2,1)}, u32[]{:S(2)}, u32[]{:S(2)}) collective-permute-start(bf16[128,256]{1,0:T(8,128)(2,1)} %convolution_convert_fusion.2), channel_id=1, source_target_pairs={{0,16},{16,32},{32,48},{48,64},{64,80},{80,96},{96,112},{112,128},... | collective-permute-start | bytes 196616 | tf_op jit(solution)/shard_map/ppermute | solution.py:30
  10.4 18.0 %collective-permute-start.1 = (bf16[128,256]{1,0:T(8,128)(2,1)}, bf16[128,256]{1,0:T(8,128)(2,1)S(1)}, u32[]{:S(2)}, u32[]{:S(2)}) collective-permute-start(bf16[128,256]{1,0:T(8,128)(2,1)} %convolution_convert_fusion.2), channel_id=1, source_target_pairs={{16,0},{32,16},{48,32},{64,48},{80,64},{96,80},{112,96},{128,112},... | collective-permute-start | bytes 196616 | tf_op jit(solution)/shard_map/ppermute | solution.py:31
  11.7 16.7 %collective-permute-start.2 = (bf16[128,256]{1,0:T(8,128)(2,1)}, bf16[128,256]{1,0:T(8,128)(2,1)S(1)}, u32[]{:S(2)}, u32[]{:S(2)}) collective-permute-start(bf16[128,256]{1,0:T(8,128)(2,1)} %convolution_convert_fusion.2), channel_id=1, source_target_pairs={{0,1},{1,2},{2,3},{3,4},{4,5},{5,6},{6,7},{7,8},{8,9},{9,10},{10,1... | collective-permute-start | bytes 196616 | tf_op jit(solution)/shard_map/ppermute | solution.py:30
  15.8 12.5 %collective-permute-start.3 = (bf16[128,256]{1,0:T(8,128)(2,1)}, bf16[128,256]{1,0:T(8,128)(2,1)S(1)}, u32[]{:S(2)}, u32[]{:S(2)}) collective-permute-start(bf16[128,256]{1,0:T(8,128)(2,1)} %convolution_convert_fusion.2), channel_id=1, source_target_pairs={{1,0},{2,1},{3,2},{4,3},{5,4},{6,5},{7,6},{8,7},{9,8},{10,9},{11,1... | collective-permute-start | bytes 196616 | tf_op jit(solution)/shard_map/ppermute | solution.py:31
  30.8 2.5 %copy-start.7 = (bf16[512,256]{1,0:T(8,128)(2,1)S(1)}, bf16[512,256]{1,0:T(8,128)(2,1)}, u32[]{:S(2)}) copy-start(bf16[512,256]{1,0:T(8,128)(2,1)} %param.17) | copy-start | bytes 786436
  33.2 1.0 copy-start.1
  34.3 1.0 copy-start.2
  35.9 12.8 %all-to-all-start = ((f32[16,8,256]{2,1,0:T(8,128)}), f32[16,8,256]{2,1,0:T(8,128)}, u32[]{:S(2)}, u32[]{:S(2)}) async-start(f32[16,8,256]{2,1,0:T(8,128)} %bitcast.13), calls=%async_computation | async-start | bytes 262144 | tf_op jit(solution)/shard_map/all_to_all | solution.py:13
  50.3 12.5 %all-to-all-start.1 = ((f32[16,8,256]{2,1,0:T(8,128)}), f32[16,8,256]{2,1,0:T(8,128)S(1)}, u32[]{:S(2)}, u32[]{:S(2)}) async-start(f32[16,8,256]{2,1,0:T(8,128)} %broadcast_in_dim.19), calls=%async_computation.1 | async-start | bytes 262144 | tf_op jit(solution)/shard_map/all_to_all | solution.py:20
  53.7 9.5 %copy-start.9 = (bf16[256,256]{1,0:T(8,128)(2,1)S(1)}, bf16[256,256]{1,0:T(8,128)(2,1)}, u32[]{:S(2)}) copy-start(bf16[256,256]{1,0:T(8,128)(2,1)} %param.18) | copy-start | bytes 393220
  53.7 11.2 %copy-start.5 = (bf16[1024,256]{1,0:T(8,128)(2,1)S(1)}, bf16[1024,256]{1,0:T(8,128)(2,1)}, u32[]{:S(2)}) copy-start(bf16[1024,256]{1,0:T(8,128)(2,1)} %param.19) | copy-start | bytes 1572868
  65.0 2.2 %copy-start.8 = (bf16[512,256]{1,0:T(8,128)(2,1)S(1)}, bf16[512,256]{1,0:T(8,128)(2,1)}, u32[]{:S(2)}) copy-start(bf16[512,256]{1,0:T(8,128)(2,1)} %param.17) | copy-start | bytes 786436
  65.0 2.2 %copy-start.14 = (bf16[8,128,256]{2,1,0:T(8,128)(2,1)S(1)}, bf16[8,128,256]{2,1,0:T(8,128)(2,1)}, u32[]{:S(2)}) copy-start(bf16[8,128,256]{2,1,0:T(8,128)(2,1)} %fusion.4) | copy-start | bytes 1572868
  68.6 36.8 %copy-start.3 = (f32[1024,256]{1,0:T(8,128)S(1)}, f32[1024,256]{1,0:T(8,128)}, u32[]{:S(2)}) copy-start(f32[1024,256]{1,0:T(8,128)} %copy-done.2) | copy-start | bytes 3145732
  68.6 14.8 %all-to-all-start.2 = ((f32[32,16,128]{2,0,1:T(8,128)}), f32[32,16,128]{2,0,1:T(8,128)S(1)}, u32[]{:S(2)}, u32[]{:S(2)}) async-start(f32[32,16,128]{2,0,1:T(8,128)} %copy.17), calls=%async_computation.2 | async-start | bytes 524288 | tf_op jit(solution)/shard_map/all_to_all | solution.py:13
  84.1 32.2 %all-to-all-start.3 = ((f32[64,1,128]{2,1,0:T(1,128)}), f32[64,1,128]{2,1,0:T(1,128)S(1)}, u32[]{:S(2)}, u32[]{:S(2)}) async-start(f32[64,1,128]{2,1,0:T(1,128)} %bitcast.23), calls=%async_computation.3 | async-start | bytes 65536 | tf_op jit(solution)/shard_map/all_to_all | solution.py:13

commit v7 on v6

--- a/solution.py
+++ b/solution.py
@@ -30,6 +30,21 @@
         tiles.append(lax.ppermute(tile, axis, forward))
         tiles.append(lax.ppermute(tile, axis, backward))
     return jnp.stack(tiles)
+
+
+def row_sums(values, precision=None):
+    ones = jnp.ones((values.shape[-1], 128), values.dtype)
+    return jnp.dot(values, ones, precision=precision, preferred_element_type=jnp.float32)
+
+
+def normalize_rows(features):
+    width = features.shape[-1]
+    repeat = width // 128
+    mean = row_sums(features) / width
+    center = features.astype(jnp.float32) - jnp.tile(mean, (1, repeat))
+    variance = row_sums(center * center, lax.Precision.HIGHEST) / width
+    inverse = lax.rsqrt(variance + eps)
+    return center * jnp.tile(inverse, (1, repeat))
 
 
 def normalize(values):
@@ -91,7 +106,7 @@
     slot_count = adj_tiles.shape[1]
     tile_rows = adj_tiles.shape[2]
     inputs = features.astype(jnp.float32)
-    normed, _ = normalize(inputs)
+    normed = normalize_rows(features)
     scaled = normed.astype(jnp.bfloat16)
     node_count = scaled.shape[0]
     pick = (bnd_index[:, None] == jnp.arange(node_count)[None, :]).astype(jnp.bfloat16)

time: 118 us -> 120 us (1.017)
  other arithmetic: 7.8 us -> 3.9 us
  matrix products: 14.5 us -> 18.4 us
  local copies, waits for them, and re-layouts: 8.8 us -> 11.5 us
    dot_general x0 -> x2, matrix products: none -> 2.38 us  [row_sums(): jnp.dot(values, ones, precision=precision, preferred_element_type=jnp.flo...]
    reduce_sum x2 -> x1, other arithmetic: 1.56 us -> 0.16 us  [normalize(): inverse = lax.rsqrt(jnp.mean(center * center, axis=-1, keepdims=True) + eps)]
    reduce_sum x1 -> x0, other arithmetic: 1.31 us -> none  [normalize(): center = values - jnp.mean(values, axis=-1, keepdims=True)]
  transfers between devices with their start and end apart: 8 -> 8, of which waited for: 4 -> 4; matrix products, arithmetic and copies ran while one was open for 8% -> 11% of each run, Pallas kernels for 0% -> 0%
where the time goes in v7:
time: 120 us; the launch traced here: 119 us
  starting transfers between devices  52.8 us (44%)
  waiting for transfers between devices  31.5 us (26%)
  matrix products  18.4 us (15%)
  local copies, waits for them, and re-layouts  11.5 us (10%)
  other arithmetic  3.9 us (3%)
    all_to_all x3, starting transfers between devices, scatter_sum(): return lax.all_to_all(pieces, axes, dim, dim, tiled=False).sum(dim)  28.3 us
    all_to_all x3, waiting for transfers between devices, scatter_sum(): return lax.all_to_all(pieces, axes, dim, dim, tiled=False).sum(dim)  25.4 us
    ppermute x2, starting transfers between devices, neighbour_tiles(): tiles.append(lax.ppermute(tile, axis, backward))  12.4 us
    ppermute x2, starting transfers between devices, neighbour_tiles(): tiles.append(lax.ppermute(tile, axis, forward))  8.72 us
    all_to_all x1, waiting for transfers between devices, all_sum(): lax.all_to_all(jnp.broadcast_to(mine, (count,) + mine.shape), axis, 0, 0,...  6.11 us
    all_to_all x1, starting transfers between devices, all_sum(): lax.all_to_all(jnp.broadcast_to(mine, (count,) + mine.shape), axis, 0, 0,...  3.41 us
    dot_general x4, matrix products, transposed_times(): lax.dot_general(operand, second, (((0,), (0,)), ((), ())), precision=prec...  2.8 us
    unnamed x34, local copies, waits for them, and re-layouts  2.66 us
  transfers between devices with their start and end apart: 8, of which 4 were waited for; matrix products, arithmetic and copies ran while one was open for 11% of the time, Pallas kernels for 0%

profile of v7, /device:TPU:1, one launch (start us, length us, event | category | flops | bytes accessed | tf_op | source)
XLA Modules:
  0.0 119.2 jit_solution(3969409566689717492)
XLA Ops:
  0.6 0.0 copy-start
  0.7 1.4 %fusion.8 = f32[1024,128]{0,1:T(8,128)S(1)} fusion(bf16[1024,256]{1,0:T(8,128)(2,1)} %param.10), kind=kOutput, calls=%fused_computation.21 | convolution fusion | flops 67239936 | bytes 1048576 | tf_op jit(solution)/shard_map/dot_general | solution.py:37
  2.1 0.2 copy.18
  2.3 0.4 tile.8
  2.7 1.0 fusion.6
  3.6 0.0 copy-start.12
  3.6 0.4 tile.20
  4.0 0.0 copy-start.11
  4.0 0.0 copy-start.13
  4.0 0.3 fusion.9
  4.3 0.0 copy-start.4
  4.3 0.0 copy-start.10
  4.3 0.9 convolution_convert_fusion.2
  5.2 4.6 %collective-permute-start = (bf16[128,256]{1,0:T(8,128)(2,1)}, bf16[128,256]{1,0:T(8,128)(2,1)}, u32[]{:S(2)}, u32[]{:S(2)}) collective-permute-start(bf16[128,256]{1,0:T(8,128)(2,1)} %convolution_convert_fusion.2), channel_id=1, source_target_pairs={{0,16},{16,32},{32,48},{48,64},{64,80},{80,96},{96,112},{112,128},... | collective-permute-start | bytes 196616 | tf_op jit(solution)/shard_map/ppermute | solution.py:30
  9.8 1.3 %collective-permute-start.1 = (bf16[128,256]{1,0:T(8,128)(2,1)}, bf16[128,256]{1,0:T(8,128)(2,1)}, u32[]{:S(2)}, u32[]{:S(2)}) collective-permute-start(bf16[128,256]{1,0:T(8,128)(2,1)} %convolution_convert_fusion.2), channel_id=1, source_target_pairs={{16,0},{32,16},{48,32},{64,48},{80,64},{96,80},{112,96},{128,112},... | collective-permute-start | bytes 196616 | tf_op jit(solution)/shard_map/ppermute | solution.py:31
  11.1 4.2 %collective-permute-start.2 = (bf16[128,256]{1,0:T(8,128)(2,1)}, bf16[128,256]{1,0:T(8,128)(2,1)}, u32[]{:S(2)}, u32[]{:S(2)}) collective-permute-start(bf16[128,256]{1,0:T(8,128)(2,1)} %convolution_convert_fusion.2), channel_id=1, source_target_pairs={{0,1},{1,2},{2,3},{3,4},{4,5},{5,6},{6,7},{7,8},{8,9},{9,10},{10,1... | collective-permute-start | bytes 196616 | tf_op jit(solution)/shard_map/ppermute | solution.py:30
  15.3 11.2 %collective-permute-start.3 = (bf16[128,256]{1,0:T(8,128)(2,1)}, bf16[128,256]{1,0:T(8,128)(2,1)}, u32[]{:S(2)}, u32[]{:S(2)}) collective-permute-start(bf16[128,256]{1,0:T(8,128)(2,1)} %convolution_convert_fusion.2), channel_id=1, source_target_pairs={{1,0},{2,1},{3,2},{4,3},{5,4},{6,5},{7,6},{8,7},{9,8},{10,9},{11,1... | collective-permute-start | bytes 196616 | tf_op jit(solution)/shard_map/ppermute | solution.py:31
  26.5 0.1 copy.19
  26.6 0.1 reshape.128
  26.7 0.1 iota_compare_fusion.5
  26.7 1.2 %fusion.20 = f32[1024,256]{1,0:T(8,128)S(1)} fusion(bf16[1024,256]{1,0:T(8,128)(2,1)S(1)} %fusion.9, bf16[512,256]{1,0:T(8,128)(2,1)} %param.17), kind=kOutput, calls=%fused_computation.44 | convolution fusion | flops 134217728 | bytes 1703936 | tf_op jit(solution)/shard_map/dot_general | solution.py:134
  27.9 1.1 convolution_bitcast_fusion.2
  29.0 0.8 bitcast_dynamic-update-slice_fusion.3
  29.9 0.8 bitcast_dynamic-update-slice_fusion.2
  30.7 0.8 bitcast_dynamic-update-slice_fusion.1
  31.6 0.8 bitcast_dynamic-update-slice_fusion
  32.4 0.4 convolution_convert_fusion
  32.8 2.0 %gather_fusion = bf16[32,128,256]{2,1,0:T(8,128)(2,1)} fusion(bf16[12,128,256]{2,1,0:T(8,128)(2,1)S(1)} %bitcast.89, s32[1024]{0:T(1024)S(1)} %pad_clamp_fusion), kind=kCustom, calls=%fused_computation | custom fusion | bytes 4194432 | tf_op jit(solution)/shard_map/gather | solution.py:125
  34.8 2.5 %fusion.3 = bf16[8,128,256]{2,1,0:T(8,128)(2,1)S(1)} fusion(bf16[8,4,128,256]{3,2,1,0:T(8,128)(2,1)} %bitcast.95, bf16[8,4,128,128]{3,2,1,0:T(8,128)(2,1)} %param.11, pred[8,4]{1,0:T(8,128)(4,1)S(1)} %iota_compare_fusion.5), kind=kOutput, calls=%fused_computation.14 | convolution fusion | flops 269221888 | bytes 3670048 | tf_op jit(solution)/shard_map/bkij,bkjh->bih/dot_general | solution.py:124
  37.3 0.3 convolution_add_fusion.1
  37.6 0.0 copy-start.6
  37.6 1.0 convolution_bitcast_fusion.3
  38.6 0.7 pad_maximum_fusion
  39.3 4.1 %all-to-all-start = ((f32[16,8,256]{2,1,0:T(8,128)}), f32[16,8,256]{2,1,0:T(8,128)}, u32[]{:S(2)}, u32[]{:S(2)}) async-start(f32[16,8,256]{2,1,0:T(8,128)} %bitcast.14), calls=%async_computation | async-start | bytes 262144 | tf_op jit(solution)/shard_map/all_to_all | solution.py:13
  43.4 0.7 gather_fusion.1
  44.1 7.5 %all-to-all-done = f32[16,8,256]{2,1,0:T(8,128)} async-done(((f32[16,8,256]{2,1,0:T(8,128)}), f32[16,8,256]{2,1,0:T(8,128)}, u32[]{:S(2)}, u32[]{:S(2)}) %all-to-all-start) | async-done | bytes 131104 | tf_op jit(solution)/shard_map/all_to_all | solution.py:13
  51.6 0.9 reduce_sum.63
  52.5 0.7 broadcast_in_dim.41
  53.2 3.4 %all-to-all-start.1 = ((f32[16,8,256]{2,1,0:T(8,128)}), f32[16,8,256]{2,1,0:T(8,128)S(1)}, u32[]{:S(2)}, u32[]{:S(2)}) async-start(f32[16,8,256]{2,1,0:T(8,128)} %broadcast_in_dim.41), calls=%async_computation.1 | async-start | bytes 262144 | tf_op jit(solution)/shard_map/all_to_all | solution.py:20
  56.6 0.0 copy-start.9
  56.6 2.6 %fusion.4 = bf16[8,128,256]{2,1,0:T(8,128)(2,1)} fusion(bf16[8,4,128,256]{3,2,1,0:T(8,128)(2,1)S(1)} %bitcast.94, bf16[8,4,128,128]{3,2,1,0:T(8,128)(2,1)} %param.11, pred[8,4]{1,0:T(8,128)(4,1)S(1)} %iota_compare_fusion.5), kind=kOutput, calls=%fused_computation.15 | convolution fusion | flops 269221888 | bytes 3670048 | tf_op jit(solution)/shard_map/bkij,bkjh->bih/dot_general | solution.py:128
  59.2 6.1 %all-to-all-done.1 = f32[16,8,256]{2,1,0:T(8,128)S(1)} async-done(((f32[16,8,256]{2,1,0:T(8,128)}), f32[16,8,256]{2,1,0:T(8,128)S(1)}, u32[]{:S(2)}, u32[]{:S(2)}) %all-to-all-start.1) | async-done | bytes 131104 | tf_op jit(solution)/shard_map/all_to_all | solution.py:20
  65.3 0.1 fusion.55
  65.4 0.1 div.45
  65.5 0.2 multiply_reduce_fusion.1
  65.7 0.1 rsqrt.16
  65.8 0.8 fusion.26
  66.6 0.6 reshape.125
  67.2 0.3 fusion.54
  67.5 2.1 %fusion.2 = bf16[1024,256]{1,0:T(8,128)(2,1)S(1)} fusion(f32[1024,256]{1,0:T(8,128)} %copy-done.2, bf16[1024,256]{1,0:T(8,128)(2,1)S(1)} %copy-done.5, s32[1024]{0:T(1024)S(1)} %copy-done.10, f32[64,256]{1,0:T(8,128)S(1)} %get-tuple-element.8, f32[64]{0:T(128)S(1)} %get-tuple-element.9, f32[64]{0:T(128)S(1)} %get-tuple-element.10, f32[64]{0:T(128)S(1)} %rsqrt.16, ...), kind=kOutput, calls=%fused_computation.13 | convolution fusion | flops 204374016 | bytes 2234368 | tf_op jit(solution)/shard_map/dot_general | solution.py:162
  69.7 0.6 fusion.7
  70.4 0.8 copy.20
  71.2 3.6 %all-to-all-start.2 = ((f32[32,16,128]{2,0,1:T(8,128)}), f32[32,16,128]{2,0,1:T(8,128)S(1)}, u32[]{:S(2)}, u32[]{:S(2)}) async-start(f32[32,16,128]{2,0,1:T(8,128)} %copy.20), calls=%async_computation.2 | async-start | bytes 524288 | tf_op jit(solution)/shard_map/all_to_all | solution.py:13
  74.7 0.6 unstack.18
  75.3 0.5 fusion.11
  75.8 0.6 copy.21
  76.4 0.8 constant_dynamic-slice_fusion
  77.2 0.1 fusion.45
  77.4 9.1 %all-to-all-done.2 = f32[32,16,128]{2,0,1:T(8,128)S(1)} async-done(((f32[32,16,128]{2,0,1:T(8,128)}), f32[32,16,128]{2,0,1:T(8,128)S(1)}, u32[]{:S(2)}, u32[]{:S(2)}) %all-to-all-start.2) | async-done | bytes 262176 | tf_op jit(solution)/shard_map/all_to_all | solution.py:13
  86.5 0.6 pad_maximum_fusion.1
  87.1 20.6 %all-to-all-start.3 = ((f32[64,1,128]{2,1,0:T(1,128)}), f32[64,1,128]{2,1,0:T(1,128)S(1)}, u32[]{:S(2)}, u32[]{:S(2)}) async-start(f32[64,1,128]{2,1,0:T(1,128)} %bitcast.24), calls=%async_computation.3 | async-start | bytes 65536 | tf_op jit(solution)/shard_map/all_to_all | solution.py:13
  107.8 2.1 %fusion.1 = bf16[1024,256]{1,0:T(8,128)(2,1)} fusion(s32[1024]{0:T(1024)S(1)} %copy-done.10, f32[64,256]{1,0:T(8,128)} %get-tuple-element.7, f32[1024,256]{1,0:T(8,128)S(1)} %copy-done.3, bf16[1024,256]{1,0:T(8,128)(2,1)S(1)} %copy-done.1), kind=kOutput, calls=%fused_computation.12 | convolution fusion | flops 35930112 | bytes 2166784 | tf_op jit(solution)/shard_map/dot_general | solution.py:145
  109.9 8.8 %all-to-all-done.3 = f32[64,1,128]{2,1,0:T(1,128)S(1)} async-done(((f32[64,1,128]{2,1,0:T(1,128)}), f32[64,1,128]{2,1,0:T(1,128)S(1)}, u32[]{:S(2)}, u32[]{:S(2)}) %all-to-all-start.3) | async-done | bytes 32800 | tf_op jit(solution)/shard_map/all_to_all | solution.py:13
  118.6 0.6 reduce_sum.69
  (34 shorter events, 0.2 us)
Async XLA Ops:
  0.6 31.8 %copy-start = (bf16[256,256]{1,0:T(8,128)(2,1)S(1)}, bf16[256,256]{1,0:T(8,128)(2,1)}, u32[]{:S(2)}) copy-start(bf16[256,256]{1,0:T(8,128)(2,1)} %param.16) | copy-start | bytes 393220
  0.6 2.0 %copy-start.1 = (bf16[1024,256]{1,0:T(8,128)(2,1)S(1)}, bf16[1024,256]{1,0:T(8,128)(2,1)}, u32[]{:S(2)}) copy-start(bf16[1024,256]{1,0:T(8,128)(2,1)} %param.10) | copy-start | bytes 1572868
  3.6 0.7 copy-start.12
  4.0 22.5 %copy-start.11 = (s32[8,4]{0,1:T(4,128)S(1)}, s32[8,4]{0,1:T(4,128)}, u32[]{:S(2)}) copy-start(s32[8,4]{0,1:T(4,128)} %param.12) | copy-start | bytes 388
  4.0 22.6 %copy-start.13 = (s32[8]{0:T(128)S(1)}, s32[8]{0:T(128)}, u32[]{:S(2)}) copy-start(s32[8]{0:T(128)} %param.13) | copy-start | bytes 100
  4.3 23.6 %copy-start.4 = (bf16[1024,256]{1,0:T(8,128)(2,1)S(1)}, bf16[1024,256]{1,0:T(8,128)(2,1)}, u32[]{:S(2)}) copy-start(bf16[1024,256]{1,0:T(8,128)(2,1)} %param.19) | copy-start | bytes 1572868
  4.3 23.6 %copy-start.10 = (s32[1024]{0:T(1024)S(1)}, s32[1024]{0:T(1024)}, u32[]{:S(2)}) copy-start(s32[1024]{0:T(1024)} %param.15) | copy-start | bytes 12292
  5.2 23.8 %collective-permute-start = (bf16[128,256]{1,0:T(8,128)(2,1)}, bf16[128,256]{1,0:T(8,128)(2,1)}, u32[]{:S(2)}, u32[]{:S(2)}) collective-permute-start(bf16[128,256]{1,0:T(8,128)(2,1)} %convolution_convert_fusion.2), channel_id=1, source_target_pairs={{0,16},{16,32},{32,48},{48,64},{64,80},{80,96},{96,112},{112,128},... | collective-permute-start | bytes 196616 | tf_op jit(solution)/shard_map/ppermute | solution.py:30
  9.8 20.1 %collective-permute-start.1 = (bf16[128,256]{1,0:T(8,128)(2,1)}, bf16[128,256]{1,0:T(8,128)(2,1)}, u32[]{:S(2)}, u32[]{:S(2)}) collective-permute-start(bf16[128,256]{1,0:T(8,128)(2,1)} %convolution_convert_fusion.2), channel_id=1, source_target_pairs={{16,0},{32,16},{48,32},{64,48},{80,64},{96,80},{112,96},{128,112},... | collective-permute-start | bytes 196616 | tf_op jit(solution)/shard_map/ppermute | solution.py:31
  11.1 19.6 %collective-permute-start.2 = (bf16[128,256]{1,0:T(8,128)(2,1)}, bf16[128,256]{1,0:T(8,128)(2,1)}, u32[]{:S(2)}, u32[]{:S(2)}) collective-permute-start(bf16[128,256]{1,0:T(8,128)(2,1)} %convolution_convert_fusion.2), channel_id=1, source_target_pairs={{0,1},{1,2},{2,3},{3,4},{4,5},{5,6},{6,7},{7,8},{8,9},{9,10},{10,1... | collective-permute-start | bytes 196616 | tf_op jit(solution)/shard_map/ppermute | solution.py:30
  15.3 16.3 %collective-permute-start.3 = (bf16[128,256]{1,0:T(8,128)(2,1)}, bf16[128,256]{1,0:T(8,128)(2,1)}, u32[]{:S(2)}, u32[]{:S(2)}) collective-permute-start(bf16[128,256]{1,0:T(8,128)(2,1)} %convolution_convert_fusion.2), channel_id=1, source_target_pairs={{1,0},{2,1},{3,2},{4,3},{5,4},{6,5},{7,6},{8,7},{9,8},{10,9},{11,1... | collective-permute-start | bytes 196616 | tf_op jit(solution)/shard_map/ppermute | solution.py:31
  34.8 2.5 %copy-start.7 = (bf16[512,256]{1,0:T(8,128)(2,1)S(1)}, bf16[512,256]{1,0:T(8,128)(2,1)}, u32[]{:S(2)}) copy-start(bf16[512,256]{1,0:T(8,128)(2,1)} %param.17) | copy-start | bytes 786436
  37.6 1.0 copy-start.2
  37.6 1.0 copy-start.6
  39.3 12.3 %all-to-all-start = ((f32[16,8,256]{2,1,0:T(8,128)}), f32[16,8,256]{2,1,0:T(8,128)}, u32[]{:S(2)}, u32[]{:S(2)}) async-start(f32[16,8,256]{2,1,0:T(8,128)} %bitcast.14), calls=%async_computation | async-start | bytes 262144 | tf_op jit(solution)/shard_map/all_to_all | solution.py:13
  53.2 12.1 %all-to-all-start.1 = ((f32[16,8,256]{2,1,0:T(8,128)}), f32[16,8,256]{2,1,0:T(8,128)S(1)}, u32[]{:S(2)}, u32[]{:S(2)}) async-start(f32[16,8,256]{2,1,0:T(8,128)} %broadcast_in_dim.41), calls=%async_computation.1 | async-start | bytes 262144 | tf_op jit(solution)/shard_map/all_to_all | solution.py:20
  56.6 9.1 %copy-start.9 = (bf16[256,256]{1,0:T(8,128)(2,1)S(1)}, bf16[256,256]{1,0:T(8,128)(2,1)}, u32[]{:S(2)}) copy-start(bf16[256,256]{1,0:T(8,128)(2,1)} %param.18) | copy-start | bytes 393220
  56.6 10.9 %copy-start.5 = (bf16[1024,256]{1,0:T(8,128)(2,1)S(1)}, bf16[1024,256]{1,0:T(8,128)(2,1)}, u32[]{:S(2)}) copy-start(bf16[1024,256]{1,0:T(8,128)(2,1)} %param.19) | copy-start | bytes 1572868
  67.5 2.2 %copy-start.8 = (bf16[512,256]{1,0:T(8,128)(2,1)S(1)}, bf16[512,256]{1,0:T(8,128)(2,1)}, u32[]{:S(2)}) copy-start(bf16[512,256]{1,0:T(8,128)(2,1)} %param.17) | copy-start | bytes 786436
  67.5 2.2 %copy-start.14 = (bf16[8,128,256]{2,1,0:T(8,128)(2,1)S(1)}, bf16[8,128,256]{2,1,0:T(8,128)(2,1)}, u32[]{:S(2)}) copy-start(bf16[8,128,256]{2,1,0:T(8,128)(2,1)} %fusion.4) | copy-start | bytes 1572868
  71.2 36.6 %copy-start.3 = (f32[1024,256]{1,0:T(8,128)S(1)}, f32[1024,256]{1,0:T(8,128)}, u32[]{:S(2)}) copy-start(f32[1024,256]{1,0:T(8,128)} %copy-done.2) | copy-start | bytes 3145732
  71.2 15.3 %all-to-all-start.2 = ((f32[32,16,128]{2,0,1:T(8,128)}), f32[32,16,128]{2,0,1:T(8,128)S(1)}, u32[]{:S(2)}, u32[]{:S(2)}) async-start(f32[32,16,128]{2,0,1:T(8,128)} %copy.20), calls=%async_computation.2 | async-start | bytes 524288 | tf_op jit(solution)/shard_map/all_to_all | solution.py:13
  87.1 31.5 %all-to-all-start.3 = ((f32[64,1,128]{2,1,0:T(1,128)}), f32[64,1,128]{2,1,0:T(1,128)S(1)}, u32[]{:S(2)}, u32[]{:S(2)}) async-start(f32[64,1,128]{2,1,0:T(1,128)} %bitcast.24), calls=%async_computation.3 | async-start | bytes 65536 | tf_op jit(solution)/shard_map/all_to_all | solution.py:13

commit v8 on v7

--- a/solution.py
+++ b/solution.py
@@ -152,13 +152,9 @@
     halves = feature_count // chunk
     rows_per_step = across_count // halves
     member = lax.axis_index("across")
-    picked_rows = lax.dynamic_index_in_dim(
-        coarse.reshape(coarse_count, -1, rows_per_step), member // halves, 2, keepdims=False
-    )
-    picked_cols = lax.dynamic_index_in_dim(
-        coarse_delta.reshape(coarse_count, halves, chunk), member % halves, 1, keepdims=False
-    )
-    coarse_grad = transposed_times(picked_rows, picked_cols)
+    picked_cols = lax.dynamic_slice_in_dim(coarse_delta, (member % halves) * chunk, chunk, 1)
+    coarse_rows = transposed_times(coarse, picked_cols).reshape(-1, rows_per_step, chunk)
+    coarse_grad = lax.dynamic_index_in_dim(coarse_rows, member // halves, 1, keepdims=False)
     hidden_delta = cotangent.astype(jnp.float32) + jnp.dot(
         assign_float,
         pooled_delta,

time: 120 us -> 119 us (level)
  waiting for transfers between devices: 31.5 us -> 34.7 us
  local copies, waits for them, and re-layouts: 11.5 us -> 9.05 us
  matrix products: 18.4 us -> 16.8 us
    all_to_all x3, waiting for transfers between devices: 25.4 us -> 28.5 us  [scatter_sum(): return lax.all_to_all(pieces, axes, dim, dim, tiled=False).sum(dim)]
    dynamic_slice x2 -> x1, local copies, waits for them, and re-layouts: 1.42 us -> 0.02 us  [local(): lax.dynamic_index_in_dim(coarse_rows, member // halves, 1, keepdims=False)]
  transfers between devices with their start and end apart: 8 -> 8, of which waited for: 4 -> 4; matrix products, arithmetic and copies ran while one was open for 11% -> 8% of each run, Pallas kernels for 0% -> 0%
where the time goes in v8:
time: 119 us; the launch traced here: 118 us
  starting transfers between devices  52.7 us (44%)
  waiting for transfers between devices  34.7 us (29%)
  matrix products  16.8 us (14%)
  local copies, waits for them, and re-layouts  9.05 us (8%)
  other arithmetic  3.64 us (3%)
    all_to_all x3, waiting for transfers between devices, scatter_sum(): return lax.all_to_all(pieces, axes, dim, dim, tiled=False).sum(dim)  28.5 us
    all_to_all x3, starting transfers between devices, scatter_sum(): return lax.all_to_all(pieces, axes, dim, dim, tiled=False).sum(dim)  28.2 us
    ppermute x2, starting transfers between devices, neighbour_tiles(): tiles.append(lax.ppermute(tile, axis, backward))  12.4 us
    ppermute x2, starting transfers between devices, neighbour_tiles(): tiles.append(lax.ppermute(tile, axis, forward))  8.72 us
    all_to_all x1, waiting for transfers between devices, all_sum(): lax.all_to_all(jnp.broadcast_to(mine, (count,) + mine.shape), axis, 0, 0,...  6.11 us
    all_to_all x1, starting transfers between devices, all_sum(): lax.all_to_all(jnp.broadcast_to(mine, (count,) + mine.shape), axis, 0, 0,...  3.41 us
    dot_general x4, matrix products, transposed_times(): lax.dot_general(operand, second, (((0,), (0,)), ((), ())), precision=prec...  2.82 us
    unnamed x34, local copies, waits for them, and re-layouts  2.66 us
  transfers between devices with their start and end apart: 8, of which 4 were waited for; matrix products, arithmetic and copies ran while one was open for 8% of the time, Pallas kernels for 0%

profile of v8, /device:TPU:1, one launch (start us, length us, event | category | flops | bytes accessed | tf_op | source)
XLA Modules:
  0.0 118.0 jit_solution(16303888725352837091)
XLA Ops:
  0.6 0.0 copy-start
  0.7 1.4 %fusion.8 = f32[1024,128]{0,1:T(8,128)S(1)} fusion(bf16[1024,256]{1,0:T(8,128)(2,1)} %param.10), kind=kOutput, calls=%fused_computation.21 | convolution fusion | flops 67239936 | bytes 1048576 | tf_op jit(solution)/shard_map/dot_general | solution.py:37
  2.1 0.2 copy.18
  2.3 0.4 tile.8
  2.7 1.0 fusion.6
  3.6 0.0 copy-start.12
  3.6 0.4 tile.20
  4.0 0.0 copy-start.11
  4.0 0.0 copy-start.13
  4.0 0.3 fusion.9
  4.3 0.0 copy-start.4
  4.3 0.0 copy-start.10
  4.3 0.9 convolution_convert_fusion.2
  5.2 4.6 %collective-permute-start = (bf16[128,256]{1,0:T(8,128)(2,1)}, bf16[128,256]{1,0:T(8,128)(2,1)}, u32[]{:S(2)}, u32[]{:S(2)}) collective-permute-start(bf16[128,256]{1,0:T(8,128)(2,1)} %convolution_convert_fusion.2), channel_id=1, source_target_pairs={{0,16},{16,32},{32,48},{48,64},{64,80},{80,96},{96,112},{112,128},... | collective-permute-start | bytes 196616 | tf_op jit(solution)/shard_map/ppermute | solution.py:30
  9.8 1.3 %collective-permute-start.1 = (bf16[128,256]{1,0:T(8,128)(2,1)}, bf16[128,256]{1,0:T(8,128)(2,1)}, u32[]{:S(2)}, u32[]{:S(2)}) collective-permute-start(bf16[128,256]{1,0:T(8,128)(2,1)} %convolution_convert_fusion.2), channel_id=1, source_target_pairs={{16,0},{32,16},{48,32},{64,48},{80,64},{96,80},{112,96},{128,112},... | collective-permute-start | bytes 196616 | tf_op jit(solution)/shard_map/ppermute | solution.py:31
  11.1 4.2 %collective-permute-start.2 = (bf16[128,256]{1,0:T(8,128)(2,1)}, bf16[128,256]{1,0:T(8,128)(2,1)}, u32[]{:S(2)}, u32[]{:S(2)}) collective-permute-start(bf16[128,256]{1,0:T(8,128)(2,1)} %convolution_convert_fusion.2), channel_id=1, source_target_pairs={{0,1},{1,2},{2,3},{3,4},{4,5},{5,6},{6,7},{7,8},{8,9},{9,10},{10,1... | collective-permute-start | bytes 196616 | tf_op jit(solution)/shard_map/ppermute | solution.py:30
  15.2 11.1 %collective-permute-start.3 = (bf16[128,256]{1,0:T(8,128)(2,1)}, bf16[128,256]{1,0:T(8,128)(2,1)}, u32[]{:S(2)}, u32[]{:S(2)}) collective-permute-start(bf16[128,256]{1,0:T(8,128)(2,1)} %convolution_convert_fusion.2), channel_id=1, source_target_pairs={{1,0},{2,1},{3,2},{4,3},{5,4},{6,5},{7,6},{8,7},{9,8},{10,9},{11,1... | collective-permute-start | bytes 196616 | tf_op jit(solution)/shard_map/ppermute | solution.py:31
  26.5 0.1 copy.19
  26.5 0.1 reshape.114
  26.6 0.1 iota_compare_fusion.5
  26.7 1.2 %fusion.18 = f32[1024,256]{1,0:T(8,128)S(1)} fusion(bf16[1024,256]{1,0:T(8,128)(2,1)S(1)} %fusion.9, bf16[512,256]{1,0:T(8,128)(2,1)} %param.17), kind=kOutput, calls=%fused_computation.41 | convolution fusion | flops 134217728 | bytes 1703936 | tf_op jit(solution)/shard_map/dot_general | solution.py:134
  27.9 1.1 convolution_bitcast_fusion.2
  29.0 0.8 bitcast_dynamic-update-slice_fusion.3
  29.9 0.8 bitcast_dynamic-update-slice_fusion.2
  30.7 0.8 bitcast_dynamic-update-slice_fusion.1
  31.6 0.8 bitcast_dynamic-update-slice_fusion
  32.4 0.4 convolution_convert_fusion
  32.8 2.0 %gather_fusion = bf16[32,128,256]{2,1,0:T(8,128)(2,1)} fusion(bf16[12,128,256]{2,1,0:T(8,128)(2,1)S(1)} %bitcast.92, s32[1024]{0:T(1024)S(1)} %pad_clamp_fusion), kind=kCustom, calls=%fused_computation | custom fusion | bytes 4194432 | tf_op jit(solution)/shard_map/gather | solution.py:125
  34.8 2.5 %fusion.3 = bf16[8,128,256]{2,1,0:T(8,128)(2,1)S(1)} fusion(bf16[8,4,128,256]{3,2,1,0:T(8,128)(2,1)} %bitcast.98, bf16[8,4,128,128]{3,2,1,0:T(8,128)(2,1)} %param.11, pred[8,4]{1,0:T(8,128)(4,1)S(1)} %iota_compare_fusion.5), kind=kOutput, calls=%fused_computation.14 | convolution fusion | flops 269221888 | bytes 3670048 | tf_op jit(solution)/shard_map/bkij,bkjh->bih/dot_general | solution.py:124
  37.2 0.3 convolution_add_fusion.1
  37.6 0.0 copy-start.6
  37.6 1.0 convolution_bitcast_fusion.3
  38.6 0.7 pad_maximum_fusion
  39.2 4.1 %all-to-all-start = ((f32[16,8,256]{2,1,0:T(8,128)}), f32[16,8,256]{2,1,0:T(8,128)}, u32[]{:S(2)}, u32[]{:S(2)}) async-start(f32[16,8,256]{2,1,0:T(8,128)} %bitcast.14), calls=%async_computation | async-start | bytes 262144 | tf_op jit(solution)/shard_map/all_to_all | solution.py:13
  43.3 0.7 gather_fusion.1
  44.0 7.6 %all-to-all-done = f32[16,8,256]{2,1,0:T(8,128)} async-done(((f32[16,8,256]{2,1,0:T(8,128)}), f32[16,8,256]{2,1,0:T(8,128)}, u32[]{:S(2)}, u32[]{:S(2)}) %all-to-all-start) | async-done | bytes 131104 | tf_op jit(solution)/shard_map/all_to_all | solution.py:13
  51.6 0.9 reduce_sum.63
  52.5 0.7 broadcast_in_dim.41
  53.2 3.4 %all-to-all-start.1 = ((f32[16,8,256]{2,1,0:T(8,128)}), f32[16,8,256]{2,1,0:T(8,128)S(1)}, u32[]{:S(2)}, u32[]{:S(2)}) async-start(f32[16,8,256]{2,1,0:T(8,128)} %broadcast_in_dim.41), calls=%async_computation.1 | async-start | bytes 262144 | tf_op jit(solution)/shard_map/all_to_all | solution.py:20
  56.6 0.0 copy-start.9
  56.6 0.0 copy-start.5
  56.6 2.6 %fusion.4 = bf16[8,128,256]{2,1,0:T(8,128)(2,1)} fusion(bf16[8,4,128,256]{3,2,1,0:T(8,128)(2,1)S(1)} %bitcast.97, bf16[8,4,128,128]{3,2,1,0:T(8,128)(2,1)} %param.11, pred[8,4]{1,0:T(8,128)(4,1)S(1)} %iota_compare_fusion.5), kind=kOutput, calls=%fused_computation.15 | convolution fusion | flops 269221888 | bytes 3670048 | tf_op jit(solution)/shard_map/bkij,bkjh->bih/dot_general | solution.py:128
  59.2 6.1 %all-to-all-done.1 = f32[16,8,256]{2,1,0:T(8,128)S(1)} async-done(((f32[16,8,256]{2,1,0:T(8,128)}), f32[16,8,256]{2,1,0:T(8,128)S(1)}, u32[]{:S(2)}, u32[]{:S(2)}) %all-to-all-start.1) | async-done | bytes 131104 | tf_op jit(solution)/shard_map/all_to_all | solution.py:20
  65.3 0.1 slice_reduce_fusion
  65.4 0.1 div.45
  65.5 0.2 multiply_reduce_fusion.1
  65.7 0.1 rsqrt.16
  65.7 0.2 fusion.24
  66.0 0.2 fusion.53
  66.1 0.2 fusion.52
  66.4 0.0 copy-start.8
  66.4 0.0 copy-start.14
  66.4 2.1 %fusion.2 = bf16[1024,256]{1,0:T(8,128)(2,1)S(1)} fusion(f32[1024,256]{1,0:T(8,128)} %copy-done.2, bf16[1024,256]{1,0:T(8,128)(2,1)S(1)} %copy-done.5, s32[1024]{0:T(1024)S(1)} %copy-done.10, f32[64,256]{1,0:T(8,128)S(1)} %fusion.53, f32[16,8,256]{2,1,0:T(8,128)S(1)} %all-to-all-done.1, f32[64]{0:T(128)S(1)} %get-tuple-element.7, ...), kind=kOutput, calls=%fused_computation.13 | convolution fusion | flops 204374016 | bytes 2234368 | tf_op jit(solution)/shard_map/dot_general | solution.py:158
  68.6 0.6 fusion.7
  69.2 0.8 copy.20
  70.0 3.4 %all-to-all-start.2 = ((f32[32,16,128]{2,0,1:T(8,128)}), f32[32,16,128]{2,0,1:T(8,128)S(1)}, u32[]{:S(2)}, u32[]{:S(2)}) async-start(f32[32,16,128]{2,0,1:T(8,128)} %copy.20), calls=%async_computation.2 | async-start | bytes 524288 | tf_op jit(solution)/shard_map/all_to_all | solution.py:13
  73.5 0.1 copy.21
  73.6 0.2 fusion.25
  73.8 11.4 %all-to-all-done.2 = f32[32,16,128]{2,0,1:T(8,128)S(1)} async-done(((f32[32,16,128]{2,0,1:T(8,128)}), f32[32,16,128]{2,0,1:T(8,128)S(1)}, u32[]{:S(2)}, u32[]{:S(2)}) %all-to-all-start.2) | async-done | bytes 262176 | tf_op jit(solution)/shard_map/all_to_all | solution.py:13
  85.2 0.6 pad_maximum_fusion.1
  85.8 20.7 %all-to-all-start.3 = ((f32[64,1,128]{2,1,0:T(1,128)}), f32[64,1,128]{2,1,0:T(1,128)S(1)}, u32[]{:S(2)}, u32[]{:S(2)}) async-start(f32[64,1,128]{2,1,0:T(1,128)} %bitcast.25), calls=%async_computation.3 | async-start | bytes 65536 | tf_op jit(solution)/shard_map/all_to_all | solution.py:13
  106.5 1.3 %fusion.1 = bf16[1024,256]{1,0:T(8,128)(2,1)} fusion(s32[1024]{0:T(1024)S(1)} %copy-done.10, f32[64,256]{1,0:T(8,128)S(1)} %get-tuple-element.6, f32[1024,256]{1,0:T(8,128)S(1)} %copy-done.3, bf16[1024,256]{1,0:T(8,128)(2,1)S(1)} %copy-done.1), kind=kOutput, calls=%fused_computation.12 | convolution fusion | flops 35930112 | bytes 2166784 | tf_op jit(solution)/shard_map/dot_general | solution.py:145
  107.8 9.5 %all-to-all-done.3 = f32[64,1,128]{2,1,0:T(1,128)S(1)} async-done(((f32[64,1,128]{2,1,0:T(1,128)}), f32[64,1,128]{2,1,0:T(1,128)S(1)}, u32[]{:S(2)}, u32[]{:S(2)}) %all-to-all-start.3) | async-done | bytes 32800 | tf_op jit(solution)/shard_map/all_to_all | solution.py:13
  117.4 0.6 reduce_sum.69
  (32 shorter events, 0.2 us)
Async XLA Ops:
  0.6 31.8 %copy-start = (bf16[256,256]{1,0:T(8,128)(2,1)S(1)}, bf16[256,256]{1,0:T(8,128)(2,1)}, u32[]{:S(2)}) copy-start(bf16[256,256]{1,0:T(8,128)(2,1)} %param.16) | copy-start | bytes 393220
  0.6 2.0 %copy-start.1 = (bf16[1024,256]{1,0:T(8,128)(2,1)S(1)}, bf16[1024,256]{1,0:T(8,128)(2,1)}, u32[]{:S(2)}) copy-start(bf16[1024,256]{1,0:T(8,128)(2,1)} %param.10) | copy-start | bytes 1572868
  3.6 0.7 copy-start.12
  4.0 22.4 %copy-start.11 = (s32[8,4]{0,1:T(4,128)S(1)}, s32[8,4]{0,1:T(4,128)}, u32[]{:S(2)}) copy-start(s32[8,4]{0,1:T(4,128)} %param.12) | copy-start | bytes 388
  4.0 22.6 %copy-start.13 = (s32[8]{0:T(128)S(1)}, s32[8]{0:T(128)}, u32[]{:S(2)}) copy-start(s32[8]{0:T(128)} %param.13) | copy-start | bytes 100
  4.3 23.6 %copy-start.4 = (bf16[1024,256]{1,0:T(8,128)(2,1)S(1)}, bf16[1024,256]{1,0:T(8,128)(2,1)}, u32[]{:S(2)}) copy-start(bf16[1024,256]{1,0:T(8,128)(2,1)} %param.19) | copy-start | bytes 1572868
  4.3 23.6 %copy-start.10 = (s32[1024]{0:T(1024)S(1)}, s32[1024]{0:T(1024)}, u32[]{:S(2)}) copy-start(s32[1024]{0:T(1024)} %param.15) | copy-start | bytes 12292
  5.2 23.8 %collective-permute-start = (bf16[128,256]{1,0:T(8,128)(2,1)}, bf16[128,256]{1,0:T(8,128)(2,1)}, u32[]{:S(2)}, u32[]{:S(2)}) collective-permute-start(bf16[128,256]{1,0:T(8,128)(2,1)} %convolution_convert_fusion.2), channel_id=1, source_target_pairs={{0,16},{16,32},{32,48},{48,64},{64,80},{80,96},{96,112},{112,128},... | collective-permute-start | bytes 196616 | tf_op jit(solution)/shard_map/ppermute | solution.py:30
  9.8 20.1 %collective-permute-start.1 = (bf16[128,256]{1,0:T(8,128)(2,1)}, bf16[128,256]{1,0:T(8,128)(2,1)}, u32[]{:S(2)}, u32[]{:S(2)}) collective-permute-start(bf16[128,256]{1,0:T(8,128)(2,1)} %convolution_convert_fusion.2), channel_id=1, source_target_pairs={{16,0},{32,16},{48,32},{64,48},{80,64},{96,80},{112,96},{128,112},... | collective-permute-start | bytes 196616 | tf_op jit(solution)/shard_map/ppermute | solution.py:31
  11.1 19.6 %collective-permute-start.2 = (bf16[128,256]{1,0:T(8,128)(2,1)}, bf16[128,256]{1,0:T(8,128)(2,1)}, u32[]{:S(2)}, u32[]{:S(2)}) collective-permute-start(bf16[128,256]{1,0:T(8,128)(2,1)} %convolution_convert_fusion.2), channel_id=1, source_target_pairs={{0,1},{1,2},{2,3},{3,4},{4,5},{5,6},{6,7},{7,8},{8,9},{9,10},{10,1... | collective-permute-start | bytes 196616 | tf_op jit(solution)/shard_map/ppermute | solution.py:30
  15.2 16.3 %collective-permute-start.3 = (bf16[128,256]{1,0:T(8,128)(2,1)}, bf16[128,256]{1,0:T(8,128)(2,1)}, u32[]{:S(2)}, u32[]{:S(2)}) collective-permute-start(bf16[128,256]{1,0:T(8,128)(2,1)} %convolution_convert_fusion.2), channel_id=1, source_target_pairs={{1,0},{2,1},{3,2},{4,3},{5,4},{6,5},{7,6},{8,7},{9,8},{10,9},{11,1... | collective-permute-start | bytes 196616 | tf_op jit(solution)/shard_map/ppermute | solution.py:31
  34.8 2.5 %copy-start.7 = (bf16[512,256]{1,0:T(8,128)(2,1)S(1)}, bf16[512,256]{1,0:T(8,128)(2,1)}, u32[]{:S(2)}) copy-start(bf16[512,256]{1,0:T(8,128)(2,1)} %param.17) | copy-start | bytes 786436
  37.6 1.0 copy-start.2
  37.6 1.0 copy-start.6
  39.2 12.3 %all-to-all-start = ((f32[16,8,256]{2,1,0:T(8,128)}), f32[16,8,256]{2,1,0:T(8,128)}, u32[]{:S(2)}, u32[]{:S(2)}) async-start(f32[16,8,256]{2,1,0:T(8,128)} %bitcast.14), calls=%async_computation | async-start | bytes 262144 | tf_op jit(solution)/shard_map/all_to_all | solution.py:13
  53.2 12.1 %all-to-all-start.1 = ((f32[16,8,256]{2,1,0:T(8,128)}), f32[16,8,256]{2,1,0:T(8,128)S(1)}, u32[]{:S(2)}, u32[]{:S(2)}) async-start(f32[16,8,256]{2,1,0:T(8,128)} %broadcast_in_dim.41), calls=%async_computation.1 | async-start | bytes 262144 | tf_op jit(solution)/shard_map/all_to_all | solution.py:20
  56.6 9.1 %copy-start.9 = (bf16[256,256]{1,0:T(8,128)(2,1)S(1)}, bf16[256,256]{1,0:T(8,128)(2,1)}, u32[]{:S(2)}) copy-start(bf16[256,256]{1,0:T(8,128)(2,1)} %param.18) | copy-start | bytes 393220
  56.6 9.8 %copy-start.5 = (bf16[1024,256]{1,0:T(8,128)(2,1)S(1)}, bf16[1024,256]{1,0:T(8,128)(2,1)}, u32[]{:S(2)}) copy-start(bf16[1024,256]{1,0:T(8,128)(2,1)} %param.19) | copy-start | bytes 1572868
  66.4 2.2 %copy-start.8 = (bf16[512,256]{1,0:T(8,128)(2,1)S(1)}, bf16[512,256]{1,0:T(8,128)(2,1)}, u32[]{:S(2)}) copy-start(bf16[512,256]{1,0:T(8,128)(2,1)} %param.17) | copy-start | bytes 786436
  66.4 2.2 %copy-start.14 = (bf16[8,128,256]{2,1,0:T(8,128)(2,1)S(1)}, bf16[8,128,256]{2,1,0:T(8,128)(2,1)}, u32[]{:S(2)}) copy-start(bf16[8,128,256]{2,1,0:T(8,128)(2,1)} %fusion.4) | copy-start | bytes 1572868
  68.6 38.0 %copy-start.3 = (f32[1024,256]{1,0:T(8,128)S(1)}, f32[1024,256]{1,0:T(8,128)}, u32[]{:S(2)}) copy-start(f32[1024,256]{1,0:T(8,128)} %copy-done.2) | copy-start | bytes 3145732
  70.0 15.2 %all-to-all-start.2 = ((f32[32,16,128]{2,0,1:T(8,128)}), f32[32,16,128]{2,0,1:T(8,128)S(1)}, u32[]{:S(2)}, u32[]{:S(2)}) async-start(f32[32,16,128]{2,0,1:T(8,128)} %copy.20), calls=%async_computation.2 | async-start | bytes 524288 | tf_op jit(solution)/shard_map/all_to_all | solution.py:13
  85.8 31.5 %all-to-all-start.3 = ((f32[64,1,128]{2,1,0:T(1,128)}), f32[64,1,128]{2,1,0:T(1,128)S(1)}, u32[]{:S(2)}, u32[]{:S(2)}) async-start(f32[64,1,128]{2,1,0:T(1,128)} %bitcast.25), calls=%async_computation.3 | async-start | bytes 65536 | tf_op jit(solution)/shard_map/all_to_all | solution.py:13

commit v9 on v8

--- a/solution.py
+++ b/solution.py
@@ -115,20 +115,18 @@
     sources = jnp.concatenate(
         [scaled.reshape(blocks, tile_rows, feature_count), halo_tiles], axis=0
     )
-    messages = jnp.dot(
-        sources.reshape(-1, feature_count), w_msg, preferred_element_type=jnp.float32
-    )
-    messages = messages.astype(jnp.bfloat16).reshape(sources.shape)
     live_slots = jnp.arange(slot_count)[None, :] < adj_count[:, None]
     masked_tiles = jnp.where(live_slots[:, :, None, None], adj_tiles, jnp.zeros((), jnp.bfloat16))
-    aggregated = jnp.einsum(
-        "bkij,bkjh->bih", masked_tiles, messages[adj_index], preferred_element_type=jnp.float32
-    )
-    aggregated = aggregated.astype(jnp.bfloat16).reshape(-1, feature_count)
-    summed_scaled = jnp.einsum(
+    summed = jnp.einsum(
         "bkij,bkjh->bih", masked_tiles, sources[adj_index], preferred_element_type=jnp.float32
-    )
-    summed_scaled = summed_scaled.astype(jnp.bfloat16).reshape(-1, feature_count)
+    ).reshape(-1, feature_count)
+    summed_high = lax.reduce_precision(summed, exponent_bits=8, mantissa_bits=7)
+    summed_scaled = summed_high.astype(jnp.bfloat16)
+    summed_low = (summed - summed_high).astype(jnp.bfloat16)
+    aggregated = (
+        jnp.dot(summed_scaled, w_msg, preferred_element_type=jnp.float32)
+        + jnp.dot(summed_low, w_msg, preferred_element_type=jnp.float32)
+    ).astype(jnp.bfloat16)
     w_first = w_update[:feature_count]
     w_second = w_update[feature_count:]
     update_pre = jnp.dot(scaled, w_first, preferred_element_type=jnp.float32) + jnp.dot(

time: 119 us -> 113 us (0.950)
  blocking collectives: 0 us -> 22.7 us
  waiting for transfers between devices: 34.7 us -> 20.4 us
  starting transfers between devices: 52.7 us -> 46.6 us
  local copies, waits for them, and re-layouts: 9.05 us -> 3.98 us
  other arithmetic: 3.64 us -> 2.22 us
    all_to_all x0 -> x2, blocking collectives: none -> 22.7 us  [the longest x1 11.8 us: all_sum(): lax.all_to_all(jnp.broadcast_to(mine, (count,) + mine.shape), axis, 0, 0,...]
    all_to_all x3 -> x2, waiting for transfers between devices: 28.5 us -> 20.4 us  [scatter_sum(): return lax.all_to_all(pieces, axes, dim, dim, tiled=False).sum(dim)]
    all_to_all x1 -> x0, waiting for transfers between devices: 6.11 us -> none  [all_sum(): lax.all_to_all(jnp.broadcast_to(mine, (count,) + mine.shape), axis, 0, 0,...]
    all_to_all x1 -> x0, starting transfers between devices: 3.41 us -> none  [all_sum(): lax.all_to_all(jnp.broadcast_to(mine, (count,) + mine.shape), axis, 0, 0,...]
    dot_general x2 -> x1, matrix products: 2.82 us -> 0.29 us  [local(): jnp.dot(summed_scaled, w_msg, preferred_element_type=jnp.float32)]
    dot_general x4, matrix products: 2.82 us -> 5.11 us  [transposed_times(): lax.dot_general(operand, second, (((0,), (0,)), ((), ())), precision=prec...]
    gather x1 -> x0, local copies, waits for them, and re-layouts: 2.02 us -> none  [local(): messages[adj_index]]
    unnamed x34 -> x36, local copies, waits for them, and re-layouts: 2.66 us -> 1.11 us
  transfers between devices with their start and end apart: 8 -> 6, of which waited for: 4 -> 2; matrix products, arithmetic and copies ran while one was open for 8% -> 4% of each run, Pallas kernels for 0% -> 0%
where the time goes in v9:
time: 113 us
  starting transfers between devices  46.6 us (41%)
  blocking collectives  22.7 us (20%)
  waiting for transfers between devices  20.4 us (18%)
  matrix products  15.8 us (14%)
  local copies, waits for them, and re-layouts  3.98 us (4%)
  other arithmetic  2.22 us (2%)
    all_to_all x2, starting transfers between devices, scatter_sum(): return lax.all_to_all(pieces, axes, dim, dim, tiled=False).sum(dim)  26.7 us
    all_to_all x2, waiting for transfers between devices, scatter_sum(): return lax.all_to_all(pieces, axes, dim, dim, tiled=False).sum(dim)  20.4 us
    all_to_all x1, blocking collectives, all_sum(): lax.all_to_all(jnp.broadcast_to(mine, (count,) + mine.shape), axis, 0, 0,...  11.8 us
    ppermute x2, starting transfers between devices, neighbour_tiles(): tiles.append(lax.ppermute(tile, axis, backward))  11.8 us
    all_to_all x1, blocking collectives, scatter_sum(): return lax.all_to_all(pieces, axes, dim, dim, tiled=False).sum(dim)  10.9 us
    ppermute x2, starting transfers between devices, neighbour_tiles(): tiles.append(lax.ppermute(tile, axis, forward))  8.1 us
    dot_general x4, matrix products, transposed_times(): lax.dot_general(operand, second, (((0,), (0,)), ((), ())), precision=prec...  5.11 us
    dot_general x2, matrix products, row_sums(): jnp.dot(values, ones, precision=precision, preferred_element_type=jnp.flo...  2.38 us
  transfers between devices with their start and end apart: 6, of which 2 were waited for; matrix products, arithmetic and copies ran while one was open for 4% of the time, Pallas kernels for 0%

profile of v9, /device:TPU:1, one launch (start us, length us, event | category | flops | bytes accessed | tf_op | source)
XLA Modules:
  0.0 112.9 jit_solution(4555041523589918604)
XLA Ops:
  0.6 0.0 copy-start
  0.7 1.4 %fusion.7 = f32[1024,128]{0,1:T(8,128)S(1)} fusion(bf16[1024,256]{1,0:T(8,128)(2,1)} %param.10), kind=kOutput, calls=%fused_computation.19 | convolution fusion | flops 67239936 | bytes 1048576 | tf_op jit(solution)/shard_map/dot_general | solution.py:37
  2.1 0.2 copy.18
  2.3 0.4 tile.8
  2.7 1.0 fusion.5
  3.6 0.0 copy-start.14
  3.6 0.4 tile.20
  4.0 0.0 copy-start.13
  4.0 0.0 copy-start.15
  4.0 0.0 copy-start.9
  4.0 0.3 fusion.9
  4.3 0.0 copy-start.6
  4.3 0.0 copy-start.12
  4.3 0.3 convolution_convert_fusion.1
  4.6 3.9 %collective-permute-start = (bf16[128,256]{1,0:T(8,128)(2,1)S(1)}, bf16[128,256]{1,0:T(8,128)(2,1)S(1)}, u32[]{:S(2)}, u32[]{:S(2)}) collective-permute-start(bf16[128,256]{1,0:T(8,128)(2,1)S(1)} %convolution_convert_fusion.1), channel_id=1, source_target_pairs={{0,16},{16,32},{32,48},{48,64},{64,80},{80,96},{96,112},{112,128},... | collective-permute-start | bytes 196616 | tf_op jit(solution)/shard_map/ppermute | solution.py:30
  8.6 1.3 %collective-permute-start.1 = (bf16[128,256]{1,0:T(8,128)(2,1)S(1)}, bf16[128,256]{1,0:T(8,128)(2,1)S(1)}, u32[]{:S(2)}, u32[]{:S(2)}) collective-permute-start(bf16[128,256]{1,0:T(8,128)(2,1)S(1)} %convolution_convert_fusion.1), channel_id=1, source_target_pairs={{16,0},{32,16},{48,32},{64,48},{80,64},{96,80},{112,96},{128,112},... | collective-permute-start | bytes 196616 | tf_op jit(solution)/shard_map/ppermute | solution.py:31
  9.9 4.2 %collective-permute-start.2 = (bf16[128,256]{1,0:T(8,128)(2,1)S(1)}, bf16[128,256]{1,0:T(8,128)(2,1)S(1)}, u32[]{:S(2)}, u32[]{:S(2)}) collective-permute-start(bf16[128,256]{1,0:T(8,128)(2,1)S(1)} %convolution_convert_fusion.1), channel_id=1, source_target_pairs={{0,1},{1,2},{2,3},{3,4},{4,5},{5,6},{6,7},{7,8},{8,9},{9,10},{10,1... | collective-permute-start | bytes 196616 | tf_op jit(solution)/shard_map/ppermute | solution.py:30
  14.0 10.5 %collective-permute-start.3 = (bf16[128,256]{1,0:T(8,128)(2,1)S(1)}, bf16[128,256]{1,0:T(8,128)(2,1)S(1)}, u32[]{:S(2)}, u32[]{:S(2)}) collective-permute-start(bf16[128,256]{1,0:T(8,128)(2,1)S(1)} %convolution_convert_fusion.1), channel_id=1, source_target_pairs={{1,0},{2,1},{3,2},{4,3},{5,4},{6,5},{7,6},{8,7},{9,8},{10,9},{11,1... | collective-permute-start | bytes 196616 | tf_op jit(solution)/shard_map/ppermute | solution.py:31
  24.7 0.1 copy.19
  24.7 0.1 reshape.102
  24.8 0.1 iota_compare_fusion.5
  24.9 0.0 copy-done.9
  24.9 1.3 %fusion.20 = f32[1024,256]{1,0:T(8,128)} fusion(bf16[1024,256]{1,0:T(8,128)(2,1)S(1)} %fusion.9, bf16[512,256]{1,0:T(8,128)(2,1)S(1)} %copy-done.9), kind=kOutput, calls=%fused_computation.41 | convolution fusion | flops 134217728 | bytes 1703936 | tf_op jit(solution)/shard_map/dot_general | solution.py:132
  26.2 0.0 copy-done.12
  26.2 1.1 convolution_bitcast_fusion
  27.2 0.0 collective-permute-done
  27.3 0.0 collective-permute-done.1
  27.3 0.0 collective-permute-done.2
  27.3 0.0 collective-permute-done.3
  27.3 0.7 gather_fusion
  28.0 1.7 %fusion.10 = f32[8,128,256,1]{2,1,3,0:T(8,128)S(1)} fusion(bf16[8,4,128,256]{3,2,1,0:T(8,128)(2,1)S(1)} %bitcast.84, bf16[8,4,128,128]{3,2,1,0:T(8,128)(2,1)} %param.11, pred[8,4]{1,0:T(8,128)(4,1)S(1)} %iota_compare_fusion.5), kind=kOutput, calls=%fused_computation.27 | convolution fusion | flops 268959744 | bytes 4194336 | tf_op jit(solution)/shard_map/bkij,bkjh->bih/dot_general | solution.py:120
  29.8 0.0 copy-start.10
  29.8 0.2 fusion.8
  29.9 0.0 copy-start.3
  29.9 0.8 copy-done.3
  30.7 0.3 fusion.54
  31.0 0.1 copy-done.2
  31.2 0.0 copy-done.10
  31.2 1.5 %convolution_add_fusion.1 = f32[1024,256]{1,0:T(8,128)} fusion(f32[1024,256]{1,0:T(8,128)S(1)} %copy-done.2, f32[1024,256]{1,0:T(8,128)S(1)} %fusion.54, bf16[1024,256]{1,0:T(8,128)(2,1)S(1)} %get-tuple-element.4, bf16[256,256]{1,0:T(8,128)(2,1)S(1)} %copy-done, bf16[512,256]{1,0:T(8,128)(2,1)S(1)} %copy-done.10), kind=kOutput, calls=%fused_computation.4 | convolution fusion | flops 269221888 | bytes 3932160 | tf_op jit(solution)/shard_map/dot_general | solution.py:132
  32.7 2.2 %convolution_bitcast_fusion.1 = f32[1,64,256]{2,1,0:T(8,128)S(1)} fusion(s32[1024]{0:T(1024)S(1)} %copy-done.12, bf16[1024,256]{1,0:T(8,128)(2,1)S(1)} %copy-done.1, f32[1024,256]{1,0:T(8,128)} %convolution_add_fusion.1), kind=kOutput, calls=%fused_computation.22 | convolution fusion | flops 202964992 | bytes 1642496 | tf_op jit(solution)/shard_map/dot_general | solution.py:62
  35.0 0.0 copy-start.7
  35.0 10.9 %all_to_all.24 = f32[16,8,256]{2,1,0:T(8,128)S(1)} all-to-all(f32[16,8,256]{2,1,0:T(8,128)S(1)} %bitcast.87), channel_id=1, replica_groups=mesh['along'=64,'across'=16] {'across'}, dimensions={0} | all-to-all | bytes 262144 | tf_op jit(solution)/shard_map/all_to_all | solution.py:13
  45.9 11.8 %all_to_all.25 = f32[16,8,256]{2,1,0:T(8,128)S(1)} all-to-all(f32[16,8,256]{2,1,0:T(8,128)S(1)} %broadcast_in_dim.40), channel_id=1, replica_groups=mesh['along'=64,'across'=16] {'across'}, dimensions={0} | all-to-all | bytes 262144 | tf_op jit(solution)/shard_map/all_to_all | solution.py:20
  57.8 0.1 slice_reduce_fusion
  57.8 0.1 div.45
  57.9 0.2 multiply_reduce_fusion.1
  58.1 0.1 rsqrt.16
  58.2 0.2 fusion.26
  58.4 0.2 fusion.55
  58.6 0.2 fusion.53
  58.8 0.0 copy-done.5
  58.8 0.0 copy-start.4
  58.8 1.6 %fusion.2 = bf16[1024,256]{1,0:T(8,128)(2,1)} fusion(f32[1024,256]{1,0:T(8,128)S(1)} %copy-done.5, bf16[1024,256]{1,0:T(8,128)(2,1)S(1)} %copy-done.7, s32[1024]{0:T(1024)S(1)} %copy-done.12, f32[64,256]{1,0:T(8,128)S(1)} %fusion.55, f32[16,8,256]{2,1,0:T(8,128)S(1)} %all_to_all.25, f32[64]{0:T(128)S(1)} %get-tuple-element.9, f32[64]{0:T(128)S(1)} %get-tuple-element.10, ...), kind=kOutput, calls=%fused_computation.12 | convolution fusion | flops 204374016 | bytes 2234368 | tf_op jit(solution)/shard_map/dot_general | solution.py:156
  60.5 1.7 %fusion.6 = f32[256,256]{1,0:T(8,128)S(1)} fusion(bf16[1024,256]{1,0:T(8,128)(2,1)S(1)} %copy-done.4, bf16[1024,256]{1,0:T(8,128)(2,1)} %fusion.2, bf16[512,256]{1,0:T(8,128)(2,1)S(1)} %copy-done.10), kind=kOutput, calls=%fused_computation.17 | convolution fusion | flops 268697600 | bytes 1441792 | tf_op jit(solution)/shard_map/dot_general | solution.py:62
  62.2 0.8 copy.20
  63.0 3.4 %all-to-all-start.2 = ((f32[32,16,128]{2,0,1:T(8,128)}), f32[32,16,128]{2,0,1:T(8,128)S(1)}, u32[]{:S(2)}, u32[]{:S(2)}) async-start(f32[32,16,128]{2,0,1:T(8,128)} %copy.20), calls=%async_computation.2 | async-start | bytes 524288 | tf_op jit(solution)/shard_map/all_to_all | solution.py:13
  66.4 0.1 copy.21
  66.5 0.2 fusion.27
  66.7 10.9 %all-to-all-done.2 = f32[32,16,128]{2,0,1:T(8,128)S(1)} async-done(((f32[32,16,128]{2,0,1:T(8,128)}), f32[32,16,128]{2,0,1:T(8,128)S(1)}, u32[]{:S(2)}, u32[]{:S(2)}) %all-to-all-start.2) | async-done | bytes 262176 | tf_op jit(solution)/shard_map/all_to_all | solution.py:13
  77.6 0.6 pad_maximum_fusion.1
  78.2 23.3 %all-to-all-start.3 = ((f32[64,1,128]{2,1,0:T(1,128)}), f32[64,1,128]{2,1,0:T(1,128)S(1)}, u32[]{:S(2)}, u32[]{:S(2)}) async-start(f32[64,1,128]{2,1,0:T(1,128)} %bitcast.20), calls=%async_computation.3 | async-start | bytes 65536 | tf_op jit(solution)/shard_map/all_to_all | solution.py:13
  101.5 1.3 %fusion.1 = bf16[1024,256]{1,0:T(8,128)(2,1)} fusion(s32[1024]{0:T(1024)S(1)} %copy-done.12, f32[64,256]{1,0:T(8,128)S(1)} %get-tuple-element.8, f32[1024,256]{1,0:T(8,128)S(1)} %copy-done.5, bf16[1024,256]{1,0:T(8,128)(2,1)S(1)} %copy-done.1), kind=kOutput, calls=%fused_computation.11 | convolution fusion | flops 35930112 | bytes 2166784 | tf_op jit(solution)/shard_map/dot_general | solution.py:143
  102.7 9.6 %all-to-all-done.3 = f32[64,1,128]{2,1,0:T(1,128)S(1)} async-done(((f32[64,1,128]{2,1,0:T(1,128)}), f32[64,1,128]{2,1,0:T(1,128)S(1)}, u32[]{:S(2)}, u32[]{:S(2)}) %all-to-all-start.3) | async-done | bytes 32800 | tf_op jit(solution)/shard_map/all_to_all | solution.py:13
  112.3 0.6 reduce_sum.69
  (31 shorter events, 0.2 us)
Async XLA Ops:
  0.6 30.1 %copy-start = (bf16[256,256]{1,0:T(8,128)(2,1)S(1)}, bf16[256,256]{1,0:T(8,128)(2,1)}, u32[]{:S(2)}) copy-start(bf16[256,256]{1,0:T(8,128)(2,1)} %param.16) | copy-start | bytes 393220
  0.6 2.0 %copy-start.1 = (bf16[1024,256]{1,0:T(8,128)(2,1)S(1)}, bf16[1024,256]{1,0:T(8,128)(2,1)}, u32[]{:S(2)}) copy-start(bf16[1024,256]{1,0:T(8,128)(2,1)} %param.10) | copy-start | bytes 1572868
  3.6 0.7 copy-start.14
  4.0 20.6 %copy-start.13 = (s32[8,4]{0,1:T(4,128)S(1)}, s32[8,4]{0,1:T(4,128)}, u32[]{:S(2)}) copy-start(s32[8,4]{0,1:T(4,128)} %param.12) | copy-start | bytes 388
  4.0 20.8 %copy-start.15 = (s32[8]{0:T(128)S(1)}, s32[8]{0:T(128)}, u32[]{:S(2)}) copy-start(s32[8]{0:T(128)} %param.13) | copy-start | bytes 100
  4.0 20.9 %copy-start.9 = (bf16[512,256]{1,0:T(8,128)(2,1)S(1)}, bf16[512,256]{1,0:T(8,128)(2,1)}, u32[]{:S(2)}) copy-start(bf16[512,256]{1,0:T(8,128)(2,1)} %param.17) | copy-start | bytes 786436
  4.3 21.9 %copy-start.6 = (bf16[1024,256]{1,0:T(8,128)(2,1)S(1)}, bf16[1024,256]{1,0:T(8,128)(2,1)}, u32[]{:S(2)}) copy-start(bf16[1024,256]{1,0:T(8,128)(2,1)} %param.19) | copy-start | bytes 1572868
  4.3 21.8 %copy-start.12 = (s32[1024]{0:T(1024)S(1)}, s32[1024]{0:T(1024)}, u32[]{:S(2)}) copy-start(s32[1024]{0:T(1024)} %param.15) | copy-start | bytes 12292
  4.6 22.6 %collective-permute-start = (bf16[128,256]{1,0:T(8,128)(2,1)S(1)}, bf16[128,256]{1,0:T(8,128)(2,1)S(1)}, u32[]{:S(2)}, u32[]{:S(2)}) collective-permute-start(bf16[128,256]{1,0:T(8,128)(2,1)S(1)} %convolution_convert_fusion.1), channel_id=1, source_target_pairs={{0,16},{16,32},{32,48},{48,64},{64,80},{80,96},{96,112},{112,128},... | collective-permute-start | bytes 196616 | tf_op jit(solution)/shard_map/ppermute | solution.py:30
  8.6 18.7 %collective-permute-start.1 = (bf16[128,256]{1,0:T(8,128)(2,1)S(1)}, bf16[128,256]{1,0:T(8,128)(2,1)S(1)}, u32[]{:S(2)}, u32[]{:S(2)}) collective-permute-start(bf16[128,256]{1,0:T(8,128)(2,1)S(1)} %convolution_convert_fusion.1), channel_id=1, source_target_pairs={{16,0},{32,16},{48,32},{64,48},{80,64},{96,80},{112,96},{128,112},... | collective-permute-start | bytes 196616 | tf_op jit(solution)/shard_map/ppermute | solution.py:31
  9.9 17.4 %collective-permute-start.2 = (bf16[128,256]{1,0:T(8,128)(2,1)S(1)}, bf16[128,256]{1,0:T(8,128)(2,1)S(1)}, u32[]{:S(2)}, u32[]{:S(2)}) collective-permute-start(bf16[128,256]{1,0:T(8,128)(2,1)S(1)} %convolution_convert_fusion.1), channel_id=1, source_target_pairs={{0,1},{1,2},{2,3},{3,4},{4,5},{5,6},{6,7},{7,8},{8,9},{9,10},{10,1... | collective-permute-start | bytes 196616 | tf_op jit(solution)/shard_map/ppermute | solution.py:30
  14.0 13.3 %collective-permute-start.3 = (bf16[128,256]{1,0:T(8,128)(2,1)S(1)}, bf16[128,256]{1,0:T(8,128)(2,1)S(1)}, u32[]{:S(2)}, u32[]{:S(2)}) collective-permute-start(bf16[128,256]{1,0:T(8,128)(2,1)S(1)} %convolution_convert_fusion.1), channel_id=1, source_target_pairs={{1,0},{2,1},{3,2},{4,3},{5,4},{6,5},{7,6},{8,7},{9,8},{10,9},{11,1... | collective-permute-start | bytes 196616 | tf_op jit(solution)/shard_map/ppermute | solution.py:31
  29.7 1.4 %copy-start.2 = (f32[1024,256]{1,0:T(8,128)S(1)}, f32[1024,256]{1,0:T(8,128)}, u32[]{:S(2)}) copy-start(f32[1024,256]{1,0:T(8,128)} %fusion.20) | copy-start | bytes 3145732
  29.8 1.4 %copy-start.10 = (bf16[512,256]{1,0:T(8,128)(2,1)S(1)}, bf16[512,256]{1,0:T(8,128)(2,1)}, u32[]{:S(2)}) copy-start(bf16[512,256]{1,0:T(8,128)(2,1)} %param.17) | copy-start | bytes 786436
  29.9 0.8 copy-start.3
  32.7 2.2 %copy-start.8 = (f32[1,64,256]{2,1,0:T(8,128)S(1)}, f32[1,64,256]{2,1,0:T(8,128)}, u32[]{:S(2)}) copy-start(f32[1,64,256]{2,1,0:T(8,128)} %convolution_bitcast_fusion) | copy-start | bytes 196612
  32.7 25.5 %copy-start.11 = (bf16[256,256]{1,0:T(8,128)(2,1)S(1)}, bf16[256,256]{1,0:T(8,128)(2,1)}, u32[]{:S(2)}) copy-start(bf16[256,256]{1,0:T(8,128)(2,1)} %param.18) | copy-start | bytes 393220
  35.0 23.8 %copy-start.5 = (f32[1024,256]{1,0:T(8,128)S(1)}, f32[1024,256]{1,0:T(8,128)}, u32[]{:S(2)}) copy-start(f32[1024,256]{1,0:T(8,128)} %convolution_add_fusion.1) | copy-start | bytes 3145732
  35.0 23.8 %copy-start.7 = (bf16[1024,256]{1,0:T(8,128)(2,1)S(1)}, bf16[1024,256]{1,0:T(8,128)(2,1)}, u32[]{:S(2)}) copy-start(bf16[1024,256]{1,0:T(8,128)(2,1)} %param.19) | copy-start | bytes 1572868
  58.8 1.7 %copy-start.4 = (bf16[1024,256]{1,0:T(8,128)(2,1)S(1)}, bf16[1024,256]{1,0:T(8,128)(2,1)}, u32[]{:S(2)}) copy-start(bf16[1024,256]{1,0:T(8,128)(2,1)} %copy-done.3) | copy-start | bytes 1572868
  63.0 14.6 %all-to-all-start.2 = ((f32[32,16,128]{2,0,1:T(8,128)}), f32[32,16,128]{2,0,1:T(8,128)S(1)}, u32[]{:S(2)}, u32[]{:S(2)}) async-start(f32[32,16,128]{2,0,1:T(8,128)} %copy.20), calls=%async_computation.2 | async-start | bytes 524288 | tf_op jit(solution)/shard_map/all_to_all | solution.py:13
  78.2 34.1 %all-to-all-start.3 = ((f32[64,1,128]{2,1,0:T(1,128)}), f32[64,1,128]{2,1,0:T(1,128)S(1)}, u32[]{:S(2)}, u32[]{:S(2)}) async-start(f32[64,1,128]{2,1,0:T(1,128)} %bitcast.20), calls=%async_computation.3 | async-start | bytes 65536 | tf_op jit(solution)/shard_map/all_to_all | solution.py:13

commit v10 on v9

--- a/solution.py
+++ b/solution.py
@@ -42,7 +42,7 @@
     repeat = width // 128
     mean = row_sums(features) / width
     center = features.astype(jnp.float32) - jnp.tile(mean, (1, repeat))
-    variance = row_sums(center * center, lax.Precision.HIGHEST) / width
+    variance = row_sums(center * center, lax.Precision.HIGH) / width
     inverse = lax.rsqrt(variance + eps)
     return center * jnp.tile(inverse, (1, repeat))
 
@@ -136,7 +136,7 @@
     coarse_count = NC_DEV * lax.axis_size("across")
     assign_float = (pool_index[:, None] == jnp.arange(coarse_count)[None, :]).astype(jnp.float32)
     assign_bits = assign_float.astype(jnp.bfloat16)
-    pooled_part = transposed_times(assign_float, hidden_one, lax.Precision.HIGHEST)
+    pooled_part = transposed_times(assign_float, hidden_one, lax.Precision.HIGH)
     cot_part = transposed_times(assign_bits, cotangent)
     pooled, coarse_cot = all_sum(jnp.stack([pooled_part, cot_part]), "across")
     coarse_norm, inverse, coarse, coarse_pre, coarse_out = coarse_forward(pooled, w_coarse)
@@ -156,7 +156,7 @@
     hidden_delta = cotangent.astype(jnp.float32) + jnp.dot(
         assign_float,
         pooled_delta,
-        precision=lax.Precision.HIGHEST,
+        precision=lax.Precision.HIGH,
         preferred_element_type=jnp.float32,
     )
     update_delta = (hidden_delta * silu_slope(update_pre)).astype(jnp.bfloat16)

time: 113 us -> 113 us (level)
  no operation moved by 1% of the time
where the time goes in v10:
time: 113 us; the launch traced here: 112 us
  starting transfers between devices  46.6 us (41%)
  blocking collectives  22.7 us (20%)
  waiting for transfers between devices  20.4 us (18%)
  matrix products  15.1 us (13%)
  local copies, waits for them, and re-layouts  3.97 us (4%)
  other arithmetic  2.22 us (2%)
    all_to_all x2, starting transfers between devices, scatter_sum(): return lax.all_to_all(pieces, axes, dim, dim, tiled=False).sum(dim)  26.7 us
    all_to_all x2, waiting for transfers between devices, scatter_sum(): return lax.all_to_all(pieces, axes, dim, dim, tiled=False).sum(dim)  20.4 us
    all_to_all x1, blocking collectives, all_sum(): lax.all_to_all(jnp.broadcast_to(mine, (count,) + mine.shape), axis, 0, 0,...  11.8 us
    ppermute x2, starting transfers between devices, neighbour_tiles(): tiles.append(lax.ppermute(tile, axis, backward))  11.8 us
    all_to_all x1, blocking collectives, scatter_sum(): return lax.all_to_all(pieces, axes, dim, dim, tiled=False).sum(dim)  10.9 us
    ppermute x2, starting transfers between devices, neighbour_tiles(): tiles.append(lax.ppermute(tile, axis, forward))  8.1 us
    dot_general x4, matrix products, transposed_times(): lax.dot_general(operand, second, (((0,), (0,)), ((), ())), precision=prec...  4.87 us
  transfers between devices with their start and end apart: 6, of which 2 were waited for; matrix products, arithmetic and copies ran while one was open for 4% of the time, Pallas kernels for 0%

profile of v10, /device:TPU:1, one launch (start us, length us, event | category | flops | bytes accessed | tf_op | source)
XLA Modules:
  0.0 112.2 jit_solution(12568418900735433139)
XLA Ops:
  0.6 0.0 copy-start
  0.7 1.4 %fusion.7 = f32[1024,128]{0,1:T(8,128)S(1)} fusion(bf16[1024,256]{1,0:T(8,128)(2,1)} %param.10), kind=kOutput, calls=%fused_computation.19 | convolution fusion | flops 67239936 | bytes 1048576 | tf_op jit(solution)/shard_map/dot_general | solution.py:37
  2.1 0.2 copy.18
  2.3 0.4 tile.8
  2.7 0.6 fusion.5
  3.2 0.0 copy-start.14
  3.2 0.4 tile.20
  3.6 0.0 copy-start.13
  3.6 0.0 copy-start.15
  3.6 0.0 copy-start.9
  3.6 0.3 fusion.9
  3.9 0.0 copy-start.6
  3.9 0.0 copy-start.12
  3.9 0.3 convolution_convert_fusion.1
  4.2 3.9 %collective-permute-start = (bf16[128,256]{1,0:T(8,128)(2,1)S(1)}, bf16[128,256]{1,0:T(8,128)(2,1)S(1)}, u32[]{:S(2)}, u32[]{:S(2)}) collective-permute-start(bf16[128,256]{1,0:T(8,128)(2,1)S(1)} %convolution_convert_fusion.1), channel_id=1, source_target_pairs={{0,16},{16,32},{32,48},{48,64},{64,80},{80,96},{96,112},{112,128},... | collective-permute-start | bytes 196616 | tf_op jit(solution)/shard_map/ppermute | solution.py:30
  8.2 1.3 %collective-permute-start.1 = (bf16[128,256]{1,0:T(8,128)(2,1)S(1)}, bf16[128,256]{1,0:T(8,128)(2,1)S(1)}, u32[]{:S(2)}, u32[]{:S(2)}) collective-permute-start(bf16[128,256]{1,0:T(8,128)(2,1)S(1)} %convolution_convert_fusion.1), channel_id=1, source_target_pairs={{16,0},{32,16},{48,32},{64,48},{80,64},{96,80},{112,96},{128,112},... | collective-permute-start | bytes 196616 | tf_op jit(solution)/shard_map/ppermute | solution.py:31
  9.5 4.2 %collective-permute-start.2 = (bf16[128,256]{1,0:T(8,128)(2,1)S(1)}, bf16[128,256]{1,0:T(8,128)(2,1)S(1)}, u32[]{:S(2)}, u32[]{:S(2)}) collective-permute-start(bf16[128,256]{1,0:T(8,128)(2,1)S(1)} %convolution_convert_fusion.1), channel_id=1, source_target_pairs={{0,1},{1,2},{2,3},{3,4},{4,5},{5,6},{6,7},{7,8},{8,9},{9,10},{10,1... | collective-permute-start | bytes 196616 | tf_op jit(solution)/shard_map/ppermute | solution.py:30
  13.6 10.5 %collective-permute-start.3 = (bf16[128,256]{1,0:T(8,128)(2,1)S(1)}, bf16[128,256]{1,0:T(8,128)(2,1)S(1)}, u32[]{:S(2)}, u32[]{:S(2)}) collective-permute-start(bf16[128,256]{1,0:T(8,128)(2,1)S(1)} %convolution_convert_fusion.1), channel_id=1, source_target_pairs={{1,0},{2,1},{3,2},{4,3},{5,4},{6,5},{7,6},{8,7},{9,8},{10,9},{11,1... | collective-permute-start | bytes 196616 | tf_op jit(solution)/shard_map/ppermute | solution.py:31
  24.3 0.1 copy.19
  24.3 0.1 reshape.102
  24.4 0.0 copy-done.15
  24.4 0.1 iota_compare_fusion.5
  24.5 1.3 %fusion.20 = f32[1024,256]{1,0:T(8,128)} fusion(bf16[1024,256]{1,0:T(8,128)(2,1)S(1)} %fusion.9, bf16[512,256]{1,0:T(8,128)(2,1)S(1)} %copy-done.9), kind=kOutput, calls=%fused_computation.41 | convolution fusion | flops 134217728 | bytes 1703936 | tf_op jit(solution)/shard_map/dot_general | solution.py:132
  25.8 1.1 convolution_bitcast_fusion
  26.8 0.0 collective-permute-done
  26.9 0.0 collective-permute-done.1
  26.9 0.0 collective-permute-done.2
  26.9 0.0 collective-permute-done.3
  26.9 0.7 gather_fusion
  27.6 1.7 %fusion.10 = f32[8,128,256,1]{2,1,3,0:T(8,128)S(1)} fusion(bf16[8,4,128,256]{3,2,1,0:T(8,128)(2,1)S(1)} %bitcast.84, bf16[8,4,128,128]{3,2,1,0:T(8,128)(2,1)} %param.11, pred[8,4]{1,0:T(8,128)(4,1)S(1)} %iota_compare_fusion.5), kind=kOutput, calls=%fused_computation.27 | convolution fusion | flops 268959744 | bytes 4194336 | tf_op jit(solution)/shard_map/bkij,bkjh->bih/dot_general | solution.py:120
  29.4 0.0 copy-start.10
  29.4 0.2 fusion.8
  29.5 0.0 copy-start.3
  29.5 0.8 copy-done.3
  30.3 0.3 fusion.54
  30.6 0.1 copy-done.2
  30.8 0.0 copy-done.10
  30.8 1.5 %convolution_add_fusion.1 = f32[1024,256]{1,0:T(8,128)} fusion(f32[1024,256]{1,0:T(8,128)S(1)} %copy-done.2, f32[1024,256]{1,0:T(8,128)S(1)} %fusion.54, bf16[1024,256]{1,0:T(8,128)(2,1)S(1)} %get-tuple-element.4, bf16[256,256]{1,0:T(8,128)(2,1)S(1)} %copy-done, bf16[512,256]{1,0:T(8,128)(2,1)S(1)} %copy-done.10), kind=kOutput, calls=%fused_computation.4 | convolution fusion | flops 269221888 | bytes 3932160 | tf_op jit(solution)/shard_map/dot_general | solution.py:132
  32.3 2.0 %convolution_bitcast_fusion.1 = f32[1,64,256]{2,1,0:T(8,128)S(1)} fusion(s32[1024]{0:T(1024)S(1)} %copy-done.12, bf16[1024,256]{1,0:T(8,128)(2,1)S(1)} %copy-done.1, f32[1024,256]{1,0:T(8,128)} %convolution_add_fusion.1), kind=kOutput, calls=%fused_computation.22 | convolution fusion | flops 102301696 | bytes 1642496 | tf_op jit(solution)/shard_map/dot_general | solution.py:62
  34.3 0.0 copy-done.8
  34.3 0.0 copy-start.5
  34.3 0.0 copy-start.7
  34.4 10.9 %all_to_all.24 = f32[16,8,256]{2,1,0:T(8,128)S(1)} all-to-all(f32[16,8,256]{2,1,0:T(8,128)S(1)} %bitcast.87), channel_id=1, replica_groups=mesh['along'=64,'across'=16] {'across'}, dimensions={0} | all-to-all | bytes 262144 | tf_op jit(solution)/shard_map/all_to_all | solution.py:13
  45.3 11.8 %all_to_all.25 = f32[16,8,256]{2,1,0:T(8,128)S(1)} all-to-all(f32[16,8,256]{2,1,0:T(8,128)S(1)} %broadcast_in_dim.40), channel_id=1, replica_groups=mesh['along'=64,'across'=16] {'across'}, dimensions={0} | all-to-all | bytes 262144 | tf_op jit(solution)/shard_map/all_to_all | solution.py:20
  57.1 0.1 slice_reduce_fusion
  57.2 0.1 div.45
  57.3 0.2 multiply_reduce_fusion.1
  57.4 0.1 rsqrt.16
  57.5 0.2 fusion.26
  57.8 0.2 fusion.55
  57.9 0.2 fusion.53
  58.2 0.0 copy-start.4
  58.2 1.5 %fusion.2 = bf16[1024,256]{1,0:T(8,128)(2,1)} fusion(f32[1024,256]{1,0:T(8,128)S(1)} %copy-done.5, bf16[1024,256]{1,0:T(8,128)(2,1)S(1)} %copy-done.7, s32[1024]{0:T(1024)S(1)} %copy-done.12, f32[64,256]{1,0:T(8,128)S(1)} %fusion.55, f32[16,8,256]{2,1,0:T(8,128)S(1)} %all_to_all.25, f32[64]{0:T(128)S(1)} %get-tuple-element.9, f32[64]{0:T(128)S(1)} %get-tuple-element.10, ...), kind=kOutput, calls=%fused_computation.12 | convolution fusion | flops 103710720 | bytes 2234368 | tf_op jit(solution)/shard_map/dot_general | solution.py:156
  59.7 1.7 %fusion.6 = f32[256,256]{1,0:T(8,128)S(1)} fusion(bf16[1024,256]{1,0:T(8,128)(2,1)S(1)} %copy-done.4, bf16[1024,256]{1,0:T(8,128)(2,1)} %fusion.2, bf16[512,256]{1,0:T(8,128)(2,1)S(1)} %copy-done.10), kind=kOutput, calls=%fused_computation.17 | convolution fusion | flops 268697600 | bytes 1441792 | tf_op jit(solution)/shard_map/dot_general | solution.py:62
  61.4 0.8 copy.20
  62.2 3.4 %all-to-all-start.2 = ((f32[32,16,128]{2,0,1:T(8,128)}), f32[32,16,128]{2,0,1:T(8,128)S(1)}, u32[]{:S(2)}, u32[]{:S(2)}) async-start(f32[32,16,128]{2,0,1:T(8,128)} %copy.20), calls=%async_computation.2 | async-start | bytes 524288 | tf_op jit(solution)/shard_map/all_to_all | solution.py:13
  65.7 0.1 copy.21
  65.8 0.2 fusion.27
  66.0 10.9 %all-to-all-done.2 = f32[32,16,128]{2,0,1:T(8,128)S(1)} async-done(((f32[32,16,128]{2,0,1:T(8,128)}), f32[32,16,128]{2,0,1:T(8,128)S(1)}, u32[]{:S(2)}, u32[]{:S(2)}) %all-to-all-start.2) | async-done | bytes 262176 | tf_op jit(solution)/shard_map/all_to_all | solution.py:13
  76.8 0.6 pad_maximum_fusion.1
  77.4 23.3 %all-to-all-start.3 = ((f32[64,1,128]{2,1,0:T(1,128)}), f32[64,1,128]{2,1,0:T(1,128)S(1)}, u32[]{:S(2)}, u32[]{:S(2)}) async-start(f32[64,1,128]{2,1,0:T(1,128)} %bitcast.20), calls=%async_computation.3 | async-start | bytes 65536 | tf_op jit(solution)/shard_map/all_to_all | solution.py:13
  100.7 1.3 %fusion.1 = bf16[1024,256]{1,0:T(8,128)(2,1)} fusion(s32[1024]{0:T(1024)S(1)} %copy-done.12, f32[64,256]{1,0:T(8,128)S(1)} %get-tuple-element.8, f32[1024,256]{1,0:T(8,128)S(1)} %copy-done.5, bf16[1024,256]{1,0:T(8,128)(2,1)S(1)} %copy-done.1), kind=kOutput, calls=%fused_computation.11 | convolution fusion | flops 35930112 | bytes 2166784 | tf_op jit(solution)/shard_map/dot_general | solution.py:143
  102.0 9.6 %all-to-all-done.3 = f32[64,1,128]{2,1,0:T(1,128)S(1)} async-done(((f32[64,1,128]{2,1,0:T(1,128)}), f32[64,1,128]{2,1,0:T(1,128)S(1)}, u32[]{:S(2)}, u32[]{:S(2)}) %all-to-all-start.3) | async-done | bytes 32800 | tf_op jit(solution)/shard_map/all_to_all | solution.py:13
  111.6 0.6 reduce_sum.69
  (31 shorter events, 0.2 us)
Async XLA Ops:
  0.6 29.7 %copy-start = (bf16[256,256]{1,0:T(8,128)(2,1)S(1)}, bf16[256,256]{1,0:T(8,128)(2,1)}, u32[]{:S(2)}) copy-start(bf16[256,256]{1,0:T(8,128)(2,1)} %param.16) | copy-start | bytes 393220
  0.6 2.0 %copy-start.1 = (bf16[1024,256]{1,0:T(8,128)(2,1)S(1)}, bf16[1024,256]{1,0:T(8,128)(2,1)}, u32[]{:S(2)}) copy-start(bf16[1024,256]{1,0:T(8,128)(2,1)} %param.10) | copy-start | bytes 1572868
  3.2 0.7 copy-start.14
  3.6 20.6 %copy-start.13 = (s32[8,4]{0,1:T(4,128)S(1)}, s32[8,4]{0,1:T(4,128)}, u32[]{:S(2)}) copy-start(s32[8,4]{0,1:T(4,128)} %param.12) | copy-start | bytes 388
  3.6 20.8 %copy-start.15 = (s32[8]{0:T(128)S(1)}, s32[8]{0:T(128)}, u32[]{:S(2)}) copy-start(s32[8]{0:T(128)} %param.13) | copy-start | bytes 100
  3.6 20.9 %copy-start.9 = (bf16[512,256]{1,0:T(8,128)(2,1)S(1)}, bf16[512,256]{1,0:T(8,128)(2,1)}, u32[]{:S(2)}) copy-start(bf16[512,256]{1,0:T(8,128)(2,1)} %param.17) | copy-start | bytes 786436
  3.9 21.9 %copy-start.6 = (bf16[1024,256]{1,0:T(8,128)(2,1)S(1)}, bf16[1024,256]{1,0:T(8,128)(2,1)}, u32[]{:S(2)}) copy-start(bf16[1024,256]{1,0:T(8,128)(2,1)} %param.19) | copy-start | bytes 1572868
  3.9 21.8 %copy-start.12 = (s32[1024]{0:T(1024)S(1)}, s32[1024]{0:T(1024)}, u32[]{:S(2)}) copy-start(s32[1024]{0:T(1024)} %param.15) | copy-start | bytes 12292
  4.2 22.6 %collective-permute-start = (bf16[128,256]{1,0:T(8,128)(2,1)S(1)}, bf16[128,256]{1,0:T(8,128)(2,1)S(1)}, u32[]{:S(2)}, u32[]{:S(2)}) collective-permute-start(bf16[128,256]{1,0:T(8,128)(2,1)S(1)} %convolution_convert_fusion.1), channel_id=1, source_target_pairs={{0,16},{16,32},{32,48},{48,64},{64,80},{80,96},{96,112},{112,128},... | collective-permute-start | bytes 196616 | tf_op jit(solution)/shard_map/ppermute | solution.py:30
  8.2 18.7 %collective-permute-start.1 = (bf16[128,256]{1,0:T(8,128)(2,1)S(1)}, bf16[128,256]{1,0:T(8,128)(2,1)S(1)}, u32[]{:S(2)}, u32[]{:S(2)}) collective-permute-start(bf16[128,256]{1,0:T(8,128)(2,1)S(1)} %convolution_convert_fusion.1), channel_id=1, source_target_pairs={{16,0},{32,16},{48,32},{64,48},{80,64},{96,80},{112,96},{128,112},... | collective-permute-start | bytes 196616 | tf_op jit(solution)/shard_map/ppermute | solution.py:31
  9.5 17.4 %collective-permute-start.2 = (bf16[128,256]{1,0:T(8,128)(2,1)S(1)}, bf16[128,256]{1,0:T(8,128)(2,1)S(1)}, u32[]{:S(2)}, u32[]{:S(2)}) collective-permute-start(bf16[128,256]{1,0:T(8,128)(2,1)S(1)} %convolution_convert_fusion.1), channel_id=1, source_target_pairs={{0,1},{1,2},{2,3},{3,4},{4,5},{5,6},{6,7},{7,8},{8,9},{9,10},{10,1... | collective-permute-start | bytes 196616 | tf_op jit(solution)/shard_map/ppermute | solution.py:30
  13.6 13.3 %collective-permute-start.3 = (bf16[128,256]{1,0:T(8,128)(2,1)S(1)}, bf16[128,256]{1,0:T(8,128)(2,1)S(1)}, u32[]{:S(2)}, u32[]{:S(2)}) collective-permute-start(bf16[128,256]{1,0:T(8,128)(2,1)S(1)} %convolution_convert_fusion.1), channel_id=1, source_target_pairs={{1,0},{2,1},{3,2},{4,3},{5,4},{6,5},{7,6},{8,7},{9,8},{10,9},{11,1... | collective-permute-start | bytes 196616 | tf_op jit(solution)/shard_map/ppermute | solution.py:31
  29.3 1.4 %copy-start.2 = (f32[1024,256]{1,0:T(8,128)S(1)}, f32[1024,256]{1,0:T(8,128)}, u32[]{:S(2)}) copy-start(f32[1024,256]{1,0:T(8,128)} %fusion.20) | copy-start | bytes 3145732
  29.4 1.4 %copy-start.10 = (bf16[512,256]{1,0:T(8,128)(2,1)S(1)}, bf16[512,256]{1,0:T(8,128)(2,1)}, u32[]{:S(2)}) copy-start(bf16[512,256]{1,0:T(8,128)(2,1)} %param.17) | copy-start | bytes 786436
  29.5 0.8 copy-start.3
  32.3 2.0 %copy-start.8 = (f32[1,64,256]{2,1,0:T(8,128)S(1)}, f32[1,64,256]{2,1,0:T(8,128)}, u32[]{:S(2)}) copy-start(f32[1,64,256]{2,1,0:T(8,128)} %convolution_bitcast_fusion) | copy-start | bytes 196612
  32.3 25.2 %copy-start.11 = (bf16[256,256]{1,0:T(8,128)(2,1)S(1)}, bf16[256,256]{1,0:T(8,128)(2,1)}, u32[]{:S(2)}) copy-start(bf16[256,256]{1,0:T(8,128)(2,1)} %param.18) | copy-start | bytes 393220
  34.3 23.8 %copy-start.5 = (f32[1024,256]{1,0:T(8,128)S(1)}, f32[1024,256]{1,0:T(8,128)}, u32[]{:S(2)}) copy-start(f32[1024,256]{1,0:T(8,128)} %convolution_add_fusion.1) | copy-start | bytes 3145732
  34.3 23.8 %copy-start.7 = (bf16[1024,256]{1,0:T(8,128)(2,1)S(1)}, bf16[1024,256]{1,0:T(8,128)(2,1)}, u32[]{:S(2)}) copy-start(bf16[1024,256]{1,0:T(8,128)(2,1)} %param.19) | copy-start | bytes 1572868
  58.2 1.5 %copy-start.4 = (bf16[1024,256]{1,0:T(8,128)(2,1)S(1)}, bf16[1024,256]{1,0:T(8,128)(2,1)}, u32[]{:S(2)}) copy-start(bf16[1024,256]{1,0:T(8,128)(2,1)} %copy-done.3) | copy-start | bytes 1572868
  62.2 14.6 %all-to-all-start.2 = ((f32[32,16,128]{2,0,1:T(8,128)}), f32[32,16,128]{2,0,1:T(8,128)S(1)}, u32[]{:S(2)}, u32[]{:S(2)}) async-start(f32[32,16,128]{2,0,1:T(8,128)} %copy.20), calls=%async_computation.2 | async-start | bytes 524288 | tf_op jit(solution)/shard_map/all_to_all | solution.py:13
  77.4 34.1 %all-to-all-start.3 = ((f32[64,1,128]{2,1,0:T(1,128)}), f32[64,1,128]{2,1,0:T(1,128)S(1)}, u32[]{:S(2)}, u32[]{:S(2)}) async-start(f32[64,1,128]{2,1,0:T(1,128)} %bitcast.20), calls=%async_computation.3 | async-start | bytes 65536 | tf_op jit(solution)/shard_map/all_to_all | solution.py:13

commit v11 on v10

--- a/solution.py
+++ b/solution.py
@@ -33,18 +33,16 @@
 
 
 def row_sums(values, precision=None):
-    ones = jnp.ones((values.shape[-1], 128), values.dtype)
+    ones = jnp.ones((values.shape[-1], values.shape[-1]), values.dtype)
     return jnp.dot(values, ones, precision=precision, preferred_element_type=jnp.float32)
 
 
 def normalize_rows(features):
     width = features.shape[-1]
-    repeat = width // 128
     mean = row_sums(features) / width
-    center = features.astype(jnp.float32) - jnp.tile(mean, (1, repeat))
+    center = features.astype(jnp.float32) - mean
     variance = row_sums(center * center, lax.Precision.HIGH) / width
-    inverse = lax.rsqrt(variance + eps)
-    return center * jnp.tile(inverse, (1, repeat))
+    return center * lax.rsqrt(variance + eps)
 
 
 def normalize(values):

time: 113 us -> 115 us (1.018)
  blocking collectives: 22.7 us -> 10.9 us
  waiting for transfers between devices: 20.4 us -> 29.2 us
  starting transfers between devices: 46.6 us -> 50 us
  local copies, waits for them, and re-layouts: 3.97 us -> 6.4 us
    all_to_all x1 -> x0, blocking collectives: 11.8 us -> none  [all_sum(): lax.all_to_all(jnp.broadcast_to(mine, (count,) + mine.shape), axis, 0, 0,...]
    all_to_all x0 -> x1, waiting for transfers between devices: none -> 8.51 us  [all_sum(): lax.all_to_all(jnp.broadcast_to(mine, (count,) + mine.shape), axis, 0, 0,...]
    all_to_all x0 -> x1, starting transfers between devices: none -> 3.41 us  [all_sum(): lax.all_to_all(jnp.broadcast_to(mine, (count,) + mine.shape), axis, 0, 0,...]
    unnamed x36 -> x39, local copies, waits for them, and re-layouts: 1.1 us -> 3.59 us
  transfers between devices with their start and end apart: 6 -> 7, of which waited for: 2 -> 3; matrix products, arithmetic and copies ran while one was open for 4% -> 4% of each run, Pallas kernels for 0% -> 0%
where the time goes in v11:
time: 115 us
  starting transfers between devices  50 us (43%)
  waiting for transfers between devices  29.2 us (25%)
  matrix products  15.2 us (13%)
  blocking collectives  10.9 us (9%)
  local copies, waits for them, and re-layouts  6.4 us (6%)
  other arithmetic  1.97 us (2%)
    all_to_all x2, starting transfers between devices, scatter_sum(): return lax.all_to_all(pieces, axes, dim, dim, tiled=False).sum(dim)  26.6 us
    all_to_all x2, waiting for transfers between devices, scatter_sum(): return lax.all_to_all(pieces, axes, dim, dim, tiled=False).sum(dim)  20.7 us
    ppermute x2, starting transfers between devices, neighbour_tiles(): tiles.append(lax.ppermute(tile, axis, backward))  11.8 us
    all_to_all x1, blocking collectives, scatter_sum(): return lax.all_to_all(pieces, axes, dim, dim, tiled=False).sum(dim)  10.9 us
    all_to_all x1, waiting for transfers between devices, all_sum(): lax.all_to_all(jnp.broadcast_to(mine, (count,) + mine.shape), axis, 0, 0,...  8.51 us
    ppermute x2, starting transfers between devices, neighbour_tiles(): tiles.append(lax.ppermute(tile, axis, forward))  8.11 us
    dot_general x4, matrix products, transposed_times(): lax.dot_general(operand, second, (((0,), (0,)), ((), ())), precision=prec...  4.99 us
    unnamed x39, local copies, waits for them, and re-layouts  3.59 us
  transfers between devices with their start and end apart: 7, of which 3 were waited for; matrix products, arithmetic and copies ran while one was open for 4% of the time, Pallas kernels for 0%

profile of v11, /device:TPU:1, one launch (start us, length us, event | category | flops | bytes accessed | tf_op | source)
XLA Modules:
  0.0 114.7 jit_solution(10765351480836824029)
XLA Ops:
  0.6 0.0 copy-start
  0.6 1.3 %copy.36 = bf16[1024,256]{0,1:T(8,128)(2,1)S(1)} copy(bf16[1024,256]{1,0:T(8,128)(2,1)} %param.10) | data formatting | bytes 1048576 | tf_op args[0]
  1.9 0.0 copy-start.3
  1.9 0.0 copy-start.14
  2.0 1.6 %fusion.1 = f32[1024,256]{0,1:T(8,128)S(1)} fusion(bf16[1024,256]{1,0:T(8,128)(2,1)} %param.10, bf16[1024,256]{0,1:T(8,128)(2,1)S(1)} %copy.36), kind=kOutput, calls=%fused_computation.8 | convolution fusion | flops 135004160 | bytes 2097152 | tf_op jit(solution)/shard_map/dot_general | solution.py:37
  3.6 0.0 copy-start.13
  3.6 0.0 copy-start.15
  3.6 0.0 copy-start.9
  3.6 0.7 fusion.6
  4.3 0.0 copy-start.2
  4.3 0.0 copy-start.12
  4.3 0.3 convolution_convert_fusion.1
  4.7 4.0 %collective-permute-start = (bf16[128,256]{1,0:T(8,128)(2,1)S(1)}, bf16[128,256]{1,0:T(8,128)(2,1)S(1)}, u32[]{:S(2)}, u32[]{:S(2)}) collective-permute-start(bf16[128,256]{1,0:T(8,128)(2,1)S(1)} %convolution_convert_fusion.1), channel_id=1, source_target_pairs={{0,16},{16,32},{32,48},{48,64},{64,80},{80,96},{96,112},{112,128},... | collective-permute-start | bytes 196616 | tf_op jit(solution)/shard_map/ppermute | solution.py:30
  8.6 1.3 %collective-permute-start.1 = (bf16[128,256]{1,0:T(8,128)(2,1)S(1)}, bf16[128,256]{1,0:T(8,128)(2,1)S(1)}, u32[]{:S(2)}, u32[]{:S(2)}) collective-permute-start(bf16[128,256]{1,0:T(8,128)(2,1)S(1)} %convolution_convert_fusion.1), channel_id=1, source_target_pairs={{16,0},{32,16},{48,32},{64,48},{80,64},{96,80},{112,96},{128,112},... | collective-permute-start | bytes 196616 | tf_op jit(solution)/shard_map/ppermute | solution.py:31
  9.9 4.2 %collective-permute-start.2 = (bf16[128,256]{1,0:T(8,128)(2,1)S(1)}, bf16[128,256]{1,0:T(8,128)(2,1)S(1)}, u32[]{:S(2)}, u32[]{:S(2)}) collective-permute-start(bf16[128,256]{1,0:T(8,128)(2,1)S(1)} %convolution_convert_fusion.1), channel_id=1, source_target_pairs={{0,1},{1,2},{2,3},{3,4},{4,5},{5,6},{6,7},{7,8},{8,9},{9,10},{10,1... | collective-permute-start | bytes 196616 | tf_op jit(solution)/shard_map/ppermute | solution.py:30
  14.1 10.5 %collective-permute-start.3 = (bf16[128,256]{1,0:T(8,128)(2,1)S(1)}, bf16[128,256]{1,0:T(8,128)(2,1)S(1)}, u32[]{:S(2)}, u32[]{:S(2)}) collective-permute-start(bf16[128,256]{1,0:T(8,128)(2,1)S(1)} %convolution_convert_fusion.1), channel_id=1, source_target_pairs={{1,0},{2,1},{3,2},{4,3},{5,4},{6,5},{7,6},{8,7},{9,8},{10,9},{11,1... | collective-permute-start | bytes 196616 | tf_op jit(solution)/shard_map/ppermute | solution.py:31
  24.6 0.2 copy.54
  24.9 0.1 copy.39
  25.0 0.1 reshape.94
  25.1 0.1 iota_compare_fusion.4
  25.1 1.3 %fusion.24 = f32[1024,256]{0,1:T(8,128)} fusion(bf16[1024,256]{0,1:T(8,128)(2,1)S(1)} %fusion.6, bf16[512,256]{1,0:T(8,128)(2,1)S(1)} %copy-done.9), kind=kOutput, calls=%fused_computation.42 | convolution fusion | flops 134217728 | bytes 1703936 | tf_op jit(solution)/shard_map/dot_general | solution.py:130
  26.5 0.0 copy-done.2
  26.5 1.1 convolution_bitcast_fusion.1
  27.5 0.0 collective-permute-done
  27.5 0.0 collective-permute-done.1
  27.6 0.0 collective-permute-done.2
  27.6 0.0 collective-permute-done.3
  27.6 0.7 gather_fusion
  28.3 1.7 %fusion.12 = f32[8,128,256,1]{2,1,3,0:T(8,128)S(1)} fusion(bf16[8,4,128,256]{3,2,1,0:T(8,128)(2,1)S(1)} %bitcast.71, bf16[8,4,128,128]{3,2,1,0:T(8,128)(2,1)} %param.11, pred[8,4]{1,0:T(8,128)(4,1)S(1)} %iota_compare_fusion.4), kind=kOutput, calls=%fused_computation.27 | convolution fusion | flops 268959744 | bytes 4194336 | tf_op jit(solution)/shard_map/bkij,bkjh->bih/dot_general | solution.py:118
  30.0 0.0 copy-start.1
  30.0 0.0 copy-start.10
  30.0 0.2 fusion.11
  30.2 0.8 copy-done.5
  31.0 0.3 fusion.58
  31.3 0.1 copy-done.1
  31.4 0.0 copy-done.10
  31.5 1.6 %convolution_add_fusion.1 = f32[1024,256]{0,1:T(8,128)} fusion(f32[1024,256]{0,1:T(8,128)S(1)} %copy-done.1, f32[1024,256]{1,0:T(8,128)S(1)} %fusion.58, bf16[1024,256]{1,0:T(8,128)(2,1)S(1)} %get-tuple-element.10, bf16[256,256]{1,0:T(8,128)(2,1)S(1)} %copy-done, bf16[512,256]{1,0:T(8,128)(2,1)S(1)} %copy-done.10), kind=kOutput, calls=%fused_computation.4 | convolution fusion | flops 269221888 | bytes 3932160 | tf_op jit(solution)/shard_map/dot_general | solution.py:130
  33.0 2.0 %convolution_bitcast_fusion = f32[1,64,256]{2,1,0:T(8,128)S(1)} fusion(s32[1024]{0:T(1024)S(1)} %copy-done.12, bf16[1024,256]{0,1:T(8,128)(2,1)} %copy-done.3, f32[1024,256]{0,1:T(8,128)} %convolution_add_fusion.1), kind=kOutput, calls=%fused_computation.23 | convolution fusion | flops 102367232 | bytes 1642496 | tf_op jit(solution)/shard_map/dot_general | solution.py:60
  35.1 0.0 copy-start.11
  35.1 10.9 %all_to_all.24 = f32[16,8,256]{2,1,0:T(8,128)S(1)} all-to-all(f32[16,8,256]{2,1,0:T(8,128)S(1)} %bitcast.73), channel_id=1, replica_groups=mesh['along'=64,'across'=16] {'across'}, dimensions={0} | all-to-all | bytes 262144 | tf_op jit(solution)/shard_map/all_to_all | solution.py:13
  46.0 0.7 broadcast_in_dim.40
  46.7 3.4 %all-to-all-start.1 = ((f32[16,8,256]{2,1,0:T(8,128)}), f32[16,8,256]{2,1,0:T(8,128)S(1)}, u32[]{:S(2)}, u32[]{:S(2)}) async-start(f32[16,8,256]{2,1,0:T(8,128)} %broadcast_in_dim.40), calls=%async_computation.1 | async-start | bytes 262144 | tf_op jit(solution)/shard_map/all_to_all | solution.py:20
  50.1 0.2 copy.43
  50.3 8.5 %all-to-all-done.1 = f32[16,8,256]{2,1,0:T(8,128)S(1)} async-done(((f32[16,8,256]{2,1,0:T(8,128)}), f32[16,8,256]{2,1,0:T(8,128)S(1)}, u32[]{:S(2)}, u32[]{:S(2)}) %all-to-all-start.1) | async-done | bytes 131104 | tf_op jit(solution)/shard_map/all_to_all | solution.py:20
  58.8 0.1 slice_reduce_fusion
  58.9 0.1 div.45
  59.0 0.2 multiply_reduce_fusion.1
  59.2 0.1 rsqrt.16
  59.3 0.2 fusion.31
  59.5 0.2 fusion.59
  59.6 0.2 fusion.57
  59.9 1.8 %fusion.8 = bf16[1024,256]{0,1:T(8,128)(2,1)} fusion(f32[1024,256]{0,1:T(8,128)S(1)} %copy-done.7, bf16[1024,256]{0,1:T(8,128)(2,1)S(1)} %copy.43, s32[1024]{0:T(1024)S(1)} %copy-done.12, f32[64,256]{1,0:T(8,128)S(1)} %fusion.59, f32[16,8,256]{2,1,0:T(8,128)S(1)} %all-to-all-done.1, f32[64]{0:T(128)S(1)} %get-tuple-element.15, ...), kind=kOutput, calls=%fused_computation.19 | convolution fusion | flops 103710720 | bytes 2234368 | tf_op jit(solution)/shard_map/dot_general | solution.py:154
  61.7 1.7 %fusion.10 = f32[256,256]{1,0:T(8,128)S(1)} fusion(bf16[1024,256]{1,0:T(8,128)(2,1)S(1)} %copy-done.6, bf16[1024,256]{0,1:T(8,128)(2,1)} %fusion.8, bf16[512,256]{1,0:T(8,128)(2,1)S(1)} %copy-done.10), kind=kOutput, calls=%fused_computation.21 | convolution fusion | flops 268697600 | bytes 1441792 | tf_op jit(solution)/shard_map/dot_general | solution.py:60
  63.4 0.8 copy.45
  64.2 3.4 %all-to-all-start.2 = ((f32[32,16,128]{2,0,1:T(8,128)}), f32[32,16,128]{2,0,1:T(8,128)S(1)}, u32[]{:S(2)}, u32[]{:S(2)}) async-start(f32[32,16,128]{2,0,1:T(8,128)} %copy.45), calls=%async_computation.2 | async-start | bytes 524288 | tf_op jit(solution)/shard_map/all_to_all | solution.py:13
  67.7 0.1 copy.46
  67.8 0.2 fusion.32
  68.0 11.4 %all-to-all-done.2 = f32[32,16,128]{2,0,1:T(8,128)S(1)} async-done(((f32[32,16,128]{2,0,1:T(8,128)}), f32[32,16,128]{2,0,1:T(8,128)S(1)}, u32[]{:S(2)}, u32[]{:S(2)}) %all-to-all-start.2) | async-done | bytes 262176 | tf_op jit(solution)/shard_map/all_to_all | solution.py:13
  79.4 0.6 pad_maximum_fusion.1
  80.0 23.2 %all-to-all-start.3 = ((f32[64,1,128]{2,1,0:T(1,128)}), f32[64,1,128]{2,1,0:T(1,128)S(1)}, u32[]{:S(2)}, u32[]{:S(2)}) async-start(f32[64,1,128]{2,1,0:T(1,128)} %bitcast.20), calls=%async_computation.3 | async-start | bytes 65536 | tf_op jit(solution)/shard_map/all_to_all | solution.py:13
  103.2 0.6 fusion.7
  103.8 1.0 copy.47
  104.8 9.2 %all-to-all-done.3 = f32[64,1,128]{2,1,0:T(1,128)S(1)} async-done(((f32[64,1,128]{2,1,0:T(1,128)}), f32[64,1,128]{2,1,0:T(1,128)S(1)}, u32[]{:S(2)}, u32[]{:S(2)}) %all-to-all-start.3) | async-done | bytes 32800 | tf_op jit(solution)/shard_map/all_to_all | solution.py:13
  114.1 0.6 reduce_sum.69
  (32 shorter events, 0.2 us)
Async XLA Ops:
  0.6 30.4 %copy-start = (bf16[256,256]{1,0:T(8,128)(2,1)S(1)}, bf16[256,256]{1,0:T(8,128)(2,1)}, u32[]{:S(2)}) copy-start(bf16[256,256]{1,0:T(8,128)(2,1)} %param.16) | copy-start | bytes 393220
  1.9 1.6 %copy-start.3 = (bf16[1024,256]{0,1:T(8,128)(2,1)}, bf16[1024,256]{0,1:T(8,128)(2,1)S(1)}, u32[]{:S(2)}) copy-start(bf16[1024,256]{0,1:T(8,128)(2,1)S(1)} %copy.36) | copy-start | bytes 1572868
  1.9 2.4 %copy-start.14 = (s32[128]{0:T(128)S(1)}, s32[128]{0:T(128)}, u32[]{:S(2)}) copy-start(s32[128]{0:T(128)} %param.14) | copy-start | bytes 1540
  3.6 21.3 %copy-start.13 = (s32[8,4]{0,1:T(4,128)S(1)}, s32[8,4]{0,1:T(4,128)}, u32[]{:S(2)}) copy-start(s32[8,4]{0,1:T(4,128)} %param.12) | copy-start | bytes 388
  3.6 21.5 %copy-start.15 = (s32[8]{0:T(128)S(1)}, s32[8]{0:T(128)}, u32[]{:S(2)}) copy-start(s32[8]{0:T(128)} %param.13) | copy-start | bytes 100
  3.6 21.6 %copy-start.9 = (bf16[512,256]{1,0:T(8,128)(2,1)S(1)}, bf16[512,256]{1,0:T(8,128)(2,1)}, u32[]{:S(2)}) copy-start(bf16[512,256]{1,0:T(8,128)(2,1)} %param.17) | copy-start | bytes 786436
  4.3 22.1 %copy-start.2 = (bf16[1024,256]{1,0:T(8,128)(2,1)S(1)}, bf16[1024,256]{1,0:T(8,128)(2,1)}, u32[]{:S(2)}) copy-start(bf16[1024,256]{1,0:T(8,128)(2,1)} %param.19) | copy-start | bytes 1572868
  4.3 22.1 %copy-start.12 = (s32[1024]{0:T(1024)S(1)}, s32[1024]{0:T(1024)}, u32[]{:S(2)}) copy-start(s32[1024]{0:T(1024)} %param.15) | copy-start | bytes 12292
  4.7 22.9 %collective-permute-start = (bf16[128,256]{1,0:T(8,128)(2,1)S(1)}, bf16[128,256]{1,0:T(8,128)(2,1)S(1)}, u32[]{:S(2)}, u32[]{:S(2)}) collective-permute-start(bf16[128,256]{1,0:T(8,128)(2,1)S(1)} %convolution_convert_fusion.1), channel_id=1, source_target_pairs={{0,16},{16,32},{32,48},{48,64},{64,80},{80,96},{96,112},{112,128},... | collective-permute-start | bytes 196616 | tf_op jit(solution)/shard_map/ppermute | solution.py:30
  8.6 18.9 %collective-permute-start.1 = (bf16[128,256]{1,0:T(8,128)(2,1)S(1)}, bf16[128,256]{1,0:T(8,128)(2,1)S(1)}, u32[]{:S(2)}, u32[]{:S(2)}) collective-permute-start(bf16[128,256]{1,0:T(8,128)(2,1)S(1)} %convolution_convert_fusion.1), channel_id=1, source_target_pairs={{16,0},{32,16},{48,32},{64,48},{80,64},{96,80},{112,96},{128,112},... | collective-permute-start | bytes 196616 | tf_op jit(solution)/shard_map/ppermute | solution.py:31
  9.9 17.7 %collective-permute-start.2 = (bf16[128,256]{1,0:T(8,128)(2,1)S(1)}, bf16[128,256]{1,0:T(8,128)(2,1)S(1)}, u32[]{:S(2)}, u32[]{:S(2)}) collective-permute-start(bf16[128,256]{1,0:T(8,128)(2,1)S(1)} %convolution_convert_fusion.1), channel_id=1, source_target_pairs={{0,1},{1,2},{2,3},{3,4},{4,5},{5,6},{6,7},{7,8},{8,9},{9,10},{10,1... | collective-permute-start | bytes 196616 | tf_op jit(solution)/shard_map/ppermute | solution.py:30
  14.1 13.5 %collective-permute-start.3 = (bf16[128,256]{1,0:T(8,128)(2,1)S(1)}, bf16[128,256]{1,0:T(8,128)(2,1)S(1)}, u32[]{:S(2)}, u32[]{:S(2)}) collective-permute-start(bf16[128,256]{1,0:T(8,128)(2,1)S(1)} %convolution_convert_fusion.1), channel_id=1, source_target_pairs={{1,0},{2,1},{3,2},{4,3},{5,4},{6,5},{7,6},{8,7},{9,8},{10,9},{11,1... | collective-permute-start | bytes 196616 | tf_op jit(solution)/shard_map/ppermute | solution.py:31
  30.0 1.4 %copy-start.1 = (f32[1024,256]{0,1:T(8,128)S(1)}, f32[1024,256]{0,1:T(8,128)}, u32[]{:S(2)}) copy-start(f32[1024,256]{0,1:T(8,128)} %fusion.24) | copy-start | bytes 3145732
  30.0 1.4 %copy-start.10 = (bf16[512,256]{1,0:T(8,128)(2,1)S(1)}, bf16[512,256]{1,0:T(8,128)(2,1)}, u32[]{:S(2)}) copy-start(bf16[512,256]{1,0:T(8,128)(2,1)} %param.17) | copy-start | bytes 786436
  30.2 0.8 copy-start.5
  33.0 2.1 %copy-start.8 = (f32[1,64,256]{2,1,0:T(8,128)S(1)}, f32[1,64,256]{2,1,0:T(8,128)}, u32[]{:S(2)}) copy-start(f32[1,64,256]{2,1,0:T(8,128)} %convolution_bitcast_fusion.1) | copy-start | bytes 196612
  35.1 24.2 %copy-start.11 = (bf16[256,256]{1,0:T(8,128)(2,1)S(1)}, bf16[256,256]{1,0:T(8,128)(2,1)}, u32[]{:S(2)}) copy-start(bf16[256,256]{1,0:T(8,128)(2,1)} %param.18) | copy-start | bytes 393220
  35.1 24.8 %copy-start.7 = (f32[1024,256]{0,1:T(8,128)S(1)}, f32[1024,256]{0,1:T(8,128)}, u32[]{:S(2)}) copy-start(f32[1024,256]{0,1:T(8,128)} %convolution_add_fusion.1) | copy-start | bytes 3145732
  46.7 12.1 %all-to-all-start.1 = ((f32[16,8,256]{2,1,0:T(8,128)}), f32[16,8,256]{2,1,0:T(8,128)S(1)}, u32[]{:S(2)}, u32[]{:S(2)}) async-start(f32[16,8,256]{2,1,0:T(8,128)} %broadcast_in_dim.40), calls=%async_computation.1 | async-start | bytes 262144 | tf_op jit(solution)/shard_map/all_to_all | solution.py:20
  59.9 1.8 %copy-start.6 = (bf16[1024,256]{1,0:T(8,128)(2,1)S(1)}, bf16[1024,256]{1,0:T(8,128)(2,1)}, u32[]{:S(2)}) copy-start(bf16[1024,256]{1,0:T(8,128)(2,1)} %copy-done.5) | copy-start | bytes 1572868
  61.7 41.5 %copy-start.4 = (bf16[1024,256]{0,1:T(8,128)(2,1)S(1)}, bf16[1024,256]{0,1:T(8,128)(2,1)}, u32[]{:S(2)}) copy-start(bf16[1024,256]{0,1:T(8,128)(2,1)} %copy-done.3) | copy-start | bytes 1572868
  64.2 15.2 %all-to-all-start.2 = ((f32[32,16,128]{2,0,1:T(8,128)}), f32[32,16,128]{2,0,1:T(8,128)S(1)}, u32[]{:S(2)}, u32[]{:S(2)}) async-start(f32[32,16,128]{2,0,1:T(8,128)} %copy.45), calls=%async_computation.2 | async-start | bytes 524288 | tf_op jit(solution)/shard_map/all_to_all | solution.py:13
  80.0 34.0 %all-to-all-start.3 = ((f32[64,1,128]{2,1,0:T(1,128)}), f32[64,1,128]{2,1,0:T(1,128)S(1)}, u32[]{:S(2)}, u32[]{:S(2)}) async-start(f32[64,1,128]{2,1,0:T(1,128)} %bitcast.20), calls=%async_computation.3 | async-start | bytes 65536 | tf_op jit(solution)/shard_map/all_to_all | solution.py:13

commit v12 on v10

--- a/solution.py
+++ b/solution.py
@@ -45,6 +45,19 @@
     variance = row_sums(center * center, lax.Precision.HIGH) / width
     inverse = lax.rsqrt(variance + eps)
     return center * jnp.tile(inverse, (1, repeat))
+
+
+def split_bf16(values):
+    high = lax.reduce_precision(values, exponent_bits=8, mantissa_bits=7)
+    return high.astype(jnp.bfloat16), (values - high).astype(jnp.bfloat16)
+
+
+def one_hot_times(one_hot, values, contract):
+    high, low = split_bf16(values)
+    dims = (((contract,), (0,)), ((), ()))
+    return lax.dot_general(one_hot, high, dims, preferred_element_type=jnp.float32) + lax.dot_general(
+        one_hot, low, dims, preferred_element_type=jnp.float32
+    )
 
 
 def normalize(values):
@@ -136,7 +149,7 @@
     coarse_count = NC_DEV * lax.axis_size("across")
     assign_float = (pool_index[:, None] == jnp.arange(coarse_count)[None, :]).astype(jnp.float32)
     assign_bits = assign_float.astype(jnp.bfloat16)
-    pooled_part = transposed_times(assign_float, hidden_one, lax.Precision.HIGH)
+    pooled_part = one_hot_times(assign_bits, hidden_one, 0)
     cot_part = transposed_times(assign_bits, cotangent)
     pooled, coarse_cot = all_sum(jnp.stack([pooled_part, cot_part]), "across")
     coarse_norm, inverse, coarse, coarse_pre, coarse_out = coarse_forward(pooled, w_coarse)
@@ -153,12 +166,7 @@
     picked_cols = lax.dynamic_slice_in_dim(coarse_delta, (member % halves) * chunk, chunk, 1)
     coarse_rows = transposed_times(coarse, picked_cols).reshape(-1, rows_per_step, chunk)
     coarse_grad = lax.dynamic_index_in_dim(coarse_rows, member // halves, 1, keepdims=False)
-    hidden_delta = cotangent.astype(jnp.float32) + jnp.dot(
-        assign_float,
-        pooled_delta,
-        precision=lax.Precision.HIGH,
-        preferred_element_type=jnp.float32,
-    )
+    hidden_delta = cotangent.astype(jnp.float32) + one_hot_times(assign_bits, pooled_delta, 1)
     update_delta = (hidden_delta * silu_slope(update_pre)).astype(jnp.bfloat16)
     aggregated_delta = times_transposed(update_delta, w_second).astype(jnp.bfloat16)
     message_grad = transposed_times(summed_scaled, aggregated_delta)

time: 113 us -> 116 us (1.027)
  matrix products: 15.1 us -> 18.3 us
    dot_general x1 -> x2, matrix products: 0.15 us -> 2.95 us  [times_transposed(): lax.dot_general(operand, second, (((1,), (1,)), ((), ())), preferred_elem...]
    dot_general x4 -> x3, matrix products: 4.87 us -> 2.62 us  [transposed_times(): lax.dot_general(operand, second, (((0,), (0,)), ((), ())), precision=prec...]
    dot_general x1, matrix products: 1.51 us -> 2.92 us  [local(): jnp.dot(aggregated, w_second, preferred_element_type=jnp.float32)]
where the time goes in v12:
time: 116 us
  starting transfers between devices  46.6 us (40%)
  blocking collectives  22.6 us (19%)
  waiting for transfers between devices  20.5 us (18%)
  matrix products  18.3 us (16%)
  local copies, waits for them, and re-layouts  3.52 us (3%)
  other arithmetic  3.02 us (3%)
    all_to_all x2, starting transfers between devices, scatter_sum(): return lax.all_to_all(pieces, axes, dim, dim, tiled=False).sum(dim)  26.7 us
    all_to_all x2, waiting for transfers between devices, scatter_sum(): return lax.all_to_all(pieces, axes, dim, dim, tiled=False).sum(dim)  20.5 us
    all_to_all x1, blocking collectives, all_sum(): lax.all_to_all(jnp.broadcast_to(mine, (count,) + mine.shape), axis, 0, 0,...  11.8 us
    ppermute x2, starting transfers between devices, neighbour_tiles(): tiles.append(lax.ppermute(tile, axis, backward))  11.8 us
    all_to_all x1, blocking collectives, scatter_sum(): return lax.all_to_all(pieces, axes, dim, dim, tiled=False).sum(dim)  10.7 us
    ppermute x2, starting transfers between devices, neighbour_tiles(): tiles.append(lax.ppermute(tile, axis, forward))  8.1 us
    dot_general x2, matrix products, times_transposed(): lax.dot_general(operand, second, (((1,), (1,)), ((), ())), preferred_elem...  2.95 us
    dot_general x1, matrix products, local(): jnp.dot(aggregated, w_second, preferred_element_type=jnp.float32)  2.92 us
  transfers between devices with their start and end apart: 6, of which 2 were waited for; matrix products, arithmetic and copies ran while one was open for 4% of the time, Pallas kernels for 0%

profile of v12, /device:TPU:1, one launch (start us, length us, event | category | flops | bytes accessed | tf_op | source)
XLA Modules:
  0.0 115.7 jit_solution(9828655500145387467)
XLA Ops:
  0.6 0.0 copy-start
  0.7 1.4 %fusion.7 = f32[1024,128]{0,1:T(8,128)S(1)} fusion(bf16[1024,256]{1,0:T(8,128)(2,1)} %param.10), kind=kOutput, calls=%fused_computation.21 | convolution fusion | flops 67239936 | bytes 1048576 | tf_op jit(solution)/shard_map/dot_general | solution.py:37
  2.1 0.2 copy.18
  2.3 0.4 tile.8
  2.7 0.6 fusion.6
  3.2 0.0 copy-start.13
  3.2 0.4 tile.20
  3.6 0.0 copy-start.9
  3.6 0.3 fusion.11
  3.9 0.0 copy-done.13
  3.9 0.0 copy-start.12
  3.9 0.0 copy-start.14
  3.9 0.0 copy-start.3
  3.9 0.0 copy-start.7
  3.9 0.3 convolution_convert_fusion.1
  4.2 3.9 %collective-permute-start = (bf16[128,256]{1,0:T(8,128)(2,1)S(1)}, bf16[128,256]{1,0:T(8,128)(2,1)S(1)}, u32[]{:S(2)}, u32[]{:S(2)}) collective-permute-start(bf16[128,256]{1,0:T(8,128)(2,1)S(1)} %convolution_convert_fusion.1), channel_id=1, source_target_pairs={{0,16},{16,32},{32,48},{48,64},{64,80},{80,96},{96,112},{112,128},... | collective-permute-start | bytes 196616 | tf_op jit(solution)/shard_map/ppermute | solution.py:30
  8.2 1.3 %collective-permute-start.1 = (bf16[128,256]{1,0:T(8,128)(2,1)S(1)}, bf16[128,256]{1,0:T(8,128)(2,1)S(1)}, u32[]{:S(2)}, u32[]{:S(2)}) collective-permute-start(bf16[128,256]{1,0:T(8,128)(2,1)S(1)} %convolution_convert_fusion.1), channel_id=1, source_target_pairs={{16,0},{32,16},{48,32},{64,48},{80,64},{96,80},{112,96},{128,112},... | collective-permute-start | bytes 196616 | tf_op jit(solution)/shard_map/ppermute | solution.py:31
  9.5 4.2 %collective-permute-start.2 = (bf16[128,256]{1,0:T(8,128)(2,1)S(1)}, bf16[128,256]{1,0:T(8,128)(2,1)S(1)}, u32[]{:S(2)}, u32[]{:S(2)}) collective-permute-start(bf16[128,256]{1,0:T(8,128)(2,1)S(1)} %convolution_convert_fusion.1), channel_id=1, source_target_pairs={{0,1},{1,2},{2,3},{3,4},{4,5},{5,6},{6,7},{7,8},{8,9},{9,10},{10,1... | collective-permute-start | bytes 196616 | tf_op jit(solution)/shard_map/ppermute | solution.py:30
  13.6 10.5 %collective-permute-start.3 = (bf16[128,256]{1,0:T(8,128)(2,1)S(1)}, bf16[128,256]{1,0:T(8,128)(2,1)S(1)}, u32[]{:S(2)}, u32[]{:S(2)}) collective-permute-start(bf16[128,256]{1,0:T(8,128)(2,1)S(1)} %convolution_convert_fusion.1), channel_id=1, source_target_pairs={{1,0},{2,1},{3,2},{4,3},{5,4},{6,5},{7,6},{8,7},{9,8},{10,9},{11,1... | collective-permute-start | bytes 196616 | tf_op jit(solution)/shard_map/ppermute | solution.py:31
  24.2 0.0 copy-done.9
  24.2 1.3 %fusion.34 = f32[1024,256]{1,0:T(8,128)} fusion(bf16[1024,256]{1,0:T(8,128)(2,1)S(1)} %fusion.11, bf16[512,256]{1,0:T(8,128)(2,1)S(1)} %copy-done.9), kind=kOutput, calls=%fused_computation.55 | convolution fusion | flops 134217728 | bytes 1703936 | tf_op jit(solution)/shard_map/dot_general | solution.py:145
  25.5 0.0 copy-done.12
  25.5 0.1 copy.19
  25.6 0.1 reshape.102
  25.7 0.1 iota_compare_fusion.10
  25.8 0.0 copy-done.3
  25.8 1.1 convolution_bitcast_fusion
  26.8 0.0 collective-permute-done
  26.9 0.0 collective-permute-done.1
  26.9 0.0 collective-permute-done.2
  26.9 0.0 collective-permute-done.3
  26.9 0.7 gather_fusion
  27.6 1.7 %fusion.17 = f32[8,128,256,1]{2,1,3,0:T(8,128)S(1)} fusion(bf16[8,4,128,256]{3,2,1,0:T(8,128)(2,1)S(1)} %bitcast.90, bf16[8,4,128,128]{3,2,1,0:T(8,128)(2,1)} %param.11, pred[8,4]{1,0:T(8,128)(4,1)S(1)} %iota_compare_fusion.10), kind=kOutput, calls=%fused_computation.36 | convolution fusion | flops 268959744 | bytes 4194336 | tf_op jit(solution)/shard_map/bkij,bkjh->bih/dot_general | solution.py:133
  29.3 0.0 copy-start.10
  29.4 0.9 fusion.9
  30.3 1.3 %fusion.62 = f32[1024,256]{1,0:T(8,128)} fusion(bf16[1024,256]{1,0:T(8,128)(2,1)S(1)} %get-tuple-element.5, bf16[256,256]{1,0:T(8,128)(2,1)S(1)} %copy-done), kind=kOutput, calls=%fused_computation.104 | convolution fusion | flops 134217728 | bytes 1703936 | tf_op jit(solution)/shard_map/dot_general | solution.py:140
  31.6 2.9 %convert_add_fusion = (f32[1024,256]{1,0:T(8,128)S(1)}, f32[1024,256]{1,0:T(8,128)}) fusion(bf16[1024,256]{1,0:T(8,128)(2,1)S(1)} %copy-done.1, f32[1024,256]{1,0:T(8,128)S(1)} %copy-done.2, bf16[512,256]{1,0:T(8,128)(2,1)S(1)} %copy-done.10, f32[1024,256]{1,0:T(8,128)} %fusion.62, bf16[1024,256]{1,0:T(8,128)(2,1)} %get-tuple-element.4, ...), kind=kOutput, calls=%fused_computation.11 | convolution fusion | flops 270794752 | bytes 5505024 | tf_op jit(solution)/shard_map/dot_general | solution.py:145
  34.6 0.4 fusion.22
  35.0 0.0 copy-start.4
  35.0 0.4 fusion.8
  35.5 10.7 %all_to_all.24 = f32[16,8,256]{2,1,0:T(8,128)S(1)} all-to-all(f32[16,8,256]{2,1,0:T(8,128)S(1)} %bitcast.93), channel_id=1, replica_groups=mesh['along'=64,'across'=16] {'across'}, dimensions={0} | all-to-all | bytes 262144 | tf_op jit(solution)/shard_map/all_to_all | solution.py:13
  46.3 11.8 %all_to_all.25 = f32[16,8,256]{2,1,0:T(8,128)S(1)} all-to-all(f32[16,8,256]{2,1,0:T(8,128)S(1)} %broadcast_in_dim.40), channel_id=1, replica_groups=mesh['along'=64,'across'=16] {'across'}, dimensions={0} | all-to-all | bytes 262144 | tf_op jit(solution)/shard_map/all_to_all | solution.py:20
  58.1 0.1 slice_reduce_fusion
  58.2 0.1 div.45
  58.3 0.2 multiply_reduce_fusion.1
  58.5 0.1 rsqrt.16
  58.6 0.8 fusion.40
  59.4 0.2 fusion.63
  59.5 0.2 fusion.61
  59.8 0.0 copy-start.11
  59.8 0.5 copy-done.11
  60.3 0.4 fusion.23
  60.7 2.8 %convolution_convert_fusion = bf16[1024,256]{1,0:T(8,128)(2,1)} fusion(f32[1024,256]{1,0:T(8,128)S(1)} %fusion.23, f32[1024,256]{1,0:T(8,128)} %get-tuple-element.8, bf16[1024,256]{1,0:T(8,128)(2,1)S(1)} %copy-done.4, s32[1024]{0:T(1024)S(1)} %copy-done.7, bf16[512,256]{1,0:T(8,128)(2,1)} %param.17, f32[64,256]{1,0:T(8,128)S(1)} %fusion.63, ...), kind=kOutput, calls=%fused_computation.13 | convolution fusion | flops 171524096 | bytes 3414016 | tf_op jit(solution)/shard_map/dot_general | solution.py:85
  63.5 1.4 %fusion.64 = f32[256,256]{1,0:T(8,128)S(1)} fusion(bf16[1024,256]{1,0:T(8,128)(2,1)S(1)} %get-tuple-element.5, bf16[1024,256]{1,0:T(8,128)(2,1)} %convolution_convert_fusion), kind=kOutput, calls=%fused_computation.106 | convolution fusion | flops 134217728 | bytes 1310720 | tf_op jit(solution)/shard_map/dot_general | solution.py:75
  64.9 0.8 copy.20
  65.7 3.4 %all-to-all-start.2 = ((f32[32,16,128]{2,0,1:T(8,128)}), f32[32,16,128]{2,0,1:T(8,128)S(1)}, u32[]{:S(2)}, u32[]{:S(2)}) async-start(f32[32,16,128]{2,0,1:T(8,128)} %copy.20), calls=%async_computation.2 | async-start | bytes 524288 | tf_op jit(solution)/shard_map/all_to_all | solution.py:13
  69.2 0.1 copy.21
  69.3 0.2 fusion.41
  69.5 10.9 %all-to-all-done.2 = f32[32,16,128]{2,0,1:T(8,128)S(1)} async-done(((f32[32,16,128]{2,0,1:T(8,128)}), f32[32,16,128]{2,0,1:T(8,128)S(1)}, u32[]{:S(2)}, u32[]{:S(2)}) %all-to-all-start.2) | async-done | bytes 262176 | tf_op jit(solution)/shard_map/all_to_all | solution.py:13
  80.3 0.6 pad_maximum_fusion.1
  81.0 23.3 %all-to-all-start.3 = ((f32[64,1,128]{2,1,0:T(1,128)}), f32[64,1,128]{2,1,0:T(1,128)S(1)}, u32[]{:S(2)}, u32[]{:S(2)}) async-start(f32[64,1,128]{2,1,0:T(1,128)} %bitcast.20), calls=%async_computation.3 | async-start | bytes 65536 | tf_op jit(solution)/shard_map/all_to_all | solution.py:13
  104.2 1.2 fusion.2
  105.4 9.7 %all-to-all-done.3 = f32[64,1,128]{2,1,0:T(1,128)S(1)} async-done(((f32[64,1,128]{2,1,0:T(1,128)}), f32[64,1,128]{2,1,0:T(1,128)S(1)}, u32[]{:S(2)}, u32[]{:S(2)}) %all-to-all-start.3) | async-done | bytes 32800 | tf_op jit(solution)/shard_map/all_to_all | solution.py:13
  115.1 0.6 reduce_sum.69
  (31 shorter events, 0.2 us)
Async XLA Ops:
  0.6 29.7 %copy-start = (bf16[256,256]{1,0:T(8,128)(2,1)S(1)}, bf16[256,256]{1,0:T(8,128)(2,1)}, u32[]{:S(2)}) copy-start(bf16[256,256]{1,0:T(8,128)(2,1)} %param.16) | copy-start | bytes 393220
  0.6 2.0 %copy-start.1 = (bf16[1024,256]{1,0:T(8,128)(2,1)S(1)}, bf16[1024,256]{1,0:T(8,128)(2,1)}, u32[]{:S(2)}) copy-start(bf16[1024,256]{1,0:T(8,128)(2,1)} %param.10) | copy-start | bytes 1572868
  3.2 0.7 copy-start.13
  3.6 20.6 %copy-start.9 = (bf16[512,256]{1,0:T(8,128)(2,1)S(1)}, bf16[512,256]{1,0:T(8,128)(2,1)}, u32[]{:S(2)}) copy-start(bf16[512,256]{1,0:T(8,128)(2,1)} %param.17) | copy-start | bytes 786436
  3.9 21.6 %copy-start.12 = (s32[8,4]{0,1:T(4,128)S(1)}, s32[8,4]{0,1:T(4,128)}, u32[]{:S(2)}) copy-start(s32[8,4]{0,1:T(4,128)} %param.12) | copy-start | bytes 388
  3.9 21.8 %copy-start.14 = (s32[8]{0:T(128)S(1)}, s32[8]{0:T(128)}, u32[]{:S(2)}) copy-start(s32[8]{0:T(128)} %param.13) | copy-start | bytes 100
  3.9 21.9 %copy-start.3 = (bf16[1024,256]{1,0:T(8,128)(2,1)S(1)}, bf16[1024,256]{1,0:T(8,128)(2,1)}, u32[]{:S(2)}) copy-start(bf16[1024,256]{1,0:T(8,128)(2,1)} %param.19) | copy-start | bytes 1572868
  3.9 21.8 %copy-start.7 = (s32[1024]{0:T(1024)S(1)}, s32[1024]{0:T(1024)}, u32[]{:S(2)}) copy-start(s32[1024]{0:T(1024)} %param.15) | copy-start | bytes 12292
  4.2 22.6 %collective-permute-start = (bf16[128,256]{1,0:T(8,128)(2,1)S(1)}, bf16[128,256]{1,0:T(8,128)(2,1)S(1)}, u32[]{:S(2)}, u32[]{:S(2)}) collective-permute-start(bf16[128,256]{1,0:T(8,128)(2,1)S(1)} %convolution_convert_fusion.1), channel_id=1, source_target_pairs={{0,16},{16,32},{32,48},{48,64},{64,80},{80,96},{96,112},{112,128},... | collective-permute-start | bytes 196616 | tf_op jit(solution)/shard_map/ppermute | solution.py:30
  8.2 18.7 %collective-permute-start.1 = (bf16[128,256]{1,0:T(8,128)(2,1)S(1)}, bf16[128,256]{1,0:T(8,128)(2,1)S(1)}, u32[]{:S(2)}, u32[]{:S(2)}) collective-permute-start(bf16[128,256]{1,0:T(8,128)(2,1)S(1)} %convolution_convert_fusion.1), channel_id=1, source_target_pairs={{16,0},{32,16},{48,32},{64,48},{80,64},{96,80},{112,96},{128,112},... | collective-permute-start | bytes 196616 | tf_op jit(solution)/shard_map/ppermute | solution.py:31
  9.5 17.4 %collective-permute-start.2 = (bf16[128,256]{1,0:T(8,128)(2,1)S(1)}, bf16[128,256]{1,0:T(8,128)(2,1)S(1)}, u32[]{:S(2)}, u32[]{:S(2)}) collective-permute-start(bf16[128,256]{1,0:T(8,128)(2,1)S(1)} %convolution_convert_fusion.1), channel_id=1, source_target_pairs={{0,1},{1,2},{2,3},{3,4},{4,5},{5,6},{6,7},{7,8},{8,9},{9,10},{10,1... | collective-permute-start | bytes 196616 | tf_op jit(solution)/shard_map/ppermute | solution.py:30
  13.6 13.3 %collective-permute-start.3 = (bf16[128,256]{1,0:T(8,128)(2,1)S(1)}, bf16[128,256]{1,0:T(8,128)(2,1)S(1)}, u32[]{:S(2)}, u32[]{:S(2)}) collective-permute-start(bf16[128,256]{1,0:T(8,128)(2,1)S(1)} %convolution_convert_fusion.1), channel_id=1, source_target_pairs={{1,0},{2,1},{3,2},{4,3},{5,4},{6,5},{7,6},{8,7},{9,8},{10,9},{11,1... | collective-permute-start | bytes 196616 | tf_op jit(solution)/shard_map/ppermute | solution.py:31
  29.3 2.3 %copy-start.2 = (f32[1024,256]{1,0:T(8,128)S(1)}, f32[1024,256]{1,0:T(8,128)}, u32[]{:S(2)}) copy-start(f32[1024,256]{1,0:T(8,128)} %fusion.34) | copy-start | bytes 3145732
  29.3 2.3 %copy-start.10 = (bf16[512,256]{1,0:T(8,128)(2,1)S(1)}, bf16[512,256]{1,0:T(8,128)(2,1)}, u32[]{:S(2)}) copy-start(bf16[512,256]{1,0:T(8,128)(2,1)} %param.17) | copy-start | bytes 786436
  34.6 0.9 copy-start.5
  34.6 24.0 %copy-start.6 = (bf16[256,256]{1,0:T(8,128)(2,1)S(1)}, bf16[256,256]{1,0:T(8,128)(2,1)}, u32[]{:S(2)}) copy-start(bf16[256,256]{1,0:T(8,128)(2,1)} %param.18) | copy-start | bytes 393220
  35.0 25.7 %copy-start.4 = (bf16[1024,256]{1,0:T(8,128)(2,1)S(1)}, bf16[1024,256]{1,0:T(8,128)(2,1)}, u32[]{:S(2)}) copy-start(bf16[1024,256]{1,0:T(8,128)(2,1)} %param.19) | copy-start | bytes 1572868
  59.8 0.5 copy-start.11
  63.5 40.7 %copy-start.8 = (f32[64,256]{1,0:T(8,128)S(1)}, f32[64,256]{1,0:T(8,128)}, u32[]{:S(2)}) copy-start(f32[64,256]{1,0:T(8,128)} %get-tuple-element.10) | copy-start | bytes 196612
  65.7 14.6 %all-to-all-start.2 = ((f32[32,16,128]{2,0,1:T(8,128)}), f32[32,16,128]{2,0,1:T(8,128)S(1)}, u32[]{:S(2)}, u32[]{:S(2)}) async-start(f32[32,16,128]{2,0,1:T(8,128)} %copy.20), calls=%async_computation.2 | async-start | bytes 524288 | tf_op jit(solution)/shard_map/all_to_all | solution.py:13
  81.0 34.1 %all-to-all-start.3 = ((f32[64,1,128]{2,1,0:T(1,128)}), f32[64,1,128]{2,1,0:T(1,128)S(1)}, u32[]{:S(2)}, u32[]{:S(2)}) async-start(f32[64,1,128]{2,1,0:T(1,128)} %bitcast.20), calls=%async_computation.3 | async-start | bytes 65536 | tf_op jit(solution)/shard_map/all_to_all | solution.py:13

commit v13 on v10

--- a/solution.py
+++ b/solution.py
@@ -136,8 +136,9 @@
     coarse_count = NC_DEV * lax.axis_size("across")
     assign_float = (pool_index[:, None] == jnp.arange(coarse_count)[None, :]).astype(jnp.float32)
     assign_bits = assign_float.astype(jnp.bfloat16)
-    pooled_part = transposed_times(assign_float, hidden_one, lax.Precision.HIGH)
-    cot_part = transposed_times(assign_bits, cotangent)
+    members = (jnp.arange(coarse_count)[:, None] == pool_index[None, :]).astype(jnp.float32)
+    pooled_part = jnp.dot(members, hidden_one, precision=lax.Precision.HIGH, preferred_element_type=jnp.float32)
+    cot_part = jnp.dot(members.astype(jnp.bfloat16), cotangent, preferred_element_type=jnp.float32)
     pooled, coarse_cot = all_sum(jnp.stack([pooled_part, cot_part]), "across")
     coarse_norm, inverse, coarse, coarse_pre, coarse_out = coarse_forward(pooled, w_coarse)
     hidden_two = hidden_one + jnp.dot(assign_bits, coarse_out, preferred_element_type=jnp.float32)

time: 113 us -> 112 us (level)
    dot_general x4 -> x2, matrix products: 4.87 us -> 1.82 us  [transposed_times(): lax.dot_general(operand, second, (((0,), (0,)), ((), ())), precision=prec...]
    dot_general x0 -> x2, matrix products: none -> 2.65 us  [the longest x1 1.82 us: local(): jnp.dot(members, hidden_one, precision=lax.Precision.HIGH, preferred_elem...]
where the time goes in v13:
time: 112 us
  starting transfers between devices  46.6 us (42%)
  blocking collectives  22.7 us (20%)
  waiting for transfers between devices  20.4 us (18%)
  matrix products  14.7 us (13%)
  local copies, waits for them, and re-layouts  3.97 us (4%)
  other arithmetic  2.22 us (2%)
    all_to_all x2, starting transfers between devices, scatter_sum(): return lax.all_to_all(pieces, axes, dim, dim, tiled=False).sum(dim)  26.7 us
    all_to_all x2, waiting for transfers between devices, scatter_sum(): return lax.all_to_all(pieces, axes, dim, dim, tiled=False).sum(dim)  20.4 us
    all_to_all x1, blocking collectives, all_sum(): lax.all_to_all(jnp.broadcast_to(mine, (count,) + mine.shape), axis, 0, 0,...  11.8 us
    ppermute x2, starting transfers between devices, neighbour_tiles(): tiles.append(lax.ppermute(tile, axis, backward))  11.8 us
    all_to_all x1, blocking collectives, scatter_sum(): return lax.all_to_all(pieces, axes, dim, dim, tiled=False).sum(dim)  10.9 us
    ppermute x2, starting transfers between devices, neighbour_tiles(): tiles.append(lax.ppermute(tile, axis, forward))  8.1 us
  transfers between devices with their start and end apart: 6, of which 2 were waited for; matrix products, arithmetic and copies ran while one was open for 4% of the time, Pallas kernels for 0%

profile of v13, /device:TPU:1, one launch (start us, length us, event | category | flops | bytes accessed | tf_op | source)
XLA Modules:
  0.0 111.7 jit_solution(16919782176864880150)
XLA Ops:
  0.6 0.0 copy-start
  0.7 1.4 %fusion.7 = f32[1024,128]{0,1:T(8,128)S(1)} fusion(bf16[1024,256]{1,0:T(8,128)(2,1)} %param.10), kind=kOutput, calls=%fused_computation.19 | convolution fusion | flops 67239936 | bytes 1048576 | tf_op jit(solution)/shard_map/dot_general | solution.py:37
  2.1 0.2 copy.18
  2.3 0.4 tile.8
  2.7 0.6 fusion.5
  3.2 0.0 copy-start.14
  3.2 0.4 tile.20
  3.6 0.0 copy-start.13
  3.6 0.0 copy-start.15
  3.6 0.0 copy-start.9
  3.6 0.3 fusion.9
  3.9 0.0 copy-start.6
  3.9 0.0 copy-start.12
  3.9 0.3 convolution_convert_fusion.1
  4.2 3.9 %collective-permute-start = (bf16[128,256]{1,0:T(8,128)(2,1)S(1)}, bf16[128,256]{1,0:T(8,128)(2,1)S(1)}, u32[]{:S(2)}, u32[]{:S(2)}) collective-permute-start(bf16[128,256]{1,0:T(8,128)(2,1)S(1)} %convolution_convert_fusion.1), channel_id=1, source_target_pairs={{0,16},{16,32},{32,48},{48,64},{64,80},{80,96},{96,112},{112,128},... | collective-permute-start | bytes 196616 | tf_op jit(solution)/shard_map/ppermute | solution.py:30
  8.2 1.3 %collective-permute-start.1 = (bf16[128,256]{1,0:T(8,128)(2,1)S(1)}, bf16[128,256]{1,0:T(8,128)(2,1)S(1)}, u32[]{:S(2)}, u32[]{:S(2)}) collective-permute-start(bf16[128,256]{1,0:T(8,128)(2,1)S(1)} %convolution_convert_fusion.1), channel_id=1, source_target_pairs={{16,0},{32,16},{48,32},{64,48},{80,64},{96,80},{112,96},{128,112},... | collective-permute-start | bytes 196616 | tf_op jit(solution)/shard_map/ppermute | solution.py:31
  9.5 4.2 %collective-permute-start.2 = (bf16[128,256]{1,0:T(8,128)(2,1)S(1)}, bf16[128,256]{1,0:T(8,128)(2,1)S(1)}, u32[]{:S(2)}, u32[]{:S(2)}) collective-permute-start(bf16[128,256]{1,0:T(8,128)(2,1)S(1)} %convolution_convert_fusion.1), channel_id=1, source_target_pairs={{0,1},{1,2},{2,3},{3,4},{4,5},{5,6},{6,7},{7,8},{8,9},{9,10},{10,1... | collective-permute-start | bytes 196616 | tf_op jit(solution)/shard_map/ppermute | solution.py:30
  13.6 10.5 %collective-permute-start.3 = (bf16[128,256]{1,0:T(8,128)(2,1)S(1)}, bf16[128,256]{1,0:T(8,128)(2,1)S(1)}, u32[]{:S(2)}, u32[]{:S(2)}) collective-permute-start(bf16[128,256]{1,0:T(8,128)(2,1)S(1)} %convolution_convert_fusion.1), channel_id=1, source_target_pairs={{1,0},{2,1},{3,2},{4,3},{5,4},{6,5},{7,6},{8,7},{9,8},{10,9},{11,1... | collective-permute-start | bytes 196616 | tf_op jit(solution)/shard_map/ppermute | solution.py:31
  24.3 0.1 copy.19
  24.3 0.1 reshape.103
  24.4 0.0 copy-done.15
  24.4 0.1 iota_compare_fusion.6
  24.5 1.3 %fusion.20 = f32[1024,256]{1,0:T(8,128)} fusion(bf16[1024,256]{1,0:T(8,128)(2,1)S(1)} %fusion.9, bf16[512,256]{1,0:T(8,128)(2,1)S(1)} %copy-done.9), kind=kOutput, calls=%fused_computation.43 | convolution fusion | flops 134217728 | bytes 1703936 | tf_op jit(solution)/shard_map/dot_general | solution.py:132
  25.8 0.0 copy-done.6
  25.8 0.8 convolution_bitcast_fusion
  26.6 0.0 collective-permute-done
  26.6 0.0 collective-permute-done.1
  26.7 0.0 collective-permute-done.2
  26.7 0.0 collective-permute-done.3
  26.7 0.7 gather_fusion
  27.4 1.7 %fusion.10 = f32[8,128,256,1]{2,1,3,0:T(8,128)S(1)} fusion(bf16[8,4,128,256]{3,2,1,0:T(8,128)(2,1)S(1)} %bitcast.84, bf16[8,4,128,128]{3,2,1,0:T(8,128)(2,1)} %param.11, pred[8,4]{1,0:T(8,128)(4,1)S(1)} %iota_compare_fusion.6), kind=kOutput, calls=%fused_computation.27 | convolution fusion | flops 268959744 | bytes 4194336 | tf_op jit(solution)/shard_map/bkij,bkjh->bih/dot_general | solution.py:120
  29.1 0.0 copy-start.2
  29.1 0.0 copy-start.10
  29.1 0.2 fusion.8
  29.3 0.0 copy-start.3
  29.3 0.8 copy-done.3
  30.1 0.3 fusion.54
  30.4 0.1 copy-done.2
  30.5 0.0 copy-done.10
  30.6 1.5 %convolution_add_fusion.1 = f32[1024,256]{1,0:T(8,128)} fusion(f32[1024,256]{1,0:T(8,128)S(1)} %copy-done.2, f32[1024,256]{1,0:T(8,128)S(1)} %fusion.54, bf16[1024,256]{1,0:T(8,128)(2,1)S(1)} %get-tuple-element.4, bf16[256,256]{1,0:T(8,128)(2,1)S(1)} %copy-done, bf16[512,256]{1,0:T(8,128)(2,1)S(1)} %copy-done.10), kind=kOutput, calls=%fused_computation.4 | convolution fusion | flops 269221888 | bytes 3932160 | tf_op jit(solution)/shard_map/dot_general | solution.py:132
  32.1 1.8 %convolution_bitcast_fusion.1 = f32[1,64,256]{2,1,0:T(8,128)S(1)} fusion(s32[1024]{0:T(1024)S(1)} %copy-done.12, bf16[1024,256]{1,0:T(8,128)(2,1)S(1)} %copy-done.1, f32[1024,256]{1,0:T(8,128)} %convolution_add_fusion.1), kind=kOutput, calls=%fused_computation.22 | convolution fusion | flops 102301696 | bytes 1642496 | tf_op jit(solution)/shard_map/dot_general | solution.py:140
  33.9 0.0 copy-start.7
  33.9 10.9 %all_to_all.24 = f32[16,8,256]{2,1,0:T(8,128)S(1)} all-to-all(f32[16,8,256]{2,1,0:T(8,128)S(1)} %bitcast.87), channel_id=1, replica_groups=mesh['along'=64,'across'=16] {'across'}, dimensions={0} | all-to-all | bytes 262144 | tf_op jit(solution)/shard_map/all_to_all | solution.py:13
  44.9 11.8 %all_to_all.25 = f32[16,8,256]{2,1,0:T(8,128)S(1)} all-to-all(f32[16,8,256]{2,1,0:T(8,128)S(1)} %broadcast_in_dim.42), channel_id=1, replica_groups=mesh['along'=64,'across'=16] {'across'}, dimensions={0} | all-to-all | bytes 262144 | tf_op jit(solution)/shard_map/all_to_all | solution.py:20
  56.7 0.1 slice_reduce_fusion
  56.8 0.1 div.45
  56.9 0.2 multiply_reduce_fusion.1
  57.0 0.1 rsqrt.16
  57.1 0.2 fusion.26
  57.4 0.2 fusion.55
  57.5 0.2 fusion.53
  57.8 0.0 copy-start.4
  57.8 1.5 %fusion.2 = bf16[1024,256]{1,0:T(8,128)(2,1)} fusion(f32[1024,256]{1,0:T(8,128)S(1)} %copy-done.5, bf16[1024,256]{1,0:T(8,128)(2,1)S(1)} %copy-done.7, s32[1024]{0:T(1024)S(1)} %copy-done.12, f32[64,256]{1,0:T(8,128)S(1)} %fusion.55, f32[16,8,256]{2,1,0:T(8,128)S(1)} %all_to_all.25, f32[64]{0:T(128)S(1)} %get-tuple-element.9, f32[64]{0:T(128)S(1)} %get-tuple-element.10, ...), kind=kOutput, calls=%fused_computation.12 | convolution fusion | flops 103710720 | bytes 2234368 | tf_op jit(solution)/shard_map/dot_general | solution.py:157
  59.3 1.7 %fusion.6 = f32[256,256]{1,0:T(8,128)S(1)} fusion(bf16[1024,256]{1,0:T(8,128)(2,1)S(1)} %copy-done.4, bf16[1024,256]{1,0:T(8,128)(2,1)} %fusion.2, bf16[512,256]{1,0:T(8,128)(2,1)S(1)} %copy-done.10), kind=kOutput, calls=%fused_computation.17 | convolution fusion | flops 268697600 | bytes 1441792 | tf_op jit(solution)/shard_map/dot_general | solution.py:62
  61.0 0.8 copy.20
  61.8 3.4 %all-to-all-start.2 = ((f32[32,16,128]{2,0,1:T(8,128)}), f32[32,16,128]{2,0,1:T(8,128)S(1)}, u32[]{:S(2)}, u32[]{:S(2)}) async-start(f32[32,16,128]{2,0,1:T(8,128)} %copy.20), calls=%async_computation.2 | async-start | bytes 524288 | tf_op jit(solution)/shard_map/all_to_all | solution.py:13
  65.3 0.1 copy.21
  65.4 0.2 fusion.27
  65.6 10.9 %all-to-all-done.2 = f32[32,16,128]{2,0,1:T(8,128)S(1)} async-done(((f32[32,16,128]{2,0,1:T(8,128)}), f32[32,16,128]{2,0,1:T(8,128)S(1)}, u32[]{:S(2)}, u32[]{:S(2)}) %all-to-all-start.2) | async-done | bytes 262176 | tf_op jit(solution)/shard_map/all_to_all | solution.py:13
  76.4 0.6 pad_maximum_fusion.1
  77.0 23.3 %all-to-all-start.3 = ((f32[64,1,128]{2,1,0:T(1,128)}), f32[64,1,128]{2,1,0:T(1,128)S(1)}, u32[]{:S(2)}, u32[]{:S(2)}) async-start(f32[64,1,128]{2,1,0:T(1,128)} %bitcast.20), calls=%async_computation.3 | async-start | bytes 65536 | tf_op jit(solution)/shard_map/all_to_all | solution.py:13
  100.3 1.3 %fusion.1 = bf16[1024,256]{1,0:T(8,128)(2,1)} fusion(s32[1024]{0:T(1024)S(1)} %copy-done.12, f32[64,256]{1,0:T(8,128)S(1)} %get-tuple-element.8, f32[1024,256]{1,0:T(8,128)S(1)} %copy-done.5, bf16[1024,256]{1,0:T(8,128)(2,1)S(1)} %copy-done.1), kind=kOutput, calls=%fused_computation.11 | convolution fusion | flops 35930112 | bytes 2166784 | tf_op jit(solution)/shard_map/dot_general | solution.py:144
  101.6 9.6 %all-to-all-done.3 = f32[64,1,128]{2,1,0:T(1,128)S(1)} async-done(((f32[64,1,128]{2,1,0:T(1,128)}), f32[64,1,128]{2,1,0:T(1,128)S(1)}, u32[]{:S(2)}, u32[]{:S(2)}) %all-to-all-start.3) | async-done | bytes 32800 | tf_op jit(solution)/shard_map/all_to_all | solution.py:13
  111.1 0.6 reduce_sum.69
  (31 shorter events, 0.2 us)
Async XLA Ops:
  0.6 29.5 %copy-start = (bf16[256,256]{1,0:T(8,128)(2,1)S(1)}, bf16[256,256]{1,0:T(8,128)(2,1)}, u32[]{:S(2)}) copy-start(bf16[256,256]{1,0:T(8,128)(2,1)} %param.16) | copy-start | bytes 393220
  0.6 2.0 %copy-start.1 = (bf16[1024,256]{1,0:T(8,128)(2,1)S(1)}, bf16[1024,256]{1,0:T(8,128)(2,1)}, u32[]{:S(2)}) copy-start(bf16[1024,256]{1,0:T(8,128)(2,1)} %param.10) | copy-start | bytes 1572868
  3.2 0.7 copy-start.14
  3.6 20.6 %copy-start.13 = (s32[8,4]{0,1:T(4,128)S(1)}, s32[8,4]{0,1:T(4,128)}, u32[]{:S(2)}) copy-start(s32[8,4]{0,1:T(4,128)} %param.12) | copy-start | bytes 388
  3.6 20.8 %copy-start.15 = (s32[8]{0:T(128)S(1)}, s32[8]{0:T(128)}, u32[]{:S(2)}) copy-start(s32[8]{0:T(128)} %param.13) | copy-start | bytes 100
  3.6 20.9 %copy-start.9 = (bf16[512,256]{1,0:T(8,128)(2,1)S(1)}, bf16[512,256]{1,0:T(8,128)(2,1)}, u32[]{:S(2)}) copy-start(bf16[512,256]{1,0:T(8,128)(2,1)} %param.17) | copy-start | bytes 786436
  3.9 21.9 %copy-start.6 = (bf16[1024,256]{1,0:T(8,128)(2,1)S(1)}, bf16[1024,256]{1,0:T(8,128)(2,1)}, u32[]{:S(2)}) copy-start(bf16[1024,256]{1,0:T(8,128)(2,1)} %param.19) | copy-start | bytes 1572868
  3.9 21.8 %copy-start.12 = (s32[1024]{0:T(1024)S(1)}, s32[1024]{0:T(1024)}, u32[]{:S(2)}) copy-start(s32[1024]{0:T(1024)} %param.15) | copy-start | bytes 12292
  4.2 22.4 %collective-permute-start = (bf16[128,256]{1,0:T(8,128)(2,1)S(1)}, bf16[128,256]{1,0:T(8,128)(2,1)S(1)}, u32[]{:S(2)}, u32[]{:S(2)}) collective-permute-start(bf16[128,256]{1,0:T(8,128)(2,1)S(1)} %convolution_convert_fusion.1), channel_id=1, source_target_pairs={{0,16},{16,32},{32,48},{48,64},{64,80},{80,96},{96,112},{112,128},... | collective-permute-start | bytes 196616 | tf_op jit(solution)/shard_map/ppermute | solution.py:30
  8.2 18.5 %collective-permute-start.1 = (bf16[128,256]{1,0:T(8,128)(2,1)S(1)}, bf16[128,256]{1,0:T(8,128)(2,1)S(1)}, u32[]{:S(2)}, u32[]{:S(2)}) collective-permute-start(bf16[128,256]{1,0:T(8,128)(2,1)S(1)} %convolution_convert_fusion.1), channel_id=1, source_target_pairs={{16,0},{32,16},{48,32},{64,48},{80,64},{96,80},{112,96},{128,112},... | collective-permute-start | bytes 196616 | tf_op jit(solution)/shard_map/ppermute | solution.py:31
  9.5 17.2 %collective-permute-start.2 = (bf16[128,256]{1,0:T(8,128)(2,1)S(1)}, bf16[128,256]{1,0:T(8,128)(2,1)S(1)}, u32[]{:S(2)}, u32[]{:S(2)}) collective-permute-start(bf16[128,256]{1,0:T(8,128)(2,1)S(1)} %convolution_convert_fusion.1), channel_id=1, source_target_pairs={{0,1},{1,2},{2,3},{3,4},{4,5},{5,6},{6,7},{7,8},{8,9},{9,10},{10,1... | collective-permute-start | bytes 196616 | tf_op jit(solution)/shard_map/ppermute | solution.py:30
  13.6 13.0 %collective-permute-start.3 = (bf16[128,256]{1,0:T(8,128)(2,1)S(1)}, bf16[128,256]{1,0:T(8,128)(2,1)S(1)}, u32[]{:S(2)}, u32[]{:S(2)}) collective-permute-start(bf16[128,256]{1,0:T(8,128)(2,1)S(1)} %convolution_convert_fusion.1), channel_id=1, source_target_pairs={{1,0},{2,1},{3,2},{4,3},{5,4},{6,5},{7,6},{8,7},{9,8},{10,9},{11,1... | collective-permute-start | bytes 196616 | tf_op jit(solution)/shard_map/ppermute | solution.py:31
  29.1 1.4 %copy-start.2 = (f32[1024,256]{1,0:T(8,128)S(1)}, f32[1024,256]{1,0:T(8,128)}, u32[]{:S(2)}) copy-start(f32[1024,256]{1,0:T(8,128)} %fusion.20) | copy-start | bytes 3145732
  29.1 1.4 %copy-start.10 = (bf16[512,256]{1,0:T(8,128)(2,1)S(1)}, bf16[512,256]{1,0:T(8,128)(2,1)}, u32[]{:S(2)}) copy-start(bf16[512,256]{1,0:T(8,128)(2,1)} %param.17) | copy-start | bytes 786436
  29.3 0.8 copy-start.3
  32.1 1.8 %copy-start.8 = (f32[1,64,256]{2,1,0:T(8,128)S(1)}, f32[1,64,256]{2,1,0:T(8,128)}, u32[]{:S(2)}) copy-start(f32[1,64,256]{2,1,0:T(8,128)} %convolution_bitcast_fusion) | copy-start | bytes 196612
  32.1 25.0 %copy-start.11 = (bf16[256,256]{1,0:T(8,128)(2,1)S(1)}, bf16[256,256]{1,0:T(8,128)(2,1)}, u32[]{:S(2)}) copy-start(bf16[256,256]{1,0:T(8,128)(2,1)} %param.18) | copy-start | bytes 393220
  33.9 23.8 %copy-start.5 = (f32[1024,256]{1,0:T(8,128)S(1)}, f32[1024,256]{1,0:T(8,128)}, u32[]{:S(2)}) copy-start(f32[1024,256]{1,0:T(8,128)} %convolution_add_fusion.1) | copy-start | bytes 3145732
  33.9 23.8 %copy-start.7 = (bf16[1024,256]{1,0:T(8,128)(2,1)S(1)}, bf16[1024,256]{1,0:T(8,128)(2,1)}, u32[]{:S(2)}) copy-start(bf16[1024,256]{1,0:T(8,128)(2,1)} %param.19) | copy-start | bytes 1572868
  57.8 1.5 %copy-start.4 = (bf16[1024,256]{1,0:T(8,128)(2,1)S(1)}, bf16[1024,256]{1,0:T(8,128)(2,1)}, u32[]{:S(2)}) copy-start(bf16[1024,256]{1,0:T(8,128)(2,1)} %copy-done.3) | copy-start | bytes 1572868
  61.8 14.6 %all-to-all-start.2 = ((f32[32,16,128]{2,0,1:T(8,128)}), f32[32,16,128]{2,0,1:T(8,128)S(1)}, u32[]{:S(2)}, u32[]{:S(2)}) async-start(f32[32,16,128]{2,0,1:T(8,128)} %copy.20), calls=%async_computation.2 | async-start | bytes 524288 | tf_op jit(solution)/shard_map/all_to_all | solution.py:13
  77.0 34.1 %all-to-all-start.3 = ((f32[64,1,128]{2,1,0:T(1,128)}), f32[64,1,128]{2,1,0:T(1,128)S(1)}, u32[]{:S(2)}, u32[]{:S(2)}) async-start(f32[64,1,128]{2,1,0:T(1,128)} %bitcast.20), calls=%async_computation.3 | async-start | bytes 65536 | tf_op jit(solution)/shard_map/all_to_all | solution.py:13
